TPU v7x, 128 devices: a whole 4x4x4 slice. The times are simulated.
128 devices in a mesh: ctx: 8 (over x, core), tp: 8 (over z_hi, y), dp: 2 (over z_lo).
Axes of the slice: x: 4, y: 4, z: 4 (z_hi: 2, z_lo: 2; z = z_hi * 2 + z_lo), core: 2. Of those that a mesh axis runs over, the one named last changes fastest.
Arguments:
- activations: bfloat16 [16384, 4096], P(('ctx', 'tp', 'dp')), may hold values from -6 to 6
- out_grad: bfloat16 [16384, 4096], P(('ctx', 'tp', 'dp')), may hold values from -6 to 6
- routes: int32 [16384, 8], P(('ctx', 'tp', 'dp')), may hold values from 0 to 127, all different within a row; in each aligned block of 128 rows (0 to 127, 128 to 255, ...) at most 12 rows name the same one
- gate_probs: bfloat16 [16384, 8], P(('ctx', 'tp', 'dp')), may hold values from 0.049804688 to 0.59765625
- saved_pre: bfloat16 [64, 2, 768, 1536], P(('ctx', 'tp'), 'dp'), may hold values from -6 to 6
- expert_weights: bfloat16 [64, 4096, 2304], P(('ctx', 'tp'), 'dp'), may hold values from -0.09375 to 0.09375
Outputs:
- input_grad: bfloat16 [16384, 4096], P(('ctx', 'tp', 'dp'))
- prob_grad: bfloat16 [16384, 8], P(('ctx', 'tp', 'dp'))
- weight_grad: bfloat16 [64, 4096, 2304], P(('ctx', 'tp'), 'dp')
Inputs may be any that keep to these rules, and one draw needn't show every extreme that they name: `routes`: each row names 8 different experts. Within the rows of one device (aligned blocks of 128 rows) no expert is named more than 12 times, a bound that some block reaches.
All inputs are finite; a program needn't handle non-finite values.
Results may differ from a plain program's by a relative error of at most 0.02.
Values may be sent and summed in bfloat16 or wider, within the bound.
No kernel may reach another device: no remote copies, remote signals or barrier semaphores. Data moves between devices by JAX's collectives and lax.ppermute only.
A program may use at most 192 MiB of HBM per device.

v0:
```python
import jax
import jax.numpy as jnp
from jax import lax
from jax.sharding import PartitionSpec as P


def body(activations, out_grad, routes, gate_probs, saved_pre, expert_weights):
    tok_count = activations.shape[0]
    top_k = routes.shape[1]
    model_width = activations.shape[1]
    ctx_size = lax.axis_size("ctx")
    tp_size = lax.axis_size("tp")
    sources = ctx_size * tp_size
    slots_all = saved_pre.shape[2]
    capacity = slots_all // sources
    hidden = saved_pre.shape[3] // 2
    flat_routes = routes.reshape(-1)
    in_window = flat_routes < sources
    onehot = (flat_routes[:, None] == jnp.arange(sources, dtype=jnp.int32)[None, :]).astype(
        jnp.int32
    )
    position = jnp.sum(jnp.cumsum(onehot, axis=0) * onehot, axis=1) - 1
    slot_index = jnp.where(in_window, flat_routes * capacity + position, sources * capacity)
    route_count = tok_count * top_k
    route_of_slot = jnp.full((sources * capacity,), route_count, jnp.int32)
    route_of_slot = route_of_slot.at[slot_index].set(
        jnp.arange(route_count, dtype=jnp.int32), mode="drop"
    )
    filled = route_of_slot < route_count
    safe_route = jnp.minimum(route_of_slot, route_count - 1)
    token_of_slot = safe_route // top_k
    zero_value = jnp.zeros((), jnp.bfloat16)
    send_rows = jnp.where(filled[:, None], activations[token_of_slot], zero_value)
    send_grads = jnp.where(filled[:, None], out_grad[token_of_slot], zero_value)
    send_probs = jnp.where(filled, gate_probs.reshape(-1)[safe_route], zero_value)
    received = (
        lax.all_to_all(
            send_rows.reshape(sources, capacity, model_width),
            ("ctx", "tp"),
            split_axis=0,
            concat_axis=0,
            tiled=True,
        ),
        lax.all_to_all(
            send_grads.reshape(sources, capacity, model_width),
            ("ctx", "tp"),
            split_axis=0,
            concat_axis=0,
            tiled=True,
        ),
        lax.all_to_all(
            send_probs.reshape(sources, capacity),
            ("ctx", "tp"),
            split_axis=0,
            concat_axis=0,
            tiled=True,
        ),
    )
    recv_rows = received[0].reshape(slots_all, model_width)
    recv_grads = received[1].reshape(slots_all, model_width)
    prob_column = received[2].reshape(slots_all, 1).astype(jnp.float32)
    saved_rows = saved_pre[0, 0]
    pre_gate = saved_rows[:, :hidden].astype(jnp.float32)
    pre_up = saved_rows[:, hidden:].astype(jnp.float32)
    sigmoid_gate = jax.nn.sigmoid(pre_gate)
    activated = pre_gate * sigmoid_gate
    hidden_act = activated * pre_up
    weights = expert_weights[0]
    down_part = weights[:, 2 * hidden :]
    gate_up_part = weights[:, : 2 * hidden]
    down_grad = jnp.dot(
        recv_grads,
        lax.all_gather(down_part, "dp", axis=0, tiled=True),
        preferred_element_type=jnp.float32,
    )
    prob_slot = jnp.sum(hidden_act * down_grad, axis=1).astype(jnp.bfloat16)
    scaled_grad = prob_column * down_grad
    finish_gate_up_grad = jnp.concatenate(
        [
            scaled_grad * pre_up * sigmoid_gate * (1.0 + pre_gate * (1.0 - sigmoid_gate)),
            scaled_grad * activated,
        ],
        axis=1,
    ).astype(jnp.bfloat16)
    finish_scaled_hidden = (prob_column * hidden_act).astype(jnp.bfloat16)
    prob_slot, gate_up_grad, scaled_hidden = (prob_slot, finish_gate_up_grad, finish_scaled_hidden)
    row_grad = lax.dot_general(
        gate_up_grad,
        lax.all_gather(gate_up_part, "dp", axis=0, tiled=True),
        (((1,), (1,)), ((), ())),
        preferred_element_type=jnp.float32,
    ).astype(jnp.bfloat16)
    gate_up_term = lax.dot_general(
        recv_rows, gate_up_grad, (((0,), (0,)), ((), ())), preferred_element_type=jnp.float32
    )
    down_piece = lax.dot_general(
        recv_grads, scaled_hidden, (((0,), (0,)), ((), ())), preferred_element_type=jnp.float32
    )
    weight_grad = lax.psum_scatter(
        jnp.concatenate([gate_up_term, down_piece], axis=1).astype(jnp.bfloat16),
        "dp",
        scatter_dimension=0,
        tiled=True,
    )[None]
    returned = (
        lax.all_to_all(
            row_grad.reshape(sources, capacity, model_width),
            ("ctx", "tp"),
            split_axis=0,
            concat_axis=0,
            tiled=True,
        ),
        lax.all_to_all(
            prob_slot.reshape(sources, capacity),
            ("ctx", "tp"),
            split_axis=0,
            concat_axis=0,
            tiled=True,
        ),
    )
    back_rows = returned[0].reshape(sources * capacity, model_width)
    back_probs = returned[1].reshape(sources * capacity)
    safe_slot = jnp.minimum(slot_index, sources * capacity - 1)
    picked = jnp.where(in_window[:, None], back_rows[safe_slot], zero_value)
    input_grad = jnp.sum(picked.reshape(tok_count, top_k, model_width).astype(jnp.float32), axis=1)
    prob_grad = jnp.where(in_window, back_probs[safe_slot], zero_value).reshape(tok_count, top_k)
    return (input_grad.astype(jnp.bfloat16), prob_grad, weight_grad)


def solution(mesh):
    placed = (
        P(("ctx", "tp", "dp"), None),
        P(("ctx", "tp", "dp"), None),
        P(("ctx", "tp", "dp"), None),
        P(("ctx", "tp", "dp"), None),
        P(("ctx", "tp"), "dp", None, None),
        P(("ctx", "tp"), "dp", None),
    )
    return jax.shard_map(
        body,
        mesh=mesh,
        in_specs=placed,
        out_specs=(
            P(("ctx", "tp", "dp"), None),
            P(("ctx", "tp", "dp"), None),
            P(("ctx", "tp"), "dp", None),
        ),
        check_vma=False,
    )
```

profile of v0, /device:TPU:1, one launch (start us, length us, event | category | flops | bytes accessed | tf_op | source)
XLA Modules:
  0.0 841.0 jit_solution(4453830217344375379)
XLA Ops:
  10.6 18.0 %reduce-window.6 = s32[64,8,128]{2,1,0:T(8,128)S(1)} reduce-window(s32[64,8,128]{2,1,0:T(8,128)S(1)} %fusion.12, s32[]{:T(128)} %constant.18.clone.1), window={size=1x1x128 pad=0_0x0_0x127_0}, to_apply=%region_0.0 | reduce-window | flops 8323072 | bytes 524292 | tf_op jit(solution)/shard_map/reduce-window
  40.0 12.3 %all-to-all-start = ((bf16[64,1,12]{2,1,0:T(2,128)(2,1)}), bf16[64,1,12]{2,1,0:T(2,128)(2,1)S(1)}, u32[]{:S(2)}, u32[]{:S(2)}) async-start(bf16[64,1,12]{2,1,0:T(2,128)(2,1)} %all_to_all.25), calls=%async_computation | async-start | bytes 65536 | tf_op jit(solution)/shard_map/all_to_all | solution.py:51
  58.1 9.9 %gather.31 = bf16[64,12,4096]{2,1,0:T(8,128)(2,1)} reshape(bf16[768,4096]{1,0:T(8,128)(2,1)} %gather_fusion.4) | data formatting | bytes 12582912 | tf_op jit(solution)/shard_map/gather | solution.py:33
  83.5 11.6 %broadcast_select_fusion = (bf16[64,12,4096]{2,1,0:T(8,128)(2,1)}, bf16[64,12,4096]{2,1,0:T(8,128)(2,1)}) fusion(bf16[64,12,4096]{2,1,0:T(8,128)(2,1)} %gather.31, pred[64,12]{1,0:T(8,128)(4,1)S(1)} %broadcast_in_dim.63, bf16[64,12,4096]{2,1,0:T(8,128)(2,1)} %gather.25), kind=kLoop, calls=%fused_computation.10 | loop fusion | flops 6291456 | bytes 25166592 | tf_op jit(solution)/shard_map/jit(_where)/select_n | solution.py:33
  95.0 10.5 %all-to-all-start.4 = ((bf16[64,12,4096]{2,1,0:T(8,128)(2,1)}), bf16[64,12,4096]{2,1,0:T(8,128)(2,1)}, u32[]{:S(2)}, u32[]{:S(2)}) async-start(bf16[64,12,4096]{2,1,0:T(8,128)(2,1)} %get-tuple-element.19), calls=%async_computation.4 | async-start | bytes 16777216 | tf_op jit(solution)/shard_map/all_to_all | solution.py:37
  109.3 95.8 %all-to-all-done.4 = bf16[64,12,4096]{2,1,0:T(8,128)(2,1)} async-done(((bf16[64,12,4096]{2,1,0:T(8,128)(2,1)}), bf16[64,12,4096]{2,1,0:T(8,128)(2,1)}, u32[]{:S(2)}, u32[]{:S(2)}) %all-to-all-start.4) | async-done | bytes 6291488 | tf_op jit(solution)/shard_map/all_to_all | solution.py:37
  205.1 19.6 %all-to-all-start.1 = ((bf16[64,12,4096]{2,1,0:T(8,128)(2,1)}), bf16[64,12,4096]{2,1,0:T(8,128)(2,1)}, u32[]{:S(2)}, u32[]{:S(2)}) async-start(bf16[64,12,4096]{2,1,0:T(8,128)(2,1)} %get-tuple-element.20), calls=%async_computation.1 | async-start | bytes 16777216 | tf_op jit(solution)/shard_map/all_to_all | solution.py:44
  235.0 10.0 %reshape.174 = bf16[768,4096]{1,0:T(8,128)(2,1)} reshape(bf16[64,12,4096]{2,1,0:T(8,128)(2,1)} %all-to-all-done.4) | data formatting | bytes 12582912 | tf_op jit(solution)/shard_map/reshape | solution.py:59
  245.0 79.3 %all-to-all-done.1 = bf16[64,12,4096]{2,1,0:T(8,128)(2,1)} async-done(((bf16[64,12,4096]{2,1,0:T(8,128)(2,1)}), bf16[64,12,4096]{2,1,0:T(8,128)(2,1)}, u32[]{:S(2)}, u32[]{:S(2)}) %all-to-all-start.1) | async-done | bytes 6291488 | tf_op jit(solution)/shard_map/all_to_all | solution.py:44
  324.3 9.8 %reshape.170 = bf16[768,4096]{1,0:T(8,128)(2,1)} reshape(bf16[64,12,4096]{2,1,0:T(8,128)(2,1)} %all-to-all-done.1) | data formatting | bytes 12582912 | tf_op jit(solution)/shard_map/reshape | solution.py:60
  334.1 10.0 %convolution_convert_fusion.1 = bf16[4096,768]{0,1:T(8,128)(2,1)} fusion(bf16[768,4096]{1,0:T(8,128)(2,1)} %reshape.170, f32[768]{0:T(1024)S(1)} %reshape.175, bf16[768,1536]{0,1:T(8,128)(2,1)S(1)} %bitcast.33), kind=kOutput, calls=%fused_computation.12 | convolution fusion | flops 4840292352 | bytes 14945280 | tf_op jit(solution)/shard_map/dot_general | solution.py:96
  344.1 10.4 %all-gather.3.cloned.1.call-done = bf16[4096,768]{1,0:T(8,128)(2,1)} async-done(((bf16[2048,768]{1,0:T(8,128)(2,1)}), bf16[4096,768]{1,0:T(8,128)(2,1)}) %all-gather.3.cloned.1.call-update) | async-done | bytes 6291472 | tf_op jit(solution)/shard_map/all_gather | solution.py:73
  354.5 11.0 %fusion.3 = (bf16[768,768]{0,1:T(8,128)(2,1)S(1)}, bf16[768,768]{0,1:T(8,128)(2,1)}, bf16[768]{0:T(1024)(128)(2,1)S(1)}) fusion(f32[768]{0:T(1024)S(1)} %reshape.175, bf16[768,1536]{0,1:T(8,128)(2,1)S(1)} %bitcast.34, bf16[768,4096]{1,0:T(8,128)(2,1)} %reshape.170, bf16[4096,768]{1,0:T(8,128)(2,1)} %all-gather.3.cloned.1.call-done), kind=kOutput, calls=%fused_computation.21 | convolution fusion | flops 4843043840 | bytes 17306112 | tf_op jit(solution)/shard_map/dot_general | solution.py:71
  365.5 13.5 %convolution_convert_fusion = bf16[4096,1536]{0,1:T(8,128)(2,1)S(1)} fusion(bf16[768,4096]{1,0:T(8,128)(2,1)} %reshape.174, bf16[768,768]{0,1:T(8,128)(2,1)} %get-tuple-element.15, bf16[768,768]{0,1:T(8,128)(2,1)S(1)} %get-tuple-element.14), kind=kOutput, calls=%fused_computation.7 | convolution fusion | flops 9674686464 | bytes 21233664 | tf_op jit(solution)/shard_map/dot_general | solution.py:93
  379.0 17.0 %pad_maximum_fusion = bf16[4096,2304]{0,1:T(8,128)(2,1)} fusion(bf16[4096,768]{0,1:T(8,128)(2,1)} %convolution_convert_fusion.1, bf16[4096,1536]{0,1:T(8,128)(2,1)S(1)} %convolution_convert_fusion), kind=kLoop, calls=%fused_computation.6 | loop fusion | flops 37748736 | bytes 37748736 | tf_op jit(solution)/shard_map/concatenate | solution.py:100
  396.7 11.3 %all-to-all-start.3 = ((bf16[64,1,12]{2,1,0:T(2,128)(2,1)}), bf16[64,1,12]{2,1,0:T(2,128)(2,1)S(1)}, u32[]{:S(2)}, u32[]{:S(2)}) async-start(bf16[64,1,12]{2,1,0:T(2,128)(2,1)} %convert_element_type.56), calls=%async_computation.3 | async-start | bytes 65536 | tf_op jit(solution)/shard_map/all_to_all | solution.py:113
  408.0 105.9 %all-gather.5.cloned.1.call-done = bf16[4096,1536]{1,0:T(8,128)(2,1)} async-done(((bf16[2048,1536]{1,0:T(8,128)(2,1)}), bf16[4096,1536]{1,0:T(8,128)(2,1)}) %all-gather.5.cloned.1.call-update) | async-done | bytes 12582928 | tf_op jit(solution)/shard_map/all_gather | solution.py:89
  513.9 14.7 %convolution_convert_fusion.2 = bf16[768,4096]{1,0:T(8,128)(2,1)} fusion(bf16[4096,1536]{1,0:T(8,128)(2,1)} %all-gather.5.cloned.1.call-done, bf16[768,768]{0,1:T(8,128)(2,1)S(1)} %copy-done.12, bf16[768,768]{0,1:T(8,128)(2,1)S(1)} %copy-done.11), kind=kOutput, calls=%fused_computation.13 | convolution fusion | flops 9671540736 | bytes 21233664 | tf_op jit(solution)/shard_map/dot_general | solution.py:87
  538.5 11.1 %all-to-all-start.2 = ((bf16[64,12,4096]{2,1,0:T(8,128)(2,1)}), bf16[64,12,4096]{2,1,0:T(8,128)(2,1)}, u32[]{:S(2)}, u32[]{:S(2)}) async-start(bf16[64,12,4096]{2,1,0:T(8,128)(2,1)} %reshape.171), calls=%async_computation.2 | async-start | bytes 16777216 | tf_op jit(solution)/shard_map/all_to_all | solution.py:106
  557.4 92.3 %all-to-all-done.2 = bf16[64,12,4096]{2,1,0:T(8,128)(2,1)} async-done(((bf16[64,12,4096]{2,1,0:T(8,128)(2,1)}), bf16[64,12,4096]{2,1,0:T(8,128)(2,1)}, u32[]{:S(2)}, u32[]{:S(2)}) %all-to-all-start.2) | async-done | bytes 6291488 | tf_op jit(solution)/shard_map/all_to_all | solution.py:106
  649.7 10.0 %reshape.172 = bf16[768,4096]{1,0:T(8,128)(2,1)} reshape(bf16[64,12,4096]{2,1,0:T(8,128)(2,1)} %all-to-all-done.2) | data formatting | bytes 12582912 | tf_op jit(solution)/shard_map/reshape | solution.py:121
  659.7 18.7 %gather_fusion.2 = bf16[1024,4096]{1,0:T(8,128)(2,1)} fusion(bf16[768,4096]{1,0:T(8,128)(2,1)} %reshape.172, s32[1024]{0:T(1024)S(1)} %broadcast_clamp_fusion), kind=kCustom, calls=%fused_computation.2 | custom fusion | bytes 16781312 | tf_op jit(solution)/shard_map/gather | solution.py:124
  686.8 134.7 %reduce-scatter.2.cloned.1.call-done = bf16[2048,2304]{0,1:T(8,128)(2,1)} async-done(((bf16[4096,2304]{0,1:T(8,128)(2,1)}), bf16[2048,2304]{0,1:T(8,128)(2,1)}) %reduce-scatter.2.cloned.1.call-update) | async-done | bytes 9437200 | tf_op jit(solution)/shard_map/reduce_scatter | solution.py:99
  821.5 12.7 %copy.33 = bf16[1,2048,2304]{2,1,0:T(8,128)(2,1)} copy(bf16[1,2048,2304]{1,2,0:T(8,128)(2,1)} %bitcast.32) | data formatting | bytes 18874368
  (80 shorter events, 77.0 us)
Async XLA Ops:
  7.2 45.2 %copy-start = (bf16[128,4096]{1,0:T(8,128)(2,1)S(1)}, bf16[128,4096]{1,0:T(8,128)(2,1)}, u32[]{:S(2)}) copy-start(bf16[128,4096]{1,0:T(8,128)(2,1)} %param.6) | copy-start | bytes 3145732
  8.7 0.6 copy-start.5
  9.4 1.2 copy-start.7
  40.0 55.0 %all-to-all-start = ((bf16[64,1,12]{2,1,0:T(2,128)(2,1)}), bf16[64,1,12]{2,1,0:T(2,128)(2,1)S(1)}, u32[]{:S(2)}, u32[]{:S(2)}) async-start(bf16[64,1,12]{2,1,0:T(2,128)(2,1)} %all_to_all.25), calls=%async_computation | async-start | bytes 65536 | tf_op jit(solution)/shard_map/all_to_all | solution.py:51
  58.1 9.9 %copy-start.2 = (bf16[128,4096]{1,0:T(8,128)(2,1)S(1)}, bf16[128,4096]{1,0:T(8,128)(2,1)}, u32[]{:S(2)}) copy-start(bf16[128,4096]{1,0:T(8,128)(2,1)} %param.7) | copy-start | bytes 3145732
  95.0 110.1 %all-to-all-start.4 = ((bf16[64,12,4096]{2,1,0:T(8,128)(2,1)}), bf16[64,12,4096]{2,1,0:T(8,128)(2,1)}, u32[]{:S(2)}, u32[]{:S(2)}) async-start(bf16[64,12,4096]{2,1,0:T(8,128)(2,1)} %get-tuple-element.19), calls=%async_computation.4 | async-start | bytes 16777216 | tf_op jit(solution)/shard_map/all_to_all | solution.py:37
  105.5 249.0 %all-gather.3.cloned.1.call-start = ((), (), s32[]{:S(2)}) async-start(), calls=%async_computation.6 | async-start | bytes 9437184 | tf_op jit(solution)/shard_map/all_gather | solution.py:73
  205.1 119.2 %all-to-all-start.1 = ((bf16[64,12,4096]{2,1,0:T(8,128)(2,1)}), bf16[64,12,4096]{2,1,0:T(8,128)(2,1)}, u32[]{:S(2)}, u32[]{:S(2)}) async-start(bf16[64,12,4096]{2,1,0:T(8,128)(2,1)} %get-tuple-element.20), calls=%async_computation.1 | async-start | bytes 16777216 | tf_op jit(solution)/shard_map/all_to_all | solution.py:44
  224.7 289.2 %all-gather.5.cloned.1.call-start = ((), (), s32[]{:S(2)}) async-start(), calls=%async_computation.7 | async-start | bytes 18874368 | tf_op jit(solution)/shard_map/all_gather | solution.py:89
  230.6 1.7 copy-start.3
  230.7 590.8 %reduce-scatter.2.cloned.1.call-start = ((), (), s32[]{:S(2)}) async-start(), calls=%async_computation.8 | async-start | bytes 28311552 | tf_op jit(solution)/shard_map/reduce_scatter | solution.py:99
  245.0 89.2 %copy-start.4 = (bf16[1,1,768,1536]{2,3,1,0:T(8,128)(2,1)S(1)}, bf16[1,1,768,1536]{2,3,1,0:T(8,128)(2,1)}, u32[]{:S(2)}) copy-start(bf16[1,1,768,1536]{2,3,1,0:T(8,128)(2,1)} %copy.30) | copy-start | bytes 7077892
  365.5 13.5 %copy-start.10 = (bf16[768,768]{0,1:T(8,128)(2,1)}, bf16[768,768]{0,1:T(8,128)(2,1)S(1)}, u32[]{:S(2)}) copy-start(bf16[768,768]{0,1:T(8,128)(2,1)S(1)} %get-tuple-element.14) | copy-start | bytes 3538948
  395.9 117.9 %copy-start.11 = (bf16[768,768]{0,1:T(8,128)(2,1)S(1)}, bf16[768,768]{0,1:T(8,128)(2,1)}, u32[]{:S(2)}) copy-start(bf16[768,768]{0,1:T(8,128)(2,1)} %copy-done.10) | copy-start | bytes 3538948
  395.9 117.9 %copy-start.12 = (bf16[768,768]{0,1:T(8,128)(2,1)S(1)}, bf16[768,768]{0,1:T(8,128)(2,1)}, u32[]{:S(2)}) copy-start(bf16[768,768]{0,1:T(8,128)(2,1)} %get-tuple-element.15) | copy-start | bytes 3538948
  396.7 141.8 %all-to-all-start.3 = ((bf16[64,1,12]{2,1,0:T(2,128)(2,1)}), bf16[64,1,12]{2,1,0:T(2,128)(2,1)S(1)}, u32[]{:S(2)}, u32[]{:S(2)}) async-start(bf16[64,1,12]{2,1,0:T(2,128)(2,1)} %convert_element_type.56), calls=%async_computation.3 | async-start | bytes 65536 | tf_op jit(solution)/shard_map/all_to_all | solution.py:113
  538.5 11.1 %copy-start.9 = (s32[1024,1]{0,1:T(1,128)S(1)}, s32[1024,1]{0,1:T(1,128)}, u32[]{:S(2)}) copy-start(s32[1024,1]{0,1:T(1,128)} %get-tuple-element.17) | copy-start | bytes 12292
  538.5 18.2 %copy-start.6 = (s32[128,8]{1,0:T(8,128)S(1)}, s32[128,8]{1,0:T(8,128)}, u32[]{:S(2)}) copy-start(s32[128,8]{1,0:T(8,128)} %copy-done.5) | copy-start | bytes 12292
  538.5 111.2 %all-to-all-start.2 = ((bf16[64,12,4096]{2,1,0:T(8,128)(2,1)}), bf16[64,12,4096]{2,1,0:T(8,128)(2,1)}, u32[]{:S(2)}, u32[]{:S(2)}) async-start(bf16[64,12,4096]{2,1,0:T(8,128)(2,1)} %reshape.171), calls=%async_computation.2 | async-start | bytes 16777216 | tf_op jit(solution)/shard_map/all_to_all | solution.py:106
  659.6 18.7 %copy-start.8 = (pred[128,8]{1,0:T(8,128)(4,1)S(1)}, pred[128,8]{1,0:T(8,128)(4,1)}, u32[]{:S(2)}) copy-start(pred[128,8]{1,0:T(8,128)(4,1)} %copy-done.7) | copy-start | bytes 3076
  821.5 12.7 %copy-start.1 = (bf16[128,4096]{1,0:T(8,128)(2,1)S(1)}, bf16[128,4096]{1,0:T(8,128)(2,1)}, u32[]{:S(2)}) copy-start(bf16[128,4096]{1,0:T(8,128)(2,1)} %param.6) | copy-start | bytes 3145732
Sparse Core Ops, SparseCore 0:
  109.4 245.0 all-gather.2
  356.7 157.0 all-gather.4
  516.3 305.1 reduce-scatter.1
where the time goes:
time: 850 us; the launch traced here: 841 us
  waiting for transfers between devices  518 us (61%)
  local copies, waits for them, and re-layouts  137 us (16%)
  starting transfers between devices  65.3 us (8%)
  other arithmetic  56.9 us (7%)
  matrix products  49.2 us (6%)
  between operations  14.2 us (2%)
    reduce_scatter x1, waiting for transfers between devices, body(): lax.psum_scatter(jnp.concatenate([gate_up_term, down_piece], axis=1).asty...  135 us
    all_gather x1, waiting for transfers between devices, body(): lax.all_gather(gate_up_part, 'dp', axis=0, tiled=True)  106 us
    all_to_all x1, waiting for transfers between devices, body(): lax.all_to_all(send_rows.reshape(sources, capacity, model_width), ('ctx',...  95.8 us
    all_to_all x1, waiting for transfers between devices, body(): lax.all_to_all(row_grad.reshape(sources, capacity, model_width), ('ctx',...  92.3 us
    all_to_all x1, waiting for transfers between devices, body(): lax.all_to_all(send_grads.reshape(sources, capacity, model_width), ('ctx'...  79.3 us
    all_to_all x1, starting transfers between devices, body(): lax.all_to_all(send_grads.reshape(sources, capacity, model_width), ('ctx'...  19.6 us
    unnamed x31, local copies, waits for them, and re-layouts  19 us
    gather x1, local copies, waits for them, and re-layouts, body(): picked = jnp.where(in_window[:, None], back_rows[safe_slot], zero_value)  18.7 us
  transfers between devices with their start and end apart: 8, of which 6 were waited for; matrix products, arithmetic and copies ran while one was open for 23% of the time, Pallas kernels for 0%

commit v1 on v0

v1 whole, which is shorter than its diff:
```python
import jax
import jax.numpy as jnp
from jax import lax
from jax.sharding import PartitionSpec as P

ALL = ("ctx", "tp", "dp")


def body(activations, out_grad, routes, gate_probs, saved_pre, expert_weights):
    tok_count = activations.shape[0]
    top_k = routes.shape[1]
    model_width = activations.shape[1]
    ctx_size = lax.axis_size("ctx")
    tp_size = lax.axis_size("tp")
    n_dp = lax.axis_size("dp")
    experts = ctx_size * tp_size
    slots_rep = saved_pre.shape[2]
    capacity = slots_rep // experts
    hidden = saved_pre.shape[3] // 2
    half = model_width // n_dp
    devices = experts * n_dp
    slots_all = n_dp * slots_rep
    lanes = 512
    rows_per_chunk = capacity * half // lanes
    f32 = jnp.float32
    bf16 = jnp.bfloat16

    flat_routes = routes.reshape(-1)
    route_count = flat_routes.shape[0]
    idx = jnp.arange(route_count, dtype=jnp.int32)
    same = (flat_routes[:, None] == flat_routes[None, :]) & (idx[None, :] < idx[:, None])
    position = jnp.sum(same.astype(jnp.int32), axis=1)
    in_window = flat_routes < experts
    slot_index = jnp.where(in_window, flat_routes * capacity + position, -1)
    slot_ids = jnp.arange(experts * capacity, dtype=jnp.int32)
    route_hit = slot_index[:, None] == slot_ids[None, :]
    token_hit = jnp.any(route_hit.reshape(tok_count, top_k, -1), axis=1)
    select = token_hit.astype(bf16).T.reshape(experts, capacity, tok_count)

    send_probs = jnp.sum(
        jnp.where(route_hit, gate_probs.reshape(-1)[:, None].astype(f32), 0.0), axis=0
    ).astype(bf16).reshape(experts, 1, capacity)
    send_probs = jnp.broadcast_to(send_probs, (experts, n_dp, capacity)).reshape(devices, capacity)

    def dispatch(x):
        x3 = x.reshape(tok_count, n_dp, half)
        sent = jnp.einsum("ept,thd->ehpd", select, x3, preferred_element_type=f32).astype(bf16)
        got = lax.all_to_all(
            sent.reshape(devices, rows_per_chunk, lanes), ALL, 0, 0, tiled=True
        )
        got = got.reshape(experts, n_dp, capacity, half).transpose(1, 0, 2, 3)
        return got.reshape(slots_all, half)

    recv_grads = dispatch(out_grad)
    recv_rows = dispatch(activations)
    got_probs = lax.all_to_all(send_probs, ALL, 0, 0, tiled=True)
    prob_column = (
        got_probs.reshape(experts, n_dp, capacity).transpose(1, 0, 2).reshape(slots_all, 1).astype(f32)
    )

    saved_rows = lax.all_gather(saved_pre[0, 0], "dp", axis=0, tiled=True)
    weights = expert_weights[0]
    down_part = weights[:, 2 * hidden :]
    gate_up_part = weights[:, : 2 * hidden]

    partial_down = jnp.dot(recv_grads, down_part, preferred_element_type=f32)
    other_down = lax.ppermute(partial_down, "dp", [(i, (i + 1) % n_dp) for i in range(n_dp)])
    down_grad = partial_down + other_down

    pre_gate = saved_rows[:, :hidden].astype(f32)
    pre_up = saved_rows[:, hidden:].astype(f32)
    sigmoid_gate = jax.nn.sigmoid(pre_gate)
    activated = pre_gate * sigmoid_gate
    hidden_act = activated * pre_up
    prob_slot = jnp.sum(hidden_act * down_grad, axis=1).astype(bf16)
    scaled_grad = prob_column * down_grad
    gate_up_grad = jnp.concatenate(
        [
            scaled_grad * pre_up * sigmoid_gate * (1.0 + pre_gate * (1.0 - sigmoid_gate)),
            scaled_grad * activated,
        ],
        axis=1,
    ).astype(bf16)
    scaled_hidden = (prob_column * hidden_act).astype(bf16)

    row_grad = lax.dot_general(
        gate_up_grad, gate_up_part, (((1,), (1,)), ((), ())), preferred_element_type=f32
    ).astype(bf16)
    gate_up_term = lax.dot_general(
        recv_rows, gate_up_grad, (((0,), (0,)), ((), ())), preferred_element_type=f32
    )
    down_term = lax.dot_general(
        recv_grads, scaled_hidden, (((0,), (0,)), ((), ())), preferred_element_type=f32
    )
    weight_grad = jnp.concatenate([gate_up_term, down_term], axis=1).astype(bf16)[None]

    ret = row_grad.reshape(n_dp, experts, capacity, half).transpose(1, 0, 2, 3)
    back = lax.all_to_all(ret.reshape(devices, rows_per_chunk, lanes), ALL, 0, 0, tiled=True)
    back = back.reshape(experts, n_dp, capacity, half)
    input_grad = jnp.einsum("ept,ehpd->thd", select, back, preferred_element_type=f32)
    input_grad = input_grad.reshape(tok_count, model_width).astype(bf16)

    ret_probs = prob_slot.reshape(n_dp, experts, capacity).transpose(1, 0, 2).reshape(devices, capacity)
    back_probs = lax.all_to_all(ret_probs, ALL, 0, 0, tiled=True)
    back_probs = back_probs.reshape(experts, n_dp, capacity)[:, 0].reshape(-1).astype(f32)
    prob_grad = jnp.sum(jnp.where(route_hit, back_probs[None, :], 0.0), axis=1)
    prob_grad = prob_grad.astype(bf16).reshape(tok_count, top_k)
    return (input_grad, prob_grad, weight_grad)


def solution(mesh):
    placed = (
        P(ALL, None),
        P(ALL, None),
        P(ALL, None),
        P(ALL, None),
        P(("ctx", "tp"), "dp", None, None),
        P(("ctx", "tp"), "dp", None),
    )
    return jax.shard_map(
        body,
        mesh=mesh,
        in_specs=placed,
        out_specs=(
            P(ALL, None),
            P(ALL, None),
            P(("ctx", "tp"), "dp", None),
        ),
        check_vma=False,
    )
```

time: 850 us -> 552 us (0.65)
  waiting for transfers between devices: 518 us -> 209 us
  local copies, waits for them, and re-layouts: 137 us -> 187 us
  other arithmetic: 56.9 us -> 27.1 us
  starting transfers between devices: 65.3 us -> 49.1 us
    all_to_all x5, waiting for transfers between devices: 267 us -> 105 us  [the longest x2 95.4 us: dispatch(): lax.all_to_all(sent.reshape(devices, rows_per_chunk, lanes), ALL, 0, 0, t...]
    reduce_scatter x1 -> x0, waiting for transfers between devices: 135 us -> none  [body(): lax.psum_scatter(jnp.concatenate([gate_up_term, down_piece], axis=1).asty...]
    all_gather x2 -> x1, waiting for transfers between devices: 116 us -> 4.87 us  [body(): saved_rows = lax.all_gather(saved_pre[0, 0], 'dp', axis=0, tiled=True)]
    ppermute x0 -> x1, waiting for transfers between devices: none -> 99.4 us  [body(): lax.ppermute(partial_down, 'dp', [(i, (i + 1) % n_dp) for i in range(n_dp)])]
    reshape x6 -> x10, local copies, waits for them, and re-layouts: 39.8 us -> 103 us  [the longest x2 23.9 us: dispatch(): sent.reshape(devices, rows_per_chunk, lanes)]
    gather x8 -> x0, local copies, waits for them, and re-layouts: 61.6 us -> none  [the longest x1 18.7 us: body(): picked = jnp.where(in_window[:, None], back_rows[safe_slot], zero_value)]
    transpose x0 -> x5, local copies, waits for them, and re-layouts: none -> 25 us  [the longest x2 16.5 us: dispatch(): got = got.reshape(experts, n_dp, capacity, half).transpose(1, 0, 2, 3)]
    dot_general x0 -> x2, local copies, waits for them, and re-layouts: none -> 24.1 us  [body(): jnp.einsum('ept,ehpd->thd', select, back, preferred_element_type=f32)]
  transfers between devices with their start and end apart: 8 -> 7, of which waited for: 6 -> 5; matrix products, arithmetic and copies ran while one was open for 23% -> 35% of each run, Pallas kernels for 0% -> 0%
where the time goes in v1:
time: 552 us; the launch traced here: 541 us
  waiting for transfers between devices  209 us (38%)
  local copies, waits for them, and re-layouts  187 us (34%)
  matrix products  54.5 us (10%)
  starting transfers between devices  49.1 us (9%)
  other arithmetic  27.1 us (5%)
  between operations  14.5 us (3%)
    ppermute x1, waiting for transfers between devices, body(): lax.ppermute(partial_down, 'dp', [(i, (i + 1) % n_dp) for i in range(n_dp)])  99.4 us
    all_to_all x2, waiting for transfers between devices, dispatch(): lax.all_to_all(sent.reshape(devices, rows_per_chunk, lanes), ALL, 0, 0, t...  95.4 us
    dot_general x2, local copies, waits for them, and re-layouts, body(): jnp.einsum('ept,ehpd->thd', select, back, preferred_element_type=f32)  24.1 us
    reshape x2, local copies, waits for them, and re-layouts, dispatch(): sent.reshape(devices, rows_per_chunk, lanes)  23.9 us
    reshape x2, local copies, waits for them, and re-layouts, dispatch(): got = got.reshape(experts, n_dp, capacity, half).transpose(1, 0, 2, 3)  23.7 us
    all_to_all x2, starting transfers between devices, dispatch(): lax.all_to_all(sent.reshape(devices, rows_per_chunk, lanes), ALL, 0, 0, t...  22.7 us
    reshape x2, local copies, waits for them, and re-layouts, dispatch(): return got.reshape(slots_all, half)  21.4 us
    unnamed x17, local copies, waits for them, and re-layouts  17.9 us
  transfers between devices with their start and end apart: 7, of which 5 were waited for; matrix products, arithmetic and copies ran while one was open for 35% of the time, Pallas kernels for 0%

profile of v1, /device:TPU:1, one launch (start us, length us, event | category | flops | bytes accessed | tf_op | source)
XLA Modules:
  0.0 541.3 jit_solution(6081036967583774645)
XLA Ops:
  20.9 11.9 %reshape.158 = bf16[128,48,512]{2,1,0:T(8,128)(2,1)} reshape(bf16[64,2,12,2048]{3,2,1,0:T(8,128)(2,1)} %copy.138) | data formatting | bytes 12582912 | tf_op jit(solution)/shard_map/reshape | solution.py:49
  32.8 11.9 %all-to-all-start.1 = ((bf16[128,48,512]{2,1,0:T(8,128)(2,1)}), bf16[128,48,512]{2,1,0:T(8,128)(2,1)}, u32[]{:S(2)}, u32[]{:S(2)}) async-start(bf16[128,48,512]{2,1,0:T(8,128)(2,1)} %reshape.158), calls=%async_computation.1 | async-start | bytes 12582912 | tf_op jit(solution)/shard_map/all_to_all | solution.py:48
  47.4 72.1 %all-to-all-done.1 = bf16[128,48,512]{2,1,0:T(8,128)(2,1)} async-done(((bf16[128,48,512]{2,1,0:T(8,128)(2,1)}), bf16[128,48,512]{2,1,0:T(8,128)(2,1)}, u32[]{:S(2)}, u32[]{:S(2)}) %all-to-all-start.1) | async-done | bytes 6291488 | tf_op jit(solution)/shard_map/all_to_all | solution.py:48
  119.6 11.9 %reshape.159 = bf16[64,2,12,2048]{3,2,1,0:T(8,128)(2,1)} reshape(bf16[128,48,512]{2,1,0:T(8,128)(2,1)} %all-to-all-done.1) | data formatting | bytes 12582912 | tf_op jit(solution)/shard_map/reshape | solution.py:51
  139.7 10.7 %reshape.160 = bf16[1536,2048]{1,0:T(8,128)(2,1)} reshape(bf16[2,64,12,2048]{3,2,1,0:T(8,128)(2,1)} %copy.139) | data formatting | bytes 12582912 | tf_op jit(solution)/shard_map/reshape | solution.py:52
  150.4 9.9 %fusion.11 = f32[1536,768]{0,1:T(8,128)} fusion(bf16[1536,2048]{1,0:T(8,128)(2,1)} %reshape.160, bf16[2048,2304]{1,0:T(8,128)(2,1)} %bitcast.65), kind=kOutput, calls=%fused_computation.29 | convolution fusion | flops 4831838208 | bytes 14155776 | tf_op jit(solution)/shard_map/dot_general | solution.py:66
  165.6 99.4 %collective-permute-done = f32[1536,768]{0,1:T(8,128)} collective-permute-done((f32[1536,768]{0,1:T(8,128)}, f32[1536,768]{0,1:T(8,128)}, u32[]{:S(2)}, u32[]{:S(2)}) %collective-permute-start) | collective-permute-done | bytes 4718624 | tf_op jit(solution)/shard_map/ppermute | solution.py:67
  271.9 11.7 %all-to-all-start.3 = ((bf16[128,1,12]{2,1,0:T(2,128)(2,1)}), bf16[128,1,12]{2,1,0:T(2,128)(2,1)S(1)}, u32[]{:S(2)}, u32[]{:S(2)}) async-start(bf16[128,1,12]{2,1,0:T(2,128)(2,1)} %copy.145), calls=%async_computation.3 | async-start | bytes 131072 | tf_op jit(solution)/shard_map/all_to_all | solution.py:104
  283.8 9.6 %all-to-all-done.3 = bf16[128,1,12]{2,1,0:T(2,128)(2,1)S(1)} async-done(((bf16[128,1,12]{2,1,0:T(2,128)(2,1)}), bf16[128,1,12]{2,1,0:T(2,128)(2,1)S(1)}, u32[]{:S(2)}, u32[]{:S(2)}) %all-to-all-start.3) | async-done | bytes 3104 | tf_op jit(solution)/shard_map/all_to_all | solution.py:104
  308.7 11.9 %reshape.166 = bf16[128,48,512]{2,1,0:T(8,128)(2,1)} reshape(bf16[64,2,12,2048]{3,2,1,0:T(8,128)(2,1)} %copy.148) | data formatting | bytes 12582912 | tf_op jit(solution)/shard_map/reshape | solution.py:49
  320.6 10.8 %all-to-all-start.4 = ((bf16[128,48,512]{2,1,0:T(8,128)(2,1)}), bf16[128,48,512]{2,1,0:T(8,128)(2,1)}, u32[]{:S(2)}, u32[]{:S(2)}) async-start(bf16[128,48,512]{2,1,0:T(8,128)(2,1)} %reshape.166), calls=%async_computation.4 | async-start | bytes 12582912 | tf_op jit(solution)/shard_map/all_to_all | solution.py:48
  339.5 13.9 %convolution_convert_fusion.1 = bf16[1536,2048]{1,0:T(8,128)(2,1)} fusion(bf16[2048,2304]{1,0:T(8,128)(2,1)} %bitcast.66, bf16[1536,768]{0,1:T(8,128)(2,1)S(1)} %get-tuple-element.27, bf16[1536,768]{0,1:T(8,128)(2,1)S(1)} %get-tuple-element.26), kind=kOutput, calls=%fused_computation.2 | convolution fusion | flops 9676259328 | bytes 17301504 | tf_op jit(solution)/shard_map/dot_general | solution.py:86
  353.4 10.6 %reshape.161 = bf16[2,64,12,2048]{3,2,1,0:T(8,128)(2,1)} reshape(bf16[1536,2048]{1,0:T(8,128)(2,1)} %convolution_convert_fusion.1) | data formatting | bytes 12582912 | tf_op jit(solution)/shard_map/reshape | solution.py:97
  372.2 11.9 %reshape.162 = bf16[128,48,512]{2,1,0:T(8,128)(2,1)} reshape(bf16[64,2,12,2048]{3,2,1,0:T(8,128)(2,1)} %copy.141) | data formatting | bytes 12582912 | tf_op jit(solution)/shard_map/reshape | solution.py:98
  384.1 23.2 %all-to-all-done.4 = bf16[128,48,512]{2,1,0:T(8,128)(2,1)} async-done(((bf16[128,48,512]{2,1,0:T(8,128)(2,1)}), bf16[128,48,512]{2,1,0:T(8,128)(2,1)}, u32[]{:S(2)}, u32[]{:S(2)}) %all-to-all-start.4) | async-done | bytes 6291488 | tf_op jit(solution)/shard_map/all_to_all | solution.py:48
  416.8 11.9 %reshape.167 = bf16[64,2,12,2048]{3,2,1,0:T(8,128)(2,1)} reshape(bf16[128,48,512]{2,1,0:T(8,128)(2,1)} %all-to-all-done.4) | data formatting | bytes 12582912 | tf_op jit(solution)/shard_map/reshape | solution.py:51
  436.9 10.7 %reshape.168 = bf16[1536,2048]{1,0:T(8,128)(2,1)} reshape(bf16[2,64,12,2048]{3,2,1,0:T(8,128)(2,1)} %copy.149) | data formatting | bytes 12582912 | tf_op jit(solution)/shard_map/reshape | solution.py:52
  448.4 9.8 %fusion.14 = bf16[1,2048,768]{1,2,0:T(8,128)(2,1)S(1)} fusion(bf16[1536,2048]{1,0:T(8,128)(2,1)} %reshape.160, f32[1536]{0:T(1024)S(1)} %reshape.170, bf16[1536,1536]{0,1:T(8,128)(2,1)} %bitcast.54), kind=kOutput, calls=%fused_computation.36 | convolution fusion | flops 4844027904 | bytes 14161920 | tf_op jit(solution)/shard_map/dot_general | solution.py:92
  458.2 11.4 %fusion = bf16[1,2048,1536]{1,2,0:T(8,128)(2,1)S(1)} fusion(bf16[1536,2048]{1,0:T(8,128)(2,1)S(1)} %copy-done, bf16[1536,768]{0,1:T(8,128)(2,1)S(1)} %copy-done.3, bf16[1536,768]{0,1:T(8,128)(2,1)S(1)} %get-tuple-element.26), kind=kOutput, calls=%fused_computation.6 | convolution fusion | flops 9676259328 | bytes 17301504 | tf_op jit(solution)/shard_map/dot_general | solution.py:89
  469.6 11.3 %pad_maximum_fusion = bf16[1,2048,2304]{1,2,0:T(8,128)(2,1)} fusion(bf16[1,2048,768]{1,2,0:T(8,128)(2,1)S(1)} %fusion.14, bf16[1,2048,1536]{1,2,0:T(8,128)(2,1)S(1)} %fusion), kind=kLoop, calls=%fused_computation | loop fusion | flops 18874368 | bytes 18874368 | tf_op jit(solution)/shard_map/concatenate | solution.py:95
  480.9 12.6 %copy.151 = bf16[1,2048,2304]{2,1,0:T(8,128)(2,1)} copy(bf16[1,2048,2304]{1,2,0:T(8,128)(2,1)} %pad_maximum_fusion) | data formatting | bytes 18874368
  493.5 11.9 %reshape.163 = bf16[64,2,12,2048]{3,2,1,0:T(8,128)(2,1)} reshape(bf16[128,48,512]{2,1,0:T(8,128)(2,1)} %all-to-all-done.2) | data formatting | bytes 12582912 | tf_op jit(solution)/shard_map/reshape | solution.py:99
  505.4 13.0 %copy.142 = bf16[2,2048,64,12]{1,0,2,3:T(2,128)(2,1)} copy(bf16[2,2048,64,12]{1,3,0,2:T(8,128)(2,1)} %bitcast.48) | data formatting | bytes 12582912 | tf_op jit(solution)/shard_map/ept,ehpd->thd/dot_general | solution.py:100
  518.4 11.1 %dot_general.29 = bf16[4096,64,12]{0,1,2:T(8,128)(2,1)} reshape(bf16[2,2048,64,12]{1,0,2,3:T(2,128)(2,1)} %copy.142) | data formatting | bytes 12582912 | tf_op jit(solution)/shard_map/ept,ehpd->thd/dot_general | solution.py:100
  (59 shorter events, 91.9 us)
Async XLA Ops:
  32.8 12.2 %copy-start.1 = (bf16[1,1,768,1536]{3,2,1,0:T(8,128)(2,1)S(1)}, bf16[1,1,768,1536]{3,2,1,0:T(8,128)(2,1)}, u32[]{:S(2)}) copy-start(bf16[1,1,768,1536]{3,2,1,0:T(8,128)(2,1)} %param.10) | copy-start | bytes 7077892
  32.8 86.8 %all-to-all-start.1 = ((bf16[128,48,512]{2,1,0:T(8,128)(2,1)}), bf16[128,48,512]{2,1,0:T(8,128)(2,1)}, u32[]{:S(2)}, u32[]{:S(2)}) async-start(bf16[128,48,512]{2,1,0:T(8,128)(2,1)} %reshape.158), calls=%async_computation.1 | async-start | bytes 12582912 | tf_op jit(solution)/shard_map/all_to_all | solution.py:48
  44.7 120.9 %all-gather.3.cloned.1.call-start = ((), (), s32[]{:S(2)}) async-start(), calls=%async_computation.5 | async-start | bytes 7077888 | tf_op jit(solution)/shard_map/all_gather | solution.py:61
  160.3 104.7 %collective-permute-start = (f32[1536,768]{0,1:T(8,128)}, f32[1536,768]{0,1:T(8,128)}, u32[]{:S(2)}, u32[]{:S(2)}) collective-permute-start(f32[1536,768]{0,1:T(8,128)} %fusion.11), channel_id=1, source_target_pairs={{0,1},{1,0},{2,3},{3,2},{4,5},{5,4},{6,7},{7,6},{8,9},{9,8},{10,11... | collective-permute-start | bytes 14155784 | tf_op jit(solution)/shard_map/ppermute | solution.py:67
  265.0 18.6 %copy-start.5 = (bf16[128,8]{0,1:T(8,128)(2,1)S(1)}, bf16[128,8]{0,1:T(8,128)(2,1)}, u32[]{:S(2)}) copy-start(bf16[128,8]{0,1:T(8,128)(2,1)} %param.9) | copy-start | bytes 6148
  265.0 34.9 %copy-start.4 = (bf16[128,4096]{1,0:T(8,128)(2,1)S(1)}, bf16[128,4096]{1,0:T(8,128)(2,1)}, u32[]{:S(2)}) copy-start(bf16[128,4096]{1,0:T(8,128)(2,1)} %param.6) | copy-start | bytes 3145732
  271.9 21.5 %all-to-all-start.3 = ((bf16[128,1,12]{2,1,0:T(2,128)(2,1)}), bf16[128,1,12]{2,1,0:T(2,128)(2,1)S(1)}, u32[]{:S(2)}, u32[]{:S(2)}) async-start(bf16[128,1,12]{2,1,0:T(2,128)(2,1)} %copy.145), calls=%async_computation.3 | async-start | bytes 131072 | tf_op jit(solution)/shard_map/all_to_all | solution.py:104
  295.4 25.3 %all-to-all-start = ((bf16[128,1,12]{2,1,0:T(2,128)(2,1)}), bf16[128,1,12]{2,1,0:T(2,128)(2,1)S(1)}, u32[]{:S(2)}, u32[]{:S(2)}) async-start(bf16[128,1,12]{2,1,0:T(2,128)(2,1)} %copy.134), calls=%async_computation | async-start | bytes 131072 | tf_op jit(solution)/shard_map/all_to_all | solution.py:56
  320.6 86.7 %all-to-all-start.4 = ((bf16[128,48,512]{2,1,0:T(8,128)(2,1)}), bf16[128,48,512]{2,1,0:T(8,128)(2,1)}, u32[]{:S(2)}, u32[]{:S(2)}) async-start(bf16[128,48,512]{2,1,0:T(8,128)(2,1)} %reshape.166), calls=%async_computation.4 | async-start | bytes 12582912 | tf_op jit(solution)/shard_map/all_to_all | solution.py:48
  338.1 1.4 copy-start.2
  407.4 86.1 %all-to-all-start.2 = ((bf16[128,48,512]{2,1,0:T(8,128)(2,1)}), bf16[128,48,512]{2,1,0:T(8,128)(2,1)}, u32[]{:S(2)}, u32[]{:S(2)}) async-start(bf16[128,48,512]{2,1,0:T(8,128)(2,1)} %reshape.162), calls=%async_computation.2 | async-start | bytes 12582912 | tf_op jit(solution)/shard_map/all_to_all | solution.py:98
  448.4 9.8 %copy-start = (bf16[1536,2048]{1,0:T(8,128)(2,1)S(1)}, bf16[1536,2048]{1,0:T(8,128)(2,1)}, u32[]{:S(2)}) copy-start(bf16[1536,2048]{1,0:T(8,128)(2,1)} %reshape.168) | copy-start | bytes 18874372
  448.4 9.8 %copy-start.3 = (bf16[1536,768]{0,1:T(8,128)(2,1)S(1)}, bf16[1536,768]{0,1:T(8,128)(2,1)}, u32[]{:S(2)}) copy-start(bf16[1536,768]{0,1:T(8,128)(2,1)} %copy-done.2) | copy-start | bytes 7077892
Sparse Core Ops, SparseCore 0:
  47.6 118.0 all-gather.2

commit v2 on v1

v2 whole, which is shorter than its diff:
```python
import jax
import jax.numpy as jnp
from jax import lax
from jax.sharding import PartitionSpec as P

ALL = ("ctx", "tp", "dp")
WIRE = ("dp", "ctx", "tp")


def body(activations, out_grad, routes, gate_probs, saved_pre, expert_weights):
    tok_count = activations.shape[0]
    top_k = routes.shape[1]
    model_width = activations.shape[1]
    ctx_size = lax.axis_size("ctx")
    tp_size = lax.axis_size("tp")
    n_dp = lax.axis_size("dp")
    experts = ctx_size * tp_size
    slots_rep = saved_pre.shape[2]
    capacity = slots_rep // experts
    cap = -(-capacity // 16) * 16
    hidden = saved_pre.shape[3] // 2
    half = model_width // n_dp
    devices = experts * n_dp
    slots_all = devices * cap
    f32 = jnp.float32
    bf16 = jnp.bfloat16

    flat_routes = routes.reshape(-1)
    route_count = flat_routes.shape[0]
    idx = jnp.arange(route_count, dtype=jnp.int32)
    same = (flat_routes[:, None] == flat_routes[None, :]) & (idx[None, :] < idx[:, None])
    position = jnp.sum(same.astype(jnp.int32), axis=1)
    in_window = flat_routes < experts
    slot_index = jnp.where(in_window, flat_routes * cap + position, -1)
    slot_ids = jnp.arange(experts * cap, dtype=jnp.int32)
    route_hit = slot_index[:, None] == slot_ids[None, :]
    token_hit = jnp.any(route_hit.reshape(tok_count, top_k, -1), axis=1)
    select = token_hit.astype(bf16).T

    send_probs = jnp.sum(
        jnp.where(route_hit, gate_probs.reshape(-1)[:, None].astype(f32), 0.0), axis=0
    ).astype(bf16)
    send_probs = jnp.broadcast_to(send_probs[None], (n_dp, experts * cap)).reshape(devices, cap)

    def dispatch(x):
        x3 = x.reshape(tok_count, n_dp, half)
        sent = jnp.einsum("st,thd->hsd", select, x3, preferred_element_type=f32).astype(bf16)
        got = lax.all_to_all(sent.reshape(devices, cap, half), WIRE, 0, 0, tiled=True)
        return got.reshape(slots_all, half)

    recv_grads = dispatch(out_grad)
    recv_rows = dispatch(activations)
    got_probs = lax.all_to_all(send_probs, WIRE, 0, 0, tiled=True)
    prob_column = got_probs.reshape(slots_all, 1).astype(f32)

    saved_rows = lax.all_gather(saved_pre[0, 0], "dp", axis=0, tiled=True)
    saved_rows = saved_rows.reshape(devices, capacity, 2 * hidden)
    saved_rows = jnp.pad(saved_rows, ((0, 0), (0, cap - capacity), (0, 0))).reshape(slots_all, -1)
    weights = expert_weights[0]
    down_part = weights[:, 2 * hidden :]
    gate_up_part = weights[:, : 2 * hidden]

    partial_down = jnp.dot(recv_grads, down_part, preferred_element_type=f32)
    used_down = partial_down.reshape(devices, cap, hidden)[:, :capacity].reshape(-1, hidden)
    other_down = lax.ppermute(used_down, "dp", [(i, (i + 1) % n_dp) for i in range(n_dp)])
    other_down = jnp.pad(
        other_down.reshape(devices, capacity, hidden), ((0, 0), (0, cap - capacity), (0, 0))
    ).reshape(slots_all, hidden)
    down_grad = partial_down + other_down

    pre_gate = saved_rows[:, :hidden].astype(f32)
    pre_up = saved_rows[:, hidden:].astype(f32)
    sigmoid_gate = jax.nn.sigmoid(pre_gate)
    activated = pre_gate * sigmoid_gate
    hidden_act = activated * pre_up
    prob_slot = jnp.sum(hidden_act * down_grad, axis=1).astype(bf16)
    scaled_grad = prob_column * down_grad
    gate_up_grad = jnp.concatenate(
        [
            scaled_grad * pre_up * sigmoid_gate * (1.0 + pre_gate * (1.0 - sigmoid_gate)),
            scaled_grad * activated,
        ],
        axis=1,
    ).astype(bf16)
    scaled_hidden = (prob_column * hidden_act).astype(bf16)

    row_grad = lax.dot_general(
        gate_up_grad, gate_up_part, (((1,), (1,)), ((), ())), preferred_element_type=f32
    ).astype(bf16)
    gate_up_term = lax.dot_general(
        recv_rows, gate_up_grad, (((0,), (0,)), ((), ())), preferred_element_type=f32
    )
    down_term = lax.dot_general(
        recv_grads, scaled_hidden, (((0,), (0,)), ((), ())), preferred_element_type=f32
    )
    weight_grad = jnp.concatenate([gate_up_term, down_term], axis=1).astype(bf16)[None]

    back = lax.all_to_all(row_grad.reshape(devices, cap, half), WIRE, 0, 0, tiled=True)
    back = back.reshape(n_dp, experts * cap, half)
    input_grad = lax.dot_general(
        select, back, (((0,), (1,)), ((), ())), preferred_element_type=f32
    )
    input_grad = input_grad.reshape(tok_count, model_width).astype(bf16)

    back_probs = lax.all_to_all(prob_slot.reshape(devices, cap), WIRE, 0, 0, tiled=True)
    back_probs = back_probs.reshape(n_dp, experts * cap)[0].astype(f32)
    prob_grad = jnp.sum(jnp.where(route_hit, back_probs[None, :], 0.0), axis=1)
    prob_grad = prob_grad.astype(bf16).reshape(tok_count, top_k)
    return (input_grad, prob_grad, weight_grad)


def solution(mesh):
    placed = (
        P(ALL, None),
        P(ALL, None),
        P(ALL, None),
        P(ALL, None),
        P(("ctx", "tp"), "dp", None, None),
        P(("ctx", "tp"), "dp", None),
    )
    return jax.shard_map(
        body,
        mesh=mesh,
        in_specs=placed,
        out_specs=(
            P(ALL, None),
            P(ALL, None),
            P(("ctx", "tp"), "dp", None),
        ),
        check_vma=False,
    )
```

time: 552 us -> 608 us (1.10)
  waiting for transfers between devices: 209 us -> 354 us
  local copies, waits for them, and re-layouts: 187 us -> 64.2 us
  matrix products: 54.5 us -> 78.3 us
  starting transfers between devices: 49.1 us -> 60.9 us
    all_to_all x5, waiting for transfers between devices: 105 us -> 247 us  [the longest x2 180 us: dispatch(): lax.all_to_all(sent.reshape(devices, cap, half), WIRE, 0, 0, tiled=True)]
    reshape x10 -> x3, local copies, waits for them, and re-layouts: 103 us -> 21.3 us  [the longest x1 8.07 us: body(): saved_rows = saved_rows.reshape(devices, capacity, 2 * hidden)]
    all_gather x1, waiting for transfers between devices: 4.87 us -> 36.5 us  [body(): saved_rows = lax.all_gather(saved_pre[0, 0], 'dp', axis=0, tiled=True)]
    ppermute x1, waiting for transfers between devices: 99.4 us -> 69.2 us  [body(): lax.ppermute(used_down, 'dp', [(i, (i + 1) % n_dp) for i in range(n_dp)])]
    transpose x5 -> x0, local copies, waits for them, and re-layouts: 25 us -> none  [the longest x2 16.5 us: dispatch(): got = got.reshape(experts, n_dp, capacity, half).transpose(1, 0, 2, 3)]
    convert_element_type x5 -> x2, local copies, waits for them, and re-layouts: 14.3 us -> 0.16 us  [the longest x1 0.08 us: body(): prob_column = got_probs.reshape(slots_all, 1).astype(f32)]
    dot_general x2 -> x1, local copies, waits for them, and re-layouts: 24.1 us -> 11.9 us  [body(): lax.dot_general(select, back, (((0,), (1,)), ((), ())), preferred_element...]
    all_to_all x5, starting transfers between devices: 48.3 us -> 60 us  [the longest x1 21.9 us: body(): lax.all_to_all(row_grad.reshape(devices, cap, half), WIRE, 0, 0, tiled=True)]
  transfers between devices with their start and end apart: 7 -> 7, of which waited for: 5 -> 7; matrix products, arithmetic and copies ran while one was open for 35% -> 20% of each run, Pallas kernels for 0% -> 0%
where the time goes in v2:
time: 608 us; the launch traced here: 600 us
  waiting for transfers between devices  354 us (58%)
  matrix products  78.3 us (13%)
  local copies, waits for them, and re-layouts  64.2 us (11%)
  starting transfers between devices  60.9 us (10%)
  other arithmetic  28.2 us (5%)
  between operations  14.4 us (2%)
    all_to_all x2, waiting for transfers between devices, dispatch(): lax.all_to_all(sent.reshape(devices, cap, half), WIRE, 0, 0, tiled=True)  180 us
    ppermute x1, waiting for transfers between devices, body(): lax.ppermute(used_down, 'dp', [(i, (i + 1) % n_dp) for i in range(n_dp)])  69.2 us
    all_to_all x1, waiting for transfers between devices, body(): lax.all_to_all(row_grad.reshape(devices, cap, half), WIRE, 0, 0, tiled=True)  54.4 us
    all_gather x1, waiting for transfers between devices, body(): saved_rows = lax.all_gather(saved_pre[0, 0], 'dp', axis=0, tiled=True)  36.5 us
    all_to_all x1, starting transfers between devices, body(): lax.all_to_all(row_grad.reshape(devices, cap, half), WIRE, 0, 0, tiled=True)  21.9 us
    all_to_all x2, starting transfers between devices, dispatch(): lax.all_to_all(sent.reshape(devices, cap, half), WIRE, 0, 0, tiled=True)  18.7 us
    unnamed x15, local copies, waits for them, and re-layouts  18.4 us
    dot_general x1, matrix products, body(): lax.dot_general(gate_up_grad, gate_up_part, (((1,), (1,)), ((), ())), pre...  18 us
  transfers between devices with their start and end apart: 7, of which 7 were waited for; matrix products, arithmetic and copies ran while one was open for 20% of the time, Pallas kernels for 0%

profile of v2, /device:TPU:1, one launch (start us, length us, event | category | flops | bytes accessed | tf_op | source)
XLA Modules:
  0.0 599.6 jit_solution(45454753212676974)
XLA Ops:
  10.9 7.0 %convolution_convert_fusion.3 = bf16[1024,2,2048]{2,0,1:T(8,128)(2,1)} fusion(bf16[16,2,8,2048]{3,2,1,0:T(8,128)(2,1)} %bitcast.62, pred[128,1024]{1,0:T(8,128)(4,1)S(1)} %fusion.10), kind=kOutput, calls=%fused_computation.23 | convolution fusion | flops 1077936128 | bytes 9568256 | tf_op jit(solution)/shard_map/st,thd->hsd/dot_general | solution.py:47
  17.9 11.9 %all-to-all-start.1 = ((bf16[128,16,2048]{2,1,0:T(8,128)(2,1)}), bf16[128,16,2048]{2,1,0:T(8,128)(2,1)}, u32[]{:S(2)}, u32[]{:S(2)}) async-start(bf16[128,16,2048]{2,1,0:T(8,128)(2,1)} %bitcast.59), calls=%async_computation.1 | async-start | bytes 16777216 | tf_op jit(solution)/shard_map/all_to_all | solution.py:48
  30.6 103.2 %all-to-all-done.1 = bf16[128,16,2048]{2,1,0:T(8,128)(2,1)} async-done(((bf16[128,16,2048]{2,1,0:T(8,128)(2,1)}), bf16[128,16,2048]{2,1,0:T(8,128)(2,1)}, u32[]{:S(2)}, u32[]{:S(2)}) %all-to-all-start.1) | async-done | bytes 8388640 | tf_op jit(solution)/shard_map/all_to_all | solution.py:48
  133.8 11.6 %fusion.11 = f32[2048,768]{1,0:T(8,128)} fusion(bf16[2048,2048]{1,0:T(8,128)(2,1)} %bitcast.3, bf16[2048,2304]{1,0:T(8,128)(2,1)} %bitcast.64), kind=kOutput, calls=%fused_computation.34 | convolution fusion | flops 6442450944 | bytes 17825792 | tf_op jit(solution)/shard_map/dot_general | solution.py:63
  145.4 6.7 %reshape.173 = f32[1536,768]{1,0:T(8,128)} reshape(f32[128,12,768]{2,1,0:T(8,128)} %bitcast.57) | data formatting | bytes 9437184 | tf_op jit(solution)/shard_map/reshape | solution.py:64
  153.0 36.5 %all-gather.3.cloned.1.call-done = bf16[1,1,1536,1536]{3,2,1,0:T(8,128)(2,1)} async-done(((bf16[1,1,768,1536]{3,2,1,0:T(8,128)(2,1)}), bf16[1,1,1536,1536]{3,2,1,0:T(8,128)(2,1)}) %all-gather.3.cloned.1.call-update) | async-done | bytes 4718608 | tf_op jit(solution)/shard_map/all_gather | solution.py:56
  189.5 8.1 %reshape.176 = bf16[128,12,1536]{2,1,0:T(8,128)(2,1)} reshape(bf16[1,1,1536,1536]{3,2,1,0:T(8,128)(2,1)} %all-gather.3.cloned.1.call-done) | data formatting | bytes 9437184 | tf_op jit(solution)/shard_map/reshape | solution.py:57
  197.6 6.5 %pad.9 = bf16[128,16,1536]{2,1,0:T(8,128)(2,1)} pad(bf16[128,12,1536]{2,1,0:T(8,128)(2,1)} %reshape.176, bf16[]{:T(256)} %constant.15.clone.1), padding=0_0x0_4x0_0 | pad | bytes 11010050 | tf_op jit(solution)/shard_map/jit(_pad)/pad | solution.py:58
  204.1 69.2 %collective-permute-done = f32[1536,768]{1,0:T(8,128)} collective-permute-done((f32[1536,768]{1,0:T(8,128)}, f32[1536,768]{1,0:T(8,128)}, u32[]{:S(2)}, u32[]{:S(2)}) %collective-permute-start) | collective-permute-done | bytes 4718624 | tf_op jit(solution)/shard_map/ppermute | solution.py:65
  273.3 6.5 %reshape.174 = f32[128,12,768]{2,1,0:T(8,128)} reshape(f32[1536,768]{1,0:T(8,128)} %collective-permute-done) | data formatting | bytes 9437184 | tf_op jit(solution)/shard_map/reshape | solution.py:67
  291.3 15.0 %all-to-all-start.3 = ((bf16[128,1,16]{2,1,0:T(2,128)(2,1)}), bf16[128,1,16]{2,1,0:T(2,128)(2,1)S(1)}, u32[]{:S(2)}, u32[]{:S(2)}) async-start(bf16[128,1,16]{2,1,0:T(2,128)(2,1)} %convert_element_type.132), calls=%async_computation.3 | async-start | bytes 131072 | tf_op jit(solution)/shard_map/all_to_all | solution.py:105
  306.5 9.1 %all-to-all-done.3 = bf16[128,1,16]{2,1,0:T(2,128)(2,1)S(1)} async-done(((bf16[128,1,16]{2,1,0:T(2,128)(2,1)}), bf16[128,1,16]{2,1,0:T(2,128)(2,1)S(1)}, u32[]{:S(2)}, u32[]{:S(2)}) %all-to-all-start.3) | async-done | bytes 4128 | tf_op jit(solution)/shard_map/all_to_all | solution.py:105
  332.0 6.7 %all-to-all-start.4 = ((bf16[128,16,2048]{2,1,0:T(8,128)(2,1)}), bf16[128,16,2048]{2,1,0:T(8,128)(2,1)}, u32[]{:S(2)}, u32[]{:S(2)}) async-start(bf16[128,16,2048]{2,1,0:T(8,128)(2,1)} %bitcast.58), calls=%async_computation.4 | async-start | bytes 16777216 | tf_op jit(solution)/shard_map/all_to_all | solution.py:48
  339.0 8.2 %fusion.3 = (bf16[2048,768]{1,0:T(8,128)(2,1)S(1)}, bf16[2048,768]{1,0:T(8,128)(2,1)S(1)}) fusion(f32[2048]{0:T(1024)S(1)} %reshape.184, bf16[2048,1536]{1,0:T(8,128)(2,1)} %bitcast.52, f32[2048,768]{1,0:T(8,128)} %fusion.11, f32[128,16,768]{2,1,0:T(8,128)} %copy-done), kind=kLoop, calls=%fused_computation.11 | loop fusion | flops 26738688 | bytes 25174016 | tf_op jit(solution)/shard_map/convert.7
  348.9 18.0 %convolution_convert_fusion = bf16[2048,2048]{1,0:T(8,128)(2,1)} fusion(bf16[2048,2304]{1,0:T(8,128)(2,1)} %bitcast.65, bf16[2048,768]{1,0:T(8,128)(2,1)S(1)} %get-tuple-element.27, bf16[2048,768]{1,0:T(8,128)(2,1)S(1)} %get-tuple-element.26), kind=kOutput, calls=%fused_computation.6 | convolution fusion | flops 12901679104 | bytes 20971520 | tf_op jit(solution)/shard_map/dot_general | solution.py:87
  367.0 76.8 %all-to-all-done.4 = bf16[128,16,2048]{2,1,0:T(8,128)(2,1)} async-done(((bf16[128,16,2048]{2,1,0:T(8,128)(2,1)}), bf16[128,16,2048]{2,1,0:T(8,128)(2,1)}, u32[]{:S(2)}, u32[]{:S(2)}) %all-to-all-start.4) | async-done | bytes 8388640 | tf_op jit(solution)/shard_map/all_to_all | solution.py:48
  443.8 21.9 %all-to-all-start.2 = ((bf16[128,16,2048]{2,1,0:T(8,128)(2,1)}), bf16[128,16,2048]{2,1,0:T(8,128)(2,1)}, u32[]{:S(2)}, u32[]{:S(2)}) async-start(bf16[128,16,2048]{2,1,0:T(8,128)(2,1)} %bitcast.61), calls=%async_computation.2 | async-start | bytes 16777216 | tf_op jit(solution)/shard_map/all_to_all | solution.py:98
  466.5 12.2 %fusion.14 = bf16[1,2048,768]{1,2,0:T(8,128)(2,1)S(1)} fusion(bf16[2048,2048]{1,0:T(8,128)(2,1)} %bitcast.3, f32[2048]{0:T(1024)S(1)} %reshape.184, bf16[2048,1536]{1,0:T(8,128)(2,1)} %bitcast.53), kind=kOutput, calls=%fused_computation.37 | convolution fusion | flops 6458179584 | bytes 17833984 | tf_op jit(solution)/shard_map/dot_general | solution.py:93
  478.6 16.5 %fusion = bf16[1,2048,1536]{1,2,0:T(8,128)(2,1)S(1)} fusion(bf16[2048,2048]{1,0:T(8,128)(2,1)} %bitcast.15, bf16[2048,768]{1,0:T(8,128)(2,1)} %copy-done.1, bf16[2048,768]{1,0:T(8,128)(2,1)S(1)} %get-tuple-element.26), kind=kOutput, calls=%fused_computation.8 | convolution fusion | flops 12900630528 | bytes 20971520 | tf_op jit(solution)/shard_map/dot_general | solution.py:90
  495.1 11.3 %pad_maximum_fusion = bf16[1,2048,2304]{1,2,0:T(8,128)(2,1)} fusion(bf16[1,2048,768]{1,2,0:T(8,128)(2,1)S(1)} %fusion.14, bf16[1,2048,1536]{1,2,0:T(8,128)(2,1)S(1)} %fusion), kind=kLoop, calls=%fused_computation.3 | loop fusion | flops 18874368 | bytes 18874368 | tf_op jit(solution)/shard_map/concatenate | solution.py:96
  506.4 12.6 %copy.89 = bf16[1,2048,2304]{2,1,0:T(8,128)(2,1)} copy(bf16[1,2048,2304]{1,2,0:T(8,128)(2,1)} %pad_maximum_fusion) | data formatting | bytes 18874368
  519.0 54.4 %all-to-all-done.2 = bf16[128,16,2048]{2,1,0:T(8,128)(2,1)} async-done(((bf16[128,16,2048]{2,1,0:T(8,128)(2,1)}), bf16[128,16,2048]{2,1,0:T(8,128)(2,1)}, u32[]{:S(2)}, u32[]{:S(2)}) %all-to-all-start.2) | async-done | bytes 8388640 | tf_op jit(solution)/shard_map/all_to_all | solution.py:98
  573.4 11.9 %copy.84 = bf16[2,2048,1024]{2,1,0:T(8,128)(2,1)} copy(bf16[2,2048,1024]{1,2,0:T(8,128)(2,1)} %bitcast.10) | data formatting | bytes 16777216 | tf_op jit(solution)/shard_map/dot_general | solution.py:100
  585.3 7.2 %convolution_convert_fusion.4 = bf16[128,4096]{1,0:T(8,128)(2,1)} fusion(pred[128,1024]{1,0:T(8,128)(4,1)S(1)} %fusion.10, bf16[4096,1024]{1,0:T(8,128)(2,1)} %bitcast.60), kind=kOutput, calls=%fused_computation.24 | convolution fusion | flops 1074266112 | bytes 9568256 | tf_op jit(solution)/shard_map/dot_general | solution.py:100
  (45 shorter events, 36.0 us)
Async XLA Ops:
  17.9 115.9 %all-to-all-start.1 = ((bf16[128,16,2048]{2,1,0:T(8,128)(2,1)}), bf16[128,16,2048]{2,1,0:T(8,128)(2,1)}, u32[]{:S(2)}, u32[]{:S(2)}) async-start(bf16[128,16,2048]{2,1,0:T(8,128)(2,1)} %bitcast.59), calls=%async_computation.1 | async-start | bytes 16777216 | tf_op jit(solution)/shard_map/all_to_all | solution.py:48
  29.8 159.7 %all-gather.3.cloned.1.call-start = ((), (), s32[]{:S(2)}) async-start(), calls=%async_computation.5 | async-start | bytes 7077888 | tf_op jit(solution)/shard_map/all_gather | solution.py:56
  152.1 121.2 %collective-permute-start = (f32[1536,768]{1,0:T(8,128)}, f32[1536,768]{1,0:T(8,128)}, u32[]{:S(2)}, u32[]{:S(2)}) collective-permute-start(f32[1536,768]{1,0:T(8,128)} %reshape.173), channel_id=1, source_target_pairs={{0,1},{1,0},{2,3},{3,2},{4,5},{5,4},{6,7},{7,6},{8,9},{9,8},{10,11... | collective-permute-start | bytes 14155784 | tf_op jit(solution)/shard_map/ppermute | solution.py:65
  273.3 12.8 %slice-start = ((s8[6291456]{0:T(1024)(128)(4,1)}), s8[2097152]{0:T(1024)(128)(4,1)S(1)}, s32[]{:S(2)}) async-start(s8[6291456]{0:T(1024)(128)(4,1)} %bitcast.54), calls=%async_computation.6 | async-start | bytes 4194304
  279.8 6.2 %slice-start.1 = ((s8[6291456]{0:T(1024)(128)(4,1)}), s8[4194304]{0:T(1024)(128)(4,1)S(1)}, s32[]{:S(2)}) async-start(s8[6291456]{0:T(1024)(128)(4,1)} %bitcast.54), calls=%async_computation.7 | async-start | bytes 8388608
  283.4 2.7 copy-start
  286.1 20.2 %copy-start.3 = (bf16[128,8]{0,1:T(8,128)(2,1)S(1)}, bf16[128,8]{0,1:T(8,128)(2,1)}, u32[]{:S(2)}) copy-start(bf16[128,8]{0,1:T(8,128)(2,1)} %param.9) | copy-start | bytes 6148
  286.1 36.5 %copy-start.2 = (bf16[128,4096]{1,0:T(8,128)(2,1)S(1)}, bf16[128,4096]{1,0:T(8,128)(2,1)}, u32[]{:S(2)}) copy-start(bf16[128,4096]{1,0:T(8,128)(2,1)} %param.6) | copy-start | bytes 3145732
  291.3 24.3 %all-to-all-start.3 = ((bf16[128,1,16]{2,1,0:T(2,128)(2,1)}), bf16[128,1,16]{2,1,0:T(2,128)(2,1)S(1)}, u32[]{:S(2)}, u32[]{:S(2)}) async-start(bf16[128,1,16]{2,1,0:T(2,128)(2,1)} %convert_element_type.132), calls=%async_computation.3 | async-start | bytes 131072 | tf_op jit(solution)/shard_map/all_to_all | solution.py:105
  318.1 13.9 %all-to-all-start = ((bf16[128,1,16]{2,1,0:T(2,128)(2,1)}), bf16[128,1,16]{2,1,0:T(2,128)(2,1)S(1)}, u32[]{:S(2)}, u32[]{:S(2)}) async-start(bf16[128,1,16]{2,1,0:T(2,128)(2,1)} %copy.81), calls=%async_computation | async-start | bytes 131072 | tf_op jit(solution)/shard_map/all_to_all | solution.py:53
  332.0 111.8 %all-to-all-start.4 = ((bf16[128,16,2048]{2,1,0:T(8,128)(2,1)}), bf16[128,16,2048]{2,1,0:T(8,128)(2,1)}, u32[]{:S(2)}, u32[]{:S(2)}) async-start(bf16[128,16,2048]{2,1,0:T(8,128)(2,1)} %bitcast.58), calls=%async_computation.4 | async-start | bytes 16777216 | tf_op jit(solution)/shard_map/all_to_all | solution.py:48
  347.3 1.7 copy-start.1
  443.8 129.6 %all-to-all-start.2 = ((bf16[128,16,2048]{2,1,0:T(8,128)(2,1)}), bf16[128,16,2048]{2,1,0:T(8,128)(2,1)}, u32[]{:S(2)}, u32[]{:S(2)}) async-start(bf16[128,16,2048]{2,1,0:T(8,128)(2,1)} %bitcast.61), calls=%async_computation.2 | async-start | bytes 16777216 | tf_op jit(solution)/shard_map/all_to_all | solution.py:98
Sparse Core Ops, SparseCore 0:
  32.3 157.1 all-gather.2

commit v3 on v2

--- a/solution.py
+++ b/solution.py
@@ -40,7 +40,6 @@
     send_probs = jnp.sum(
         jnp.where(route_hit, gate_probs.reshape(-1)[:, None].astype(f32), 0.0), axis=0
     ).astype(bf16)
-    send_probs = jnp.broadcast_to(send_probs[None], (n_dp, experts * cap)).reshape(devices, cap)
 
     def dispatch(x):
         x3 = x.reshape(tok_count, n_dp, half)
@@ -50,7 +49,9 @@
 
     recv_grads = dispatch(out_grad)
     recv_rows = dispatch(activations)
-    got_probs = lax.all_to_all(send_probs, WIRE, 0, 0, tiled=True)
+    all_probs = lax.all_gather(send_probs.reshape(1, experts, cap), WIRE, axis=0, tiled=True)
+    me = lax.axis_index("ctx") * tp_size + lax.axis_index("tp")
+    got_probs = lax.dynamic_index_in_dim(all_probs, me, axis=1, keepdims=False)
     prob_column = got_probs.reshape(slots_all, 1).astype(f32)
 
     saved_rows = lax.all_gather(saved_pre[0, 0], "dp", axis=0, tiled=True)

time: 608 us -> 914 us (1.50)
  blocking collectives: 0 us -> 392 us
  waiting for transfers between devices: 354 us -> 268 us
    all_gather x0 -> x1, blocking collectives: none -> 392 us  [body(): lax.all_gather(send_probs.reshape(1, experts, cap), WIRE, axis=0, tiled=T...]
    all_to_all x2, waiting for transfers between devices: 180 us -> 103 us  [dispatch(): lax.all_to_all(sent.reshape(devices, cap, half), WIRE, 0, 0, tiled=True)]
  transfers between devices with their start and end apart: 7 -> 6, of which waited for: 7 -> 5; matrix products, arithmetic and copies ran while one was open for 20% -> 13% of each run, Pallas kernels for 0% -> 0%
where the time goes in v3:
time: 914 us; the launch traced here: 900 us
  blocking collectives  392 us (43%)
  waiting for transfers between devices  268 us (29%)
  matrix products  78.3 us (9%)
  local copies, waits for them, and re-layouts  63.3 us (7%)
  starting transfers between devices  55.1 us (6%)
  other arithmetic  28.5 us (3%)
  between operations  14.6 us (2%)
    all_gather x1, blocking collectives, body(): lax.all_gather(send_probs.reshape(1, experts, cap), WIRE, axis=0, tiled=T...  392 us
    all_to_all x2, waiting for transfers between devices, dispatch(): lax.all_to_all(sent.reshape(devices, cap, half), WIRE, 0, 0, tiled=True)  103 us
    ppermute x1, waiting for transfers between devices, body(): lax.ppermute(used_down, 'dp', [(i, (i + 1) % n_dp) for i in range(n_dp)])  69.2 us
    all_to_all x1, waiting for transfers between devices, body(): lax.all_to_all(row_grad.reshape(devices, cap, half), WIRE, 0, 0, tiled=True)  51.3 us
    all_gather x1, waiting for transfers between devices, body(): saved_rows = lax.all_gather(saved_pre[0, 0], 'dp', axis=0, tiled=True)  36.5 us
    all_to_all x1, starting transfers between devices, body(): lax.all_to_all(row_grad.reshape(devices, cap, half), WIRE, 0, 0, tiled=True)  20.6 us
    all_to_all x2, starting transfers between devices, dispatch(): lax.all_to_all(sent.reshape(devices, cap, half), WIRE, 0, 0, tiled=True)  18.6 us
    unnamed x15, local copies, waits for them, and re-layouts  18.4 us
  transfers between devices with their start and end apart: 6, of which 5 were waited for; matrix products, arithmetic and copies ran while one was open for 13% of the time, Pallas kernels for 0%

profile of v3, /device:TPU:1, one launch (start us, length us, event | category | flops | bytes accessed | tf_op | source)
XLA Modules:
  0.0 899.6 jit_solution(16033255971374799120)
XLA Ops:
  10.9 7.0 convolution_convert_fusion.3
  17.9 11.9 %all-to-all-start = ((bf16[128,16,2048]{2,1,0:T(8,128)(2,1)}), bf16[128,16,2048]{2,1,0:T(8,128)(2,1)}, u32[]{:S(2)}, u32[]{:S(2)}) async-start(bf16[128,16,2048]{2,1,0:T(8,128)(2,1)} %bitcast.57), calls=%async_computation | async-start | bytes 16777216 | tf_op jit(solution)/shard_map/all_to_all | solution.py:47
  30.6 103.2 %all-to-all-done = bf16[128,16,2048]{2,1,0:T(8,128)(2,1)} async-done(((bf16[128,16,2048]{2,1,0:T(8,128)(2,1)}), bf16[128,16,2048]{2,1,0:T(8,128)(2,1)}, u32[]{:S(2)}, u32[]{:S(2)}) %all-to-all-start) | async-done | bytes 8388640 | tf_op jit(solution)/shard_map/all_to_all | solution.py:47
  133.8 11.6 %fusion.11 = f32[2048,768]{1,0:T(8,128)} fusion(bf16[2048,2048]{1,0:T(8,128)(2,1)} %bitcast.3, bf16[2048,2304]{1,0:T(8,128)(2,1)} %bitcast.62), kind=kOutput, calls=%fused_computation.34 | convolution fusion | flops 6442450944 | bytes 17825792 | tf_op jit(solution)/shard_map/dot_general | solution.py:64
  145.4 6.8 reshape.173
  153.0 36.5 %all-gather.3.cloned.1.call-done = bf16[1,1,1536,1536]{3,2,1,0:T(8,128)(2,1)} async-done(((bf16[1,1,768,1536]{3,2,1,0:T(8,128)(2,1)}), bf16[1,1,1536,1536]{3,2,1,0:T(8,128)(2,1)}) %all-gather.3.cloned.1.call-update) | async-done | bytes 4718608 | tf_op jit(solution)/shard_map/all_gather | solution.py:57
  189.5 8.1 reshape.176
  197.6 6.5 pad.9
  204.1 69.2 %collective-permute-done = f32[1536,768]{1,0:T(8,128)} collective-permute-done((f32[1536,768]{1,0:T(8,128)}, f32[1536,768]{1,0:T(8,128)}, u32[]{:S(2)}, u32[]{:S(2)}) %collective-permute-start) | collective-permute-done | bytes 4718624 | tf_op jit(solution)/shard_map/ppermute | solution.py:66
  273.3 6.5 reshape.174
  291.3 15.0 %all-to-all-start.2 = ((bf16[128,1,16]{2,1,0:T(2,128)(2,1)}), bf16[128,1,16]{2,1,0:T(2,128)(2,1)S(1)}, u32[]{:S(2)}, u32[]{:S(2)}) async-start(bf16[128,1,16]{2,1,0:T(2,128)(2,1)} %convert_element_type.135), calls=%async_computation.2 | async-start | bytes 131072 | tf_op jit(solution)/shard_map/all_to_all | solution.py:106
  312.1 6.8 all-to-all-done.2
  318.9 6.7 all-to-all-start.3
  327.4 392.2 %all_gather.6 = bf16[128,64,16]{1,2,0:T(8,128)(2,1)S(1)} all-gather(bf16[1,64,16]{1,2,0:T(8,128)(2,1)S(1)} %copy.66), channel_id=1, replica_groups=mesh['ctx'=8,'tp'=8,'dp'=2] {'dp','ctx','tp'}, dimensions={0}, use_global_device_ids=true | all-gather | bytes 264192 | tf_op jit(solution)/shard_map/all_gather | solution.py:52
  720.2 8.3 fusion.3
  730.1 18.0 %convolution_convert_fusion = bf16[2048,2048]{1,0:T(8,128)(2,1)} fusion(bf16[2048,2304]{1,0:T(8,128)(2,1)} %bitcast.63, bf16[2048,768]{1,0:T(8,128)(2,1)S(1)} %get-tuple-element.24, bf16[2048,768]{1,0:T(8,128)(2,1)S(1)} %get-tuple-element.23), kind=kOutput, calls=%fused_computation.6 | convolution fusion | flops 12901679104 | bytes 20971520 | tf_op jit(solution)/shard_map/dot_general | solution.py:88
  748.1 20.6 %all-to-all-start.1 = ((bf16[128,16,2048]{2,1,0:T(8,128)(2,1)}), bf16[128,16,2048]{2,1,0:T(8,128)(2,1)}, u32[]{:S(2)}, u32[]{:S(2)}) async-start(bf16[128,16,2048]{2,1,0:T(8,128)(2,1)} %bitcast.59), calls=%async_computation.1 | async-start | bytes 16777216 | tf_op jit(solution)/shard_map/all_to_all | solution.py:99
  768.7 12.2 %fusion.14 = bf16[1,2048,768]{1,2,0:T(8,128)(2,1)S(1)} fusion(bf16[2048,2048]{1,0:T(8,128)(2,1)} %bitcast.3, f32[2048]{0:T(1024)S(1)} %reshape.184, bf16[2048,1536]{1,0:T(8,128)(2,1)} %bitcast.51), kind=kOutput, calls=%fused_computation.37 | convolution fusion | flops 6458179584 | bytes 17833984 | tf_op jit(solution)/shard_map/dot_general | solution.py:94
  780.9 16.5 %fusion = bf16[1,2048,1536]{1,2,0:T(8,128)(2,1)S(1)} fusion(bf16[2048,2048]{1,0:T(8,128)(2,1)} %bitcast.15, bf16[2048,768]{1,0:T(8,128)(2,1)} %copy-done.1, bf16[2048,768]{1,0:T(8,128)(2,1)S(1)} %get-tuple-element.23), kind=kOutput, calls=%fused_computation.8 | convolution fusion | flops 12900630528 | bytes 20971520 | tf_op jit(solution)/shard_map/dot_general | solution.py:91
  797.4 11.3 %pad_maximum_fusion = bf16[1,2048,2304]{1,2,0:T(8,128)(2,1)} fusion(bf16[1,2048,768]{1,2,0:T(8,128)(2,1)S(1)} %fusion.14, bf16[1,2048,1536]{1,2,0:T(8,128)(2,1)S(1)} %fusion), kind=kLoop, calls=%fused_computation.3 | loop fusion | flops 18874368 | bytes 18874368 | tf_op jit(solution)/shard_map/concatenate | solution.py:97
  808.7 12.6 %copy.74 = bf16[1,2048,2304]{2,1,0:T(8,128)(2,1)} copy(bf16[1,2048,2304]{1,2,0:T(8,128)(2,1)} %pad_maximum_fusion) | data formatting | bytes 18874368
  822.0 51.3 %all-to-all-done.1 = bf16[128,16,2048]{2,1,0:T(8,128)(2,1)} async-done(((bf16[128,16,2048]{2,1,0:T(8,128)(2,1)}), bf16[128,16,2048]{2,1,0:T(8,128)(2,1)}, u32[]{:S(2)}, u32[]{:S(2)}) %all-to-all-start.1) | async-done | bytes 8388640 | tf_op jit(solution)/shard_map/all_to_all | solution.py:99
  873.3 11.9 %copy.69 = bf16[2,2048,1024]{2,1,0:T(8,128)(2,1)} copy(bf16[2,2048,1024]{1,2,0:T(8,128)(2,1)} %bitcast.10) | data formatting | bytes 16777216 | tf_op jit(solution)/shard_map/dot_general | solution.py:101
  885.2 7.2 convolution_convert_fusion.4
  (41 shorter events, 27.3 us)
Async XLA Ops:
  17.9 115.9 %all-to-all-start = ((bf16[128,16,2048]{2,1,0:T(8,128)(2,1)}), bf16[128,16,2048]{2,1,0:T(8,128)(2,1)}, u32[]{:S(2)}, u32[]{:S(2)}) async-start(bf16[128,16,2048]{2,1,0:T(8,128)(2,1)} %bitcast.57), calls=%async_computation | async-start | bytes 16777216 | tf_op jit(solution)/shard_map/all_to_all | solution.py:47
  29.8 159.7 %all-gather.3.cloned.1.call-start = ((), (), s32[]{:S(2)}) async-start(), calls=%async_computation.4 | async-start | bytes 7077888 | tf_op jit(solution)/shard_map/all_gather | solution.py:57
  152.1 121.2 %collective-permute-start = (f32[1536,768]{1,0:T(8,128)}, f32[1536,768]{1,0:T(8,128)}, u32[]{:S(2)}, u32[]{:S(2)}) collective-permute-start(f32[1536,768]{1,0:T(8,128)} %reshape.173), channel_id=1, source_target_pairs={{0,1},{1,0},{2,3},{3,2},{4,5},{5,4},{6,7},{7,6},{8,9},{9,8},{10,11... | collective-permute-start | bytes 14155784 | tf_op jit(solution)/shard_map/ppermute | solution.py:66
  273.3 12.8 %slice-start = ((s8[6291456]{0:T(1024)(128)(4,1)}), s8[2097152]{0:T(1024)(128)(4,1)S(1)}, s32[]{:S(2)}) async-start(s8[6291456]{0:T(1024)(128)(4,1)} %bitcast.52), calls=%async_computation.5 | async-start | bytes 4194304
  279.8 6.2 slice-start.1
  283.4 2.7 copy-start
  286.1 20.2 %copy-start.2 = (bf16[128,4096]{1,0:T(8,128)(2,1)S(1)}, bf16[128,4096]{1,0:T(8,128)(2,1)}, u32[]{:S(2)}) copy-start(bf16[128,4096]{1,0:T(8,128)(2,1)} %param.6) | copy-start | bytes 3145732
  291.3 27.6 %all-to-all-start.2 = ((bf16[128,1,16]{2,1,0:T(2,128)(2,1)}), bf16[128,1,16]{2,1,0:T(2,128)(2,1)S(1)}, u32[]{:S(2)}, u32[]{:S(2)}) async-start(bf16[128,1,16]{2,1,0:T(2,128)(2,1)} %convert_element_type.135), calls=%async_computation.2 | async-start | bytes 131072 | tf_op jit(solution)/shard_map/all_to_all | solution.py:106
  318.9 6.7 copy-start.3
  318.9 429.3 %all-to-all-start.3 = ((bf16[128,16,2048]{2,1,0:T(8,128)(2,1)}), bf16[128,16,2048]{2,1,0:T(8,128)(2,1)}, u32[]{:S(2)}, u32[]{:S(2)}) async-start(bf16[128,16,2048]{2,1,0:T(8,128)(2,1)} %bitcast.56), calls=%async_computation.3 | async-start | bytes 16777216 | tf_op jit(solution)/shard_map/all_to_all | solution.py:47
  728.4 1.7 copy-start.1
  748.1 125.2 %all-to-all-start.1 = ((bf16[128,16,2048]{2,1,0:T(8,128)(2,1)}), bf16[128,16,2048]{2,1,0:T(8,128)(2,1)}, u32[]{:S(2)}, u32[]{:S(2)}) async-start(bf16[128,16,2048]{2,1,0:T(8,128)(2,1)} %bitcast.59), calls=%async_computation.1 | async-start | bytes 16777216 | tf_op jit(solution)/shard_map/all_to_all | solution.py:99
Sparse Core Ops, SparseCore 0:
  32.3 157.1 all-gather.2

commit v4 on v1

--- a/solution.py
+++ b/solution.py
@@ -36,44 +36,40 @@
     route_hit = slot_index[:, None] == slot_ids[None, :]
     token_hit = jnp.any(route_hit.reshape(tok_count, top_k, -1), axis=1)
     select = token_hit.astype(bf16).T.reshape(experts, capacity, tok_count)
+    flat_probs = gate_probs.reshape(-1).astype(f32)
+    prob_select = jnp.sum(
+        jnp.where(route_hit, flat_probs[:, None], 0.0).reshape(tok_count, top_k, -1), axis=1
+    ).astype(bf16).T.reshape(experts, capacity, tok_count)
 
-    send_probs = jnp.sum(
-        jnp.where(route_hit, gate_probs.reshape(-1)[:, None].astype(f32), 0.0), axis=0
-    ).astype(bf16).reshape(experts, 1, capacity)
-    send_probs = jnp.broadcast_to(send_probs, (experts, n_dp, capacity)).reshape(devices, capacity)
-
-    def dispatch(x):
+    def dispatch(x, sel):
         x3 = x.reshape(tok_count, n_dp, half)
-        sent = jnp.einsum("ept,thd->ehpd", select, x3, preferred_element_type=f32).astype(bf16)
+        sent = jnp.einsum("ept,thd->ehpd", sel, x3, preferred_element_type=f32).astype(bf16)
         got = lax.all_to_all(
             sent.reshape(devices, rows_per_chunk, lanes), ALL, 0, 0, tiled=True
         )
         got = got.reshape(experts, n_dp, capacity, half).transpose(1, 0, 2, 3)
         return got.reshape(slots_all, half)
 
-    recv_grads = dispatch(out_grad)
-    recv_rows = dispatch(activations)
-    got_probs = lax.all_to_all(send_probs, ALL, 0, 0, tiled=True)
-    prob_column = (
-        got_probs.reshape(experts, n_dp, capacity).transpose(1, 0, 2).reshape(slots_all, 1).astype(f32)
-    )
+    recv_pgrads = dispatch(out_grad, prob_select)
+    recv_rows = dispatch(activations, select)
 
     saved_rows = lax.all_gather(saved_pre[0, 0], "dp", axis=0, tiled=True)
     weights = expert_weights[0]
     down_part = weights[:, 2 * hidden :]
     gate_up_part = weights[:, : 2 * hidden]
 
-    partial_down = jnp.dot(recv_grads, down_part, preferred_element_type=f32)
-    other_down = lax.ppermute(partial_down, "dp", [(i, (i + 1) % n_dp) for i in range(n_dp)])
-    down_grad = partial_down + other_down
+    partial_down = jnp.dot(recv_pgrads, down_part, preferred_element_type=f32)
+    other_down = lax.ppermute(
+        partial_down.astype(bf16), "dp", [(i, (i + 1) % n_dp) for i in range(n_dp)]
+    )
+    scaled_grad = partial_down + other_down.astype(f32)
 
     pre_gate = saved_rows[:, :hidden].astype(f32)
     pre_up = saved_rows[:, hidden:].astype(f32)
     sigmoid_gate = jax.nn.sigmoid(pre_gate)
     activated = pre_gate * sigmoid_gate
     hidden_act = activated * pre_up
-    prob_slot = jnp.sum(hidden_act * down_grad, axis=1).astype(bf16)
-    scaled_grad = prob_column * down_grad
+    scaled_slot_prob = jnp.sum(hidden_act * scaled_grad, axis=1)
     gate_up_grad = jnp.concatenate(
         [
             scaled_grad * pre_up * sigmoid_gate * (1.0 + pre_gate * (1.0 - sigmoid_gate)),
@@ -81,7 +77,6 @@
         ],
         axis=1,
     ).astype(bf16)
-    scaled_hidden = (prob_column * hidden_act).astype(bf16)
 
     row_grad = lax.dot_general(
         gate_up_grad, gate_up_part, (((1,), (1,)), ((), ())), preferred_element_type=f32
@@ -90,7 +85,7 @@
         recv_rows, gate_up_grad, (((0,), (0,)), ((), ())), preferred_element_type=f32
     )
     down_term = lax.dot_general(
-        recv_grads, scaled_hidden, (((0,), (0,)), ((), ())), preferred_element_type=f32
+        recv_pgrads, hidden_act.astype(bf16), (((0,), (0,)), ((), ())), preferred_element_type=f32
     )
     weight_grad = jnp.concatenate([gate_up_term, down_term], axis=1).astype(bf16)[None]
 
@@ -100,10 +95,11 @@
     input_grad = jnp.einsum("ept,ehpd->thd", select, back, preferred_element_type=f32)
     input_grad = input_grad.reshape(tok_count, model_width).astype(bf16)
 
-    ret_probs = prob_slot.reshape(n_dp, experts, capacity).transpose(1, 0, 2).reshape(devices, capacity)
-    back_probs = lax.all_to_all(ret_probs, ALL, 0, 0, tiled=True)
-    back_probs = back_probs.reshape(experts, n_dp, capacity)[:, 0].reshape(-1).astype(f32)
-    prob_grad = jnp.sum(jnp.where(route_hit, back_probs[None, :], 0.0), axis=1)
+    ret_probs = scaled_slot_prob.reshape(n_dp, experts, capacity).transpose(1, 0, 2)
+    back_probs = lax.all_to_all(ret_probs.reshape(devices, capacity), ALL, 0, 0, tiled=True)
+    back_probs = back_probs.reshape(experts, n_dp, capacity)[:, 0].reshape(-1)
+    picked = jnp.sum(jnp.where(route_hit, back_probs[None, :], 0.0), axis=1)
+    prob_grad = jnp.where(in_window, picked / flat_probs, 0.0)
     prob_grad = prob_grad.astype(bf16).reshape(tok_count, top_k)
     return (input_grad, prob_grad, weight_grad)
 

time: 552 us -> 514 us (0.931)
  waiting for transfers between devices: 209 us -> 179 us
    all_gather x1, waiting for transfers between devices: 4.87 us -> 122 us  [body(): saved_rows = lax.all_gather(saved_pre[0, 0], 'dp', axis=0, tiled=True)]
    ppermute x1, waiting for transfers between devices: 99.4 us -> 2.62 us  [body(): lax.ppermute(partial_down.astype(bf16), 'dp', [(i, (i + 1) % n_dp) for i...]
    all_to_all x2, waiting for transfers between devices: 95.4 us -> 53.9 us  [dispatch(): lax.all_to_all(sent.reshape(devices, rows_per_chunk, lanes), ALL, 0, 0, t...]
    all_to_all x2 -> x1, waiting for transfers between devices: 9.59 us -> 0.01 us  [body(): lax.all_to_all(ret_probs.reshape(devices, capacity), ALL, 0, 0, tiled=True)]
    another operation x1 -> x0, other arithmetic: 6.45 us -> none
    all_to_all x2 -> x1, starting transfers between devices: 16.2 us -> 11.4 us  [body(): lax.all_to_all(ret_probs.reshape(devices, capacity), ALL, 0, 0, tiled=True)]
    convert_element_type x10 -> x4, local copies, waits for them, and re-layouts: 14.8 us -> 15 us  [the longest x2 14.1 us: dispatch(): jnp.einsum('ept,thd->ehpd', sel, x3, preferred_element_type=f32)]
  transfers between devices with their start and end apart: 7 -> 6, of which waited for: 5 -> 3; matrix products, arithmetic and copies ran while one was open for 35% -> 39% of each run, Pallas kernels for 0% -> 0%
where the time goes in v4:
time: 514 us; the launch traced here: 504 us
  local copies, waits for them, and re-layouts  187 us (36%)
  waiting for transfers between devices  179 us (35%)
  matrix products  55 us (11%)
  starting transfers between devices  45.3 us (9%)
  other arithmetic  22.8 us (4%)
  between operations  14.7 us (3%)
    all_gather x1, waiting for transfers between devices, body(): saved_rows = lax.all_gather(saved_pre[0, 0], 'dp', axis=0, tiled=True)  122 us
    all_to_all x2, waiting for transfers between devices, dispatch(): lax.all_to_all(sent.reshape(devices, rows_per_chunk, lanes), ALL, 0, 0, t...  53.9 us
    dot_general x2, local copies, waits for them, and re-layouts, body(): jnp.einsum('ept,ehpd->thd', select, back, preferred_element_type=f32)  24.1 us
    reshape x2, local copies, waits for them, and re-layouts, dispatch(): sent.reshape(devices, rows_per_chunk, lanes)  23.9 us
    reshape x2, local copies, waits for them, and re-layouts, dispatch(): got = got.reshape(experts, n_dp, capacity, half).transpose(1, 0, 2, 3)  23.7 us
    all_to_all x2, starting transfers between devices, dispatch(): lax.all_to_all(sent.reshape(devices, rows_per_chunk, lanes), ALL, 0, 0, t...  21.6 us
    reshape x2, local copies, waits for them, and re-layouts, dispatch(): return got.reshape(slots_all, half)  21.4 us
    transpose x2, local copies, waits for them, and re-layouts, dispatch(): got = got.reshape(experts, n_dp, capacity, half).transpose(1, 0, 2, 3)  17.4 us
  transfers between devices with their start and end apart: 6, of which 3 were waited for; matrix products, arithmetic and copies ran while one was open for 39% of the time, Pallas kernels for 0%

profile of v4, /device:TPU:1, one launch (start us, length us, event | category | flops | bytes accessed | tf_op | source)
XLA Modules:
  0.0 503.5 jit_solution(2339299565005924048)
XLA Ops:
  21.6 11.9 %reshape.140 = bf16[128,48,512]{2,1,0:T(8,128)(2,1)} reshape(bf16[64,2,12,2048]{3,2,1,0:T(8,128)(2,1)} %copy.99) | data formatting | bytes 12582912 | tf_op jit(solution)/shard_map/reshape | solution.py:48
  33.5 12.5 %all-to-all-start = ((bf16[128,48,512]{2,1,0:T(8,128)(2,1)}), bf16[128,48,512]{2,1,0:T(8,128)(2,1)}, u32[]{:S(2)}, u32[]{:S(2)}) async-start(bf16[128,48,512]{2,1,0:T(8,128)(2,1)} %reshape.140), calls=%async_computation | async-start | bytes 12582912 | tf_op jit(solution)/shard_map/all_to_all | solution.py:47
  56.2 11.9 %reshape.149 = bf16[128,48,512]{2,1,0:T(8,128)(2,1)} reshape(bf16[64,2,12,2048]{3,2,1,0:T(8,128)(2,1)} %copy.111) | data formatting | bytes 12582912 | tf_op jit(solution)/shard_map/reshape | solution.py:48
  68.1 53.9 %all-to-all-done = bf16[128,48,512]{2,1,0:T(8,128)(2,1)} async-done(((bf16[128,48,512]{2,1,0:T(8,128)(2,1)}), bf16[128,48,512]{2,1,0:T(8,128)(2,1)}, u32[]{:S(2)}, u32[]{:S(2)}) %all-to-all-start) | async-done | bytes 6291488 | tf_op jit(solution)/shard_map/all_to_all | solution.py:47
  122.0 9.1 %all-to-all-start.3 = ((bf16[128,48,512]{2,1,0:T(8,128)(2,1)}), bf16[128,48,512]{2,1,0:T(8,128)(2,1)}, u32[]{:S(2)}, u32[]{:S(2)}) async-start(bf16[128,48,512]{2,1,0:T(8,128)(2,1)} %reshape.149), calls=%async_computation.3 | async-start | bytes 12582912 | tf_op jit(solution)/shard_map/all_to_all | solution.py:47
  133.8 11.9 %reshape.141 = bf16[64,2,12,2048]{3,2,1,0:T(8,128)(2,1)} reshape(bf16[128,48,512]{2,1,0:T(8,128)(2,1)} %all-to-all-done) | data formatting | bytes 12582912 | tf_op jit(solution)/shard_map/reshape | solution.py:50
  145.7 9.2 %copy.100 = bf16[2,64,12,2048]{3,2,1,0:T(8,128)(2,1)} copy(bf16[2,64,12,2048]{3,2,0,1:T(8,128)(2,1)} %bitcast.53) | data formatting | bytes 12582912 | tf_op jit(solution)/shard_map/transpose | solution.py:50
  154.9 10.7 %reshape.142 = bf16[1536,2048]{1,0:T(8,128)(2,1)} reshape(bf16[2,64,12,2048]{3,2,1,0:T(8,128)(2,1)} %copy.100) | data formatting | bytes 12582912 | tf_op jit(solution)/shard_map/reshape | solution.py:51
  165.6 10.0 %fusion.25 = (bf16[1536,768]{0,1:T(8,128)(2,1)}, f32[1536,768]{0,1:T(8,128)}) fusion(bf16[1536,2048]{1,0:T(8,128)(2,1)} %reshape.142, bf16[2048,2304]{1,0:T(8,128)(2,1)} %bitcast.67), kind=kOutput, calls=%fused_computation.53 | convolution fusion | flops 4833017856 | bytes 16515072 | tf_op jit(solution)/shard_map/dot_general | solution.py:61
  177.1 122.1 %all-gather.3.cloned.1.call-done = bf16[1,1,1536,1536]{2,3,1,0:T(8,128)(2,1)} async-done(((bf16[1,1,768,1536]{2,3,1,0:T(8,128)(2,1)}), bf16[1,1,1536,1536]{2,3,1,0:T(8,128)(2,1)}) %all-gather.3.cloned.1.call-update) | async-done | bytes 4718608 | tf_op jit(solution)/shard_map/all_gather | solution.py:56
  311.0 11.4 %all-to-all-start.2 = ((f32[128,1,12]{2,1,0:T(1,128)}), f32[128,1,12]{2,1,0:T(1,128)S(1)}, u32[]{:S(2)}, u32[]{:S(2)}) async-start(f32[128,1,12]{2,1,0:T(1,128)} %bitcast.13), calls=%async_computation.2 | async-start | bytes 131072 | tf_op jit(solution)/shard_map/all_to_all | solution.py:99
  322.3 14.6 %convolution_convert_fusion.1 = bf16[1536,2048]{1,0:T(8,128)(2,1)} fusion(bf16[2048,2304]{1,0:T(8,128)(2,1)} %bitcast.68, bf16[1536,768]{0,1:T(8,128)(2,1)S(1)} %get-tuple-element.19, bf16[1536,768]{0,1:T(8,128)(2,1)} %get-tuple-element.20), kind=kOutput, calls=%fused_computation.2 | convolution fusion | flops 9676259328 | bytes 17301504 | tf_op jit(solution)/shard_map/dot_general | solution.py:81
  337.0 10.6 %reshape.143 = bf16[2,64,12,2048]{3,2,1,0:T(8,128)(2,1)} reshape(bf16[1536,2048]{1,0:T(8,128)(2,1)} %convolution_convert_fusion.1) | data formatting | bytes 12582912 | tf_op jit(solution)/shard_map/reshape | solution.py:92
  355.8 11.9 %reshape.144 = bf16[128,48,512]{2,1,0:T(8,128)(2,1)} reshape(bf16[64,2,12,2048]{3,2,1,0:T(8,128)(2,1)} %copy.102) | data formatting | bytes 12582912 | tf_op jit(solution)/shard_map/reshape | solution.py:93
  367.8 10.6 %all-to-all-start.1 = ((bf16[128,48,512]{2,1,0:T(8,128)(2,1)}), bf16[128,48,512]{2,1,0:T(8,128)(2,1)}, u32[]{:S(2)}, u32[]{:S(2)}) async-start(bf16[128,48,512]{2,1,0:T(8,128)(2,1)} %reshape.144), calls=%async_computation.1 | async-start | bytes 12582912 | tf_op jit(solution)/shard_map/all_to_all | solution.py:93
  378.4 11.9 %reshape.150 = bf16[64,2,12,2048]{3,2,1,0:T(8,128)(2,1)} reshape(bf16[128,48,512]{2,1,0:T(8,128)(2,1)} %all-to-all-done.3) | data formatting | bytes 12582912 | tf_op jit(solution)/shard_map/reshape | solution.py:50
  398.5 10.7 %reshape.151 = bf16[1536,2048]{1,0:T(8,128)(2,1)} reshape(bf16[2,64,12,2048]{3,2,1,0:T(8,128)(2,1)} %copy.112) | data formatting | bytes 12582912 | tf_op jit(solution)/shard_map/reshape | solution.py:51
  409.2 9.4 %fusion.15 = bf16[1,2048,768]{1,2,0:T(8,128)(2,1)S(1)} fusion(bf16[1536,2048]{1,0:T(8,128)(2,1)} %reshape.142, bf16[1536,1536]{0,1:T(8,128)(2,1)} %bitcast.57), kind=kOutput, calls=%fused_computation.37 | convolution fusion | flops 4842848256 | bytes 14155776 | tf_op jit(solution)/shard_map/dot_general | solution.py:87
  418.6 11.4 %fusion = bf16[1,2048,1536]{1,2,0:T(8,128)(2,1)S(1)} fusion(bf16[1536,2048]{1,0:T(8,128)(2,1)S(1)} %copy-done, bf16[1536,768]{0,1:T(8,128)(2,1)S(1)} %get-tuple-element.19, bf16[1536,768]{0,1:T(8,128)(2,1)S(1)} %copy-done.1), kind=kOutput, calls=%fused_computation.6 | convolution fusion | flops 9676259328 | bytes 17301504 | tf_op jit(solution)/shard_map/dot_general | solution.py:84
  430.0 11.3 %pad_maximum_fusion = bf16[1,2048,2304]{1,2,0:T(8,128)(2,1)} fusion(bf16[1,2048,768]{1,2,0:T(8,128)(2,1)S(1)} %fusion.15, bf16[1,2048,1536]{1,2,0:T(8,128)(2,1)S(1)} %fusion), kind=kLoop, calls=%fused_computation | loop fusion | flops 18874368 | bytes 18874368 | tf_op jit(solution)/shard_map/concatenate | solution.py:90
  441.3 12.6 %copy.113 = bf16[1,2048,2304]{2,1,0:T(8,128)(2,1)} copy(bf16[1,2048,2304]{1,2,0:T(8,128)(2,1)} %pad_maximum_fusion) | data formatting | bytes 18874368
  455.4 11.9 %reshape.145 = bf16[64,2,12,2048]{3,2,1,0:T(8,128)(2,1)} reshape(bf16[128,48,512]{2,1,0:T(8,128)(2,1)} %all-to-all-done.1) | data formatting | bytes 12582912 | tf_op jit(solution)/shard_map/reshape | solution.py:94
  467.3 13.1 %copy.103 = bf16[2,2048,64,12]{1,0,2,3:T(2,128)(2,1)} copy(bf16[2,2048,64,12]{1,3,0,2:T(8,128)(2,1)} %bitcast.52) | data formatting | bytes 12582912 | tf_op jit(solution)/shard_map/ept,ehpd->thd/dot_general | solution.py:95
  480.4 11.1 %dot_general.29 = bf16[4096,64,12]{0,1,2:T(8,128)(2,1)} reshape(bf16[2,2048,64,12]{1,0,2,3:T(2,128)(2,1)} %copy.103) | data formatting | bytes 12582912 | tf_op jit(solution)/shard_map/ept,ehpd->thd/dot_general | solution.py:95
  (53 shorter events, 63.3 us)
Async XLA Ops:
  33.5 13.8 %copy-start.4 = (bf16[128,4096]{1,0:T(8,128)(2,1)S(1)}, bf16[128,4096]{1,0:T(8,128)(2,1)}, u32[]{:S(2)}) copy-start(bf16[128,4096]{1,0:T(8,128)(2,1)} %param.6) | copy-start | bytes 3145732
  33.5 88.5 %all-to-all-start = ((bf16[128,48,512]{2,1,0:T(8,128)(2,1)}), bf16[128,48,512]{2,1,0:T(8,128)(2,1)}, u32[]{:S(2)}, u32[]{:S(2)}) async-start(bf16[128,48,512]{2,1,0:T(8,128)(2,1)} %reshape.140), calls=%async_computation | async-start | bytes 12582912 | tf_op jit(solution)/shard_map/all_to_all | solution.py:47
  68.1 63.2 %copy-start.3 = (bf16[1,1,768,1536]{3,2,1,0:T(8,128)(2,1)S(1)}, bf16[1,1,768,1536]{3,2,1,0:T(8,128)(2,1)}, u32[]{:S(2)}) copy-start(bf16[1,1,768,1536]{3,2,1,0:T(8,128)(2,1)} %param.10) | copy-start | bytes 7077892
  122.0 189.0 %all-to-all-start.3 = ((bf16[128,48,512]{2,1,0:T(8,128)(2,1)}), bf16[128,48,512]{2,1,0:T(8,128)(2,1)}, u32[]{:S(2)}, u32[]{:S(2)}) async-start(bf16[128,48,512]{2,1,0:T(8,128)(2,1)} %reshape.149), calls=%async_computation.3 | async-start | bytes 12582912 | tf_op jit(solution)/shard_map/all_to_all | solution.py:47
  131.1 168.0 %all-gather.3.cloned.1.call-start = ((), (), s32[]{:S(2)}) async-start(), calls=%async_computation.4 | async-start | bytes 7077888 | tf_op jit(solution)/shard_map/all_gather | solution.py:56
  175.6 126.2 %collective-permute-start = (bf16[1536,768]{0,1:T(8,128)(2,1)}, bf16[1536,768]{0,1:T(8,128)(2,1)S(1)}, u32[]{:S(2)}, u32[]{:S(2)}) collective-permute-start(bf16[1536,768]{0,1:T(8,128)(2,1)} %get-tuple-element.21), channel_id=1, source_target_pairs={{0,1},{1,0},{2,3},{3,2},{4,5},{5,4},{6,7},{7,6},{8,9},{9,8},{10,11... | collective-permute-start | bytes 7077896 | tf_op jit(solution)/shard_map/ppermute | solution.py:62
  301.7 1.4 copy-start.2
  311.0 56.8 %all-to-all-start.2 = ((f32[128,1,12]{2,1,0:T(1,128)}), f32[128,1,12]{2,1,0:T(1,128)S(1)}, u32[]{:S(2)}, u32[]{:S(2)}) async-start(f32[128,1,12]{2,1,0:T(1,128)} %bitcast.13), calls=%async_computation.2 | async-start | bytes 131072 | tf_op jit(solution)/shard_map/all_to_all | solution.py:99
  367.8 87.6 %all-to-all-start.1 = ((bf16[128,48,512]{2,1,0:T(8,128)(2,1)}), bf16[128,48,512]{2,1,0:T(8,128)(2,1)}, u32[]{:S(2)}, u32[]{:S(2)}) async-start(bf16[128,48,512]{2,1,0:T(8,128)(2,1)} %reshape.144), calls=%async_computation.1 | async-start | bytes 12582912 | tf_op jit(solution)/shard_map/all_to_all | solution.py:93
  409.2 9.4 %copy-start = (bf16[1536,2048]{1,0:T(8,128)(2,1)S(1)}, bf16[1536,2048]{1,0:T(8,128)(2,1)}, u32[]{:S(2)}) copy-start(bf16[1536,2048]{1,0:T(8,128)(2,1)} %reshape.151) | copy-start | bytes 18874372
  409.2 9.4 %copy-start.1 = (bf16[1536,768]{0,1:T(8,128)(2,1)S(1)}, bf16[1536,768]{0,1:T(8,128)(2,1)}, u32[]{:S(2)}) copy-start(bf16[1536,768]{0,1:T(8,128)(2,1)} %get-tuple-element.20) | copy-start | bytes 7077892
  441.3 13.5 %copy-start.5 = (s32[128,8]{0,1:T(8,128)S(1)}, s32[128,8]{0,1:T(8,128)}, u32[]{:S(2)}) copy-start(s32[128,8]{0,1:T(8,128)} %param.8) | copy-start | bytes 12292
  441.3 13.5 %copy-start.6 = (bf16[128,8]{0,1:T(8,128)(2,1)S(1)}, bf16[128,8]{0,1:T(8,128)(2,1)}, u32[]{:S(2)}) copy-start(bf16[128,8]{0,1:T(8,128)(2,1)} %param.9) | copy-start | bytes 6148
Sparse Core Ops, SparseCore 0:
  133.9 165.1 all-gather.2

commit v5 on v4

--- a/solution.py
+++ b/solution.py
@@ -4,6 +4,7 @@
 from jax.sharding import PartitionSpec as P
 
 ALL = ("ctx", "tp", "dp")
+WIRE = ("dp", "ctx", "tp")
 
 
 def body(activations, out_grad, routes, gate_probs, saved_pre, expert_weights):
@@ -35,25 +36,34 @@
     slot_ids = jnp.arange(experts * capacity, dtype=jnp.int32)
     route_hit = slot_index[:, None] == slot_ids[None, :]
     token_hit = jnp.any(route_hit.reshape(tok_count, top_k, -1), axis=1)
-    select = token_hit.astype(bf16).T.reshape(experts, capacity, tok_count)
+    select = token_hit.astype(bf16).T
     flat_probs = gate_probs.reshape(-1).astype(f32)
     prob_select = jnp.sum(
         jnp.where(route_hit, flat_probs[:, None], 0.0).reshape(tok_count, top_k, -1), axis=1
-    ).astype(bf16).T.reshape(experts, capacity, tok_count)
+    ).astype(bf16).T
 
     def dispatch(x, sel):
         x3 = x.reshape(tok_count, n_dp, half)
-        sent = jnp.einsum("ept,thd->ehpd", sel, x3, preferred_element_type=f32).astype(bf16)
+        sent = jnp.einsum("st,thd->hsd", sel, x3, preferred_element_type=f32).astype(bf16)
         got = lax.all_to_all(
-            sent.reshape(devices, rows_per_chunk, lanes), ALL, 0, 0, tiled=True
+            sent.reshape(devices, rows_per_chunk, lanes), WIRE, 0, 0, tiled=True
         )
-        got = got.reshape(experts, n_dp, capacity, half).transpose(1, 0, 2, 3)
         return got.reshape(slots_all, half)
 
     recv_pgrads = dispatch(out_grad, prob_select)
     recv_rows = dispatch(activations, select)
 
-    saved_rows = lax.all_gather(saved_pre[0, 0], "dp", axis=0, tiled=True)
+    own_saved = saved_pre[0, 0]
+    if n_dp == 2:
+        other_saved = lax.ppermute(own_saved, "dp", [(0, 1), (1, 0)])
+        first = lax.axis_index("dp") == 0
+        saved_rows = jnp.where(
+            first,
+            jnp.concatenate([own_saved, other_saved], axis=0),
+            jnp.concatenate([other_saved, own_saved], axis=0),
+        )
+    else:
+        saved_rows = lax.all_gather(own_saved, "dp", axis=0, tiled=True)
     weights = expert_weights[0]
     down_part = weights[:, 2 * hidden :]
     gate_up_part = weights[:, : 2 * hidden]
@@ -89,15 +99,13 @@
     )
     weight_grad = jnp.concatenate([gate_up_term, down_term], axis=1).astype(bf16)[None]
 
-    ret = row_grad.reshape(n_dp, experts, capacity, half).transpose(1, 0, 2, 3)
-    back = lax.all_to_all(ret.reshape(devices, rows_per_chunk, lanes), ALL, 0, 0, tiled=True)
-    back = back.reshape(experts, n_dp, capacity, half)
-    input_grad = jnp.einsum("ept,ehpd->thd", select, back, preferred_element_type=f32)
+    back = lax.all_to_all(row_grad.reshape(devices, rows_per_chunk, lanes), WIRE, 0, 0, tiled=True)
+    back = back.reshape(n_dp, experts * capacity, half)
+    input_grad = jnp.einsum("st,hsd->thd", select, back, preferred_element_type=f32)
     input_grad = input_grad.reshape(tok_count, model_width).astype(bf16)
 
-    ret_probs = scaled_slot_prob.reshape(n_dp, experts, capacity).transpose(1, 0, 2)
-    back_probs = lax.all_to_all(ret_probs.reshape(devices, capacity), ALL, 0, 0, tiled=True)
-    back_probs = back_probs.reshape(experts, n_dp, capacity)[:, 0].reshape(-1)
+    back_probs = lax.all_to_all(scaled_slot_prob.reshape(devices, capacity), WIRE, 0, 0, tiled=True)
+    back_probs = back_probs.reshape(n_dp, experts * capacity)[0]
     picked = jnp.sum(jnp.where(route_hit, back_probs[None, :], 0.0), axis=1)
     prob_grad = jnp.where(in_window, picked / flat_probs, 0.0)
     prob_grad = prob_grad.astype(bf16).reshape(tok_count, top_k)

time: 514 us -> 454 us (0.88); the launches traced: 504 us -> 450 us
  local copies, waits for them, and re-layouts: 187 us -> 91.4 us
  waiting for transfers between devices: 179 us -> 224 us
  between operations: 14.7 us -> 0.8 us
  matrix products: 55 us -> 61.6 us
    all_gather x1 -> x0, waiting for transfers between devices: 122 us -> none  [body(): saved_rows = lax.all_gather(saved_pre[0, 0], 'dp', axis=0, tiled=True)]
    ppermute x0 -> x1, waiting for transfers between devices: none -> 95.2 us  [body(): other_saved = lax.ppermute(own_saved, 'dp', [(0, 1), (1, 0)])]
    ppermute x1, waiting for transfers between devices: 2.62 us -> 46.6 us  [body(): lax.ppermute(partial_down.astype(bf16), 'dp', [(i, (i + 1) % n_dp) for i...]
    reshape x8 -> x2, local copies, waits for them, and re-layouts: 58.4 us -> 21.4 us  [the longest x1 10.7 us: body(): row_grad.reshape(devices, rows_per_chunk, lanes)]
    all_to_all x4, waiting for transfers between devices: 53.9 us -> 82.6 us  [the longest x2 61.8 us: dispatch(): lax.all_to_all(sent.reshape(devices, rows_per_chunk, lanes), WIRE, 0, 0,...]
    transpose x5 -> x0, local copies, waits for them, and re-layouts: 26.6 us -> none  [the longest x2 17.4 us: dispatch(): got = got.reshape(experts, n_dp, capacity, half).transpose(1, 0, 2, 3)]
    dot_general x2 -> x1, local copies, waits for them, and re-layouts: 24.1 us -> 8.64 us  [body(): jnp.einsum('st,hsd->thd', select, back, preferred_element_type=f32)]
    convert_element_type x3 -> x0, local copies, waits for them, and re-layouts: 14.2 us -> none  [the longest x2 14.1 us: dispatch(): jnp.einsum('ept,thd->ehpd', sel, x3, preferred_element_type=f32)]
  transfers between devices with their start and end apart: 6 -> 6, of which waited for: 3 -> 4; matrix products, arithmetic and copies ran while one was open for 39% -> 29% of each run, Pallas kernels for 0% -> 0%
where the time goes in v5:
time: 454 us; the launch traced here: 450 us
  waiting for transfers between devices  224 us (49%)
  local copies, waits for them, and re-layouts  91.4 us (20%)
  matrix products  61.6 us (14%)
  starting transfers between devices  46.1 us (10%)
  other arithmetic  25.3 us (6%)
    ppermute x1, waiting for transfers between devices, body(): other_saved = lax.ppermute(own_saved, 'dp', [(0, 1), (1, 0)])  95.2 us
    all_to_all x2, waiting for transfers between devices, dispatch(): lax.all_to_all(sent.reshape(devices, rows_per_chunk, lanes), WIRE, 0, 0,...  61.8 us
    ppermute x1, waiting for transfers between devices, body(): lax.ppermute(partial_down.astype(bf16), 'dp', [(i, (i + 1) % n_dp) for i...  46.6 us
    all_to_all x2, starting transfers between devices, dispatch(): lax.all_to_all(sent.reshape(devices, rows_per_chunk, lanes), WIRE, 0, 0,...  22.5 us
    reshape x2, local copies, waits for them, and re-layouts, dispatch(): sent.reshape(devices, rows_per_chunk, lanes)  21.5 us
    reshape x2, local copies, waits for them, and re-layouts, dispatch(): return got.reshape(slots_all, half)  21.4 us
    all_to_all x1, waiting for transfers between devices, body(): lax.all_to_all(row_grad.reshape(devices, rows_per_chunk, lanes), WIRE, 0,...  20.8 us
    unnamed x17, local copies, waits for them, and re-layouts  16.3 us
  transfers between devices with their start and end apart: 6, of which 4 were waited for; matrix products, arithmetic and copies ran while one was open for 29% of the time, Pallas kernels for 0%

profile of v5, /device:TPU:1, one launch (start us, length us, event | category | flops | bytes accessed | tf_op | source)
XLA Modules:
  0.0 449.5 jit_solution(15964494901388721542)
XLA Ops:
  4.8 5.8 %convert_bitcast_fusion.1 = bf16[2,768,2048]{2,1,0:T(8,128)(2,1)} fusion(bf16[16,2,8,2048]{3,2,1,0:T(8,128)(2,1)} %bitcast.36, bf16[128,768]{1,0:T(8,128)(2,1)S(1)} %select_reduce_fusion.1), kind=kOutput, calls=%fused_computation.9 | convolution fusion | flops 808452096 | bytes 7536640 | tf_op jit(solution)/shard_map/st,thd->hsd/dot_general | solution.py:47
  10.6 10.7 %reshape.120 = bf16[128,48,512]{2,1,0:T(8,128)(2,1)} reshape(bf16[2,768,2048]{2,1,0:T(8,128)(2,1)} %convert_bitcast_fusion.1) | data formatting | bytes 12582912 | tf_op jit(solution)/shard_map/reshape | solution.py:49
  21.3 11.9 %all-to-all-start = ((bf16[128,48,512]{2,1,0:T(8,128)(2,1)}), bf16[128,48,512]{2,1,0:T(8,128)(2,1)}, u32[]{:S(2)}, u32[]{:S(2)}) async-start(bf16[128,48,512]{2,1,0:T(8,128)(2,1)} %reshape.120), calls=%async_computation | async-start | bytes 12582912 | tf_op jit(solution)/shard_map/all_to_all | solution.py:48
  38.7 10.8 %reshape.125 = bf16[128,48,512]{2,1,0:T(8,128)(2,1)} reshape(bf16[2,768,2048]{2,1,0:T(8,128)(2,1)} %convert_bitcast_fusion) | data formatting | bytes 12582912 | tf_op jit(solution)/shard_map/reshape | solution.py:49
  49.5 61.8 %all-to-all-done = bf16[128,48,512]{2,1,0:T(8,128)(2,1)} async-done(((bf16[128,48,512]{2,1,0:T(8,128)(2,1)}), bf16[128,48,512]{2,1,0:T(8,128)(2,1)}, u32[]{:S(2)}, u32[]{:S(2)}) %all-to-all-start) | async-done | bytes 6291488 | tf_op jit(solution)/shard_map/all_to_all | solution.py:48
  111.3 10.6 %all-to-all-start.3 = ((bf16[128,48,512]{2,1,0:T(8,128)(2,1)}), bf16[128,48,512]{2,1,0:T(8,128)(2,1)}, u32[]{:S(2)}, u32[]{:S(2)}) async-start(bf16[128,48,512]{2,1,0:T(8,128)(2,1)} %reshape.125), calls=%async_computation.3 | async-start | bytes 12582912 | tf_op jit(solution)/shard_map/all_to_all | solution.py:48
  126.3 10.7 %reshape.121 = bf16[1536,2048]{1,0:T(8,128)(2,1)} reshape(bf16[128,48,512]{2,1,0:T(8,128)(2,1)} %all-to-all-done) | data formatting | bytes 12582912 | tf_op jit(solution)/shard_map/reshape | solution.py:51
  137.0 10.0 %fusion.26 = (bf16[1536,768]{0,1:T(8,128)(2,1)}, f32[1536,768]{0,1:T(8,128)}) fusion(bf16[1536,2048]{1,0:T(8,128)(2,1)} %reshape.121, bf16[2048,2304]{1,0:T(8,128)(2,1)} %bitcast.38), kind=kOutput, calls=%fused_computation.53 | convolution fusion | flops 4833017856 | bytes 16515072 | tf_op jit(solution)/shard_map/dot_general | solution.py:71
  147.0 95.2 %collective-permute-done.1 = bf16[768,1536]{0,1:T(8,128)(2,1)} collective-permute-done((bf16[768,1536]{0,1:T(8,128)(2,1)S(1)}, bf16[768,1536]{0,1:T(8,128)(2,1)}, u32[]{:S(2)}, u32[]{:S(2)}) %collective-permute-start.1) | collective-permute-done | bytes 2359328 | tf_op jit(solution)/shard_map/ppermute | solution.py:58
  246.1 46.6 %collective-permute-done = bf16[1536,768]{0,1:T(8,128)(2,1)} collective-permute-done((bf16[1536,768]{0,1:T(8,128)(2,1)}, bf16[1536,768]{0,1:T(8,128)(2,1)}, u32[]{:S(2)}, u32[]{:S(2)}) %collective-permute-start) | collective-permute-done | bytes 2359328 | tf_op jit(solution)/shard_map/ppermute | solution.py:72
  292.7 5.7 %multiply_reduce_fusion = (f32[1536]{0:T(1024)S(1)}, bf16[1536,768]{0,1:T(8,128)(2,1)S(1)}, bf16[1536,768]{0,1:T(8,128)(2,1)}) fusion(f32[1536,768]{0,1:T(8,128)S(1)} %copy-done.2, bf16[1536,768]{0,1:T(8,128)(2,1)} %collective-permute-done, bf16[1536,1536]{0,1:T(8,128)(2,1)S(1)} %maximum_select_fusion), kind=kLoop, calls=%fused_computation.22 | loop fusion | flops 23591424 | bytes 16521216 | tf_op jit(solution)/shard_map/reduce_sum | solution.py:82
  299.2 11.8 %all-to-all-start.2 = ((f32[128,1,12]{2,1,0:T(1,128)}), f32[128,1,12]{2,1,0:T(1,128)S(1)}, u32[]{:S(2)}, u32[]{:S(2)}) async-start(f32[128,1,12]{2,1,0:T(1,128)} %bitcast.6), calls=%async_computation.2 | async-start | bytes 131072 | tf_op jit(solution)/shard_map/all_to_all | solution.py:107
  311.0 14.6 %convolution_convert_fusion.1 = bf16[1536,2048]{1,0:T(8,128)(2,1)} fusion(bf16[2048,2304]{1,0:T(8,128)(2,1)} %bitcast.39, bf16[1536,768]{0,1:T(8,128)(2,1)S(1)} %get-tuple-element.22, bf16[1536,768]{0,1:T(8,128)(2,1)} %get-tuple-element.23), kind=kOutput, calls=%fused_computation.2 | convolution fusion | flops 9676259328 | bytes 17301504 | tf_op jit(solution)/shard_map/dot_general | solution.py:91
  325.6 10.7 %reshape.122 = bf16[128,48,512]{2,1,0:T(8,128)(2,1)} reshape(bf16[1536,2048]{1,0:T(8,128)(2,1)} %convolution_convert_fusion.1) | data formatting | bytes 12582912 | tf_op jit(solution)/shard_map/reshape | solution.py:102
  336.3 10.2 %all-to-all-start.1 = ((bf16[128,48,512]{2,1,0:T(8,128)(2,1)}), bf16[128,48,512]{2,1,0:T(8,128)(2,1)}, u32[]{:S(2)}, u32[]{:S(2)}) async-start(bf16[128,48,512]{2,1,0:T(8,128)(2,1)} %reshape.122), calls=%async_computation.1 | async-start | bytes 12582912 | tf_op jit(solution)/shard_map/all_to_all | solution.py:102
  346.5 10.8 %reshape.126 = bf16[1536,2048]{1,0:T(8,128)(2,1)} reshape(bf16[128,48,512]{2,1,0:T(8,128)(2,1)} %all-to-all-done.3) | data formatting | bytes 12582912 | tf_op jit(solution)/shard_map/reshape | solution.py:51
  357.3 9.4 %fusion.14 = bf16[1,2048,768]{1,2,0:T(8,128)(2,1)S(1)} fusion(bf16[1536,2048]{1,0:T(8,128)(2,1)} %reshape.121, bf16[1536,1536]{0,1:T(8,128)(2,1)} %copy-done), kind=kOutput, calls=%fused_computation.37 | convolution fusion | flops 4842848256 | bytes 14155776 | tf_op jit(solution)/shard_map/dot_general | solution.py:97
  366.7 11.4 %fusion = bf16[1,2048,1536]{1,2,0:T(8,128)(2,1)S(1)} fusion(bf16[1536,2048]{1,0:T(8,128)(2,1)S(1)} %copy-done.1, bf16[1536,768]{0,1:T(8,128)(2,1)S(1)} %get-tuple-element.22, bf16[1536,768]{0,1:T(8,128)(2,1)S(1)} %copy-done.3), kind=kOutput, calls=%fused_computation.6 | convolution fusion | flops 9676259328 | bytes 17301504 | tf_op jit(solution)/shard_map/dot_general | solution.py:94
  378.1 11.3 %pad_maximum_fusion = bf16[1,2048,2304]{1,2,0:T(8,128)(2,1)} fusion(bf16[1,2048,768]{1,2,0:T(8,128)(2,1)S(1)} %fusion.14, bf16[1,2048,1536]{1,2,0:T(8,128)(2,1)S(1)} %fusion), kind=kLoop, calls=%fused_computation | loop fusion | flops 18874368 | bytes 18874368 | tf_op jit(solution)/shard_map/concatenate | solution.py:100
  389.4 12.6 %copy.86 = bf16[1,2048,2304]{2,1,0:T(8,128)(2,1)} copy(bf16[1,2048,2304]{1,2,0:T(8,128)(2,1)} %pad_maximum_fusion) | data formatting | bytes 18874368
  403.5 20.8 %all-to-all-done.1 = bf16[128,48,512]{2,1,0:T(8,128)(2,1)} async-done(((bf16[128,48,512]{2,1,0:T(8,128)(2,1)}), bf16[128,48,512]{2,1,0:T(8,128)(2,1)}, u32[]{:S(2)}, u32[]{:S(2)}) %all-to-all-start.1) | async-done | bytes 6291488 | tf_op jit(solution)/shard_map/all_to_all | solution.py:102
  424.3 10.7 %reshape.123 = bf16[2,768,2048]{2,1,0:T(8,128)(2,1)} reshape(bf16[128,48,512]{2,1,0:T(8,128)(2,1)} %all-to-all-done.1) | data formatting | bytes 12582912 | tf_op jit(solution)/shard_map/reshape | solution.py:103
  435.0 8.6 %copy.81 = bf16[2,2048,768]{2,1,0:T(8,128)(2,1)} copy(bf16[2,2048,768]{1,2,0:T(8,128)(2,1)} %bitcast.33) | data formatting | bytes 12582912 | tf_op jit(solution)/shard_map/st,hsd->thd/dot_general | solution.py:104
  443.6 5.9 %convolution_convert_fusion.2 = bf16[128,4096]{1,0:T(8,128)(2,1)} fusion(pred[128,768]{1,0:T(8,128)(4,1)S(1)} %fusion.13, bf16[4096,768]{1,0:T(8,128)(2,1)} %bitcast.32), kind=kOutput, calls=%fused_computation.12 | convolution fusion | flops 805830656 | bytes 7438336 | tf_op jit(solution)/shard_map/st,hsd->thd/dot_general | solution.py:104
  (39 shorter events, 20.3 us)
Async XLA Ops:
  21.3 12.9 %copy-start.4 = (bf16[128,4096]{1,0:T(8,128)(2,1)S(1)}, bf16[128,4096]{1,0:T(8,128)(2,1)}, u32[]{:S(2)}) copy-start(bf16[128,4096]{1,0:T(8,128)(2,1)} %param.6) | copy-start | bytes 3145732
  21.3 90.0 %all-to-all-start = ((bf16[128,48,512]{2,1,0:T(8,128)(2,1)}), bf16[128,48,512]{2,1,0:T(8,128)(2,1)}, u32[]{:S(2)}, u32[]{:S(2)}) async-start(bf16[128,48,512]{2,1,0:T(8,128)(2,1)} %reshape.120), calls=%async_computation | async-start | bytes 12582912 | tf_op jit(solution)/shard_map/all_to_all | solution.py:48
  111.3 187.9 %all-to-all-start.3 = ((bf16[128,48,512]{2,1,0:T(8,128)(2,1)}), bf16[128,48,512]{2,1,0:T(8,128)(2,1)}, u32[]{:S(2)}, u32[]{:S(2)}) async-start(bf16[128,48,512]{2,1,0:T(8,128)(2,1)} %reshape.125), calls=%async_computation.3 | async-start | bytes 12582912 | tf_op jit(solution)/shard_map/all_to_all | solution.py:48
  124.8 117.4 %collective-permute-start.1 = (bf16[768,1536]{0,1:T(8,128)(2,1)S(1)}, bf16[768,1536]{0,1:T(8,128)(2,1)}, u32[]{:S(2)}, u32[]{:S(2)}) collective-permute-start(bf16[768,1536]{0,1:T(8,128)(2,1)S(1)} %bitcast.34), channel_id=1, source_target_pairs={{0,1},{1,0},{2,3},{3,2},{4,5},{5,4},{6,7},{7,6},{8,9},{9,8},{10,11... | collective-permute-start | bytes 7077896 | tf_op jit(solution)/shard_map/ppermute | solution.py:58
  147.0 145.7 %collective-permute-start = (bf16[1536,768]{0,1:T(8,128)(2,1)}, bf16[1536,768]{0,1:T(8,128)(2,1)}, u32[]{:S(2)}, u32[]{:S(2)}) collective-permute-start(bf16[1536,768]{0,1:T(8,128)(2,1)} %get-tuple-element.24), channel_id=1, source_target_pairs={{0,1},{1,0},{2,3},{3,2},{4,5},{5,4},{6,7},{7,6},{8,9},{9,8},{10,11... | collective-permute-start | bytes 7077896 | tf_op jit(solution)/shard_map/ppermute | solution.py:72
  147.0 145.7 %copy-start.2 = (f32[1536,768]{0,1:T(8,128)S(1)}, f32[1536,768]{0,1:T(8,128)}, u32[]{:S(2)}) copy-start(f32[1536,768]{0,1:T(8,128)} %get-tuple-element.25) | copy-start | bytes 14155780
  246.1 52.4 %copy-start = (bf16[1536,1536]{0,1:T(8,128)(2,1)}, bf16[1536,1536]{0,1:T(8,128)(2,1)S(1)}, u32[]{:S(2)}) copy-start(bf16[1536,1536]{0,1:T(8,128)(2,1)S(1)} %maximum_select_fusion) | copy-start | bytes 14155780
  299.2 37.2 %all-to-all-start.2 = ((f32[128,1,12]{2,1,0:T(1,128)}), f32[128,1,12]{2,1,0:T(1,128)S(1)}, u32[]{:S(2)}, u32[]{:S(2)}) async-start(f32[128,1,12]{2,1,0:T(1,128)} %bitcast.6), calls=%async_computation.2 | async-start | bytes 131072 | tf_op jit(solution)/shard_map/all_to_all | solution.py:107
  336.3 88.0 %all-to-all-start.1 = ((bf16[128,48,512]{2,1,0:T(8,128)(2,1)}), bf16[128,48,512]{2,1,0:T(8,128)(2,1)}, u32[]{:S(2)}, u32[]{:S(2)}) async-start(bf16[128,48,512]{2,1,0:T(8,128)(2,1)} %reshape.122), calls=%async_computation.1 | async-start | bytes 12582912 | tf_op jit(solution)/shard_map/all_to_all | solution.py:102
  357.3 9.4 %copy-start.1 = (bf16[1536,2048]{1,0:T(8,128)(2,1)S(1)}, bf16[1536,2048]{1,0:T(8,128)(2,1)}, u32[]{:S(2)}) copy-start(bf16[1536,2048]{1,0:T(8,128)(2,1)} %reshape.126) | copy-start | bytes 18874372
  357.3 9.4 %copy-start.3 = (bf16[1536,768]{0,1:T(8,128)(2,1)S(1)}, bf16[1536,768]{0,1:T(8,128)(2,1)}, u32[]{:S(2)}) copy-start(bf16[1536,768]{0,1:T(8,128)(2,1)} %get-tuple-element.23) | copy-start | bytes 7077892
  389.4 13.6 %copy-start.5 = (s32[128,8]{0,1:T(8,128)S(1)}, s32[128,8]{0,1:T(8,128)}, u32[]{:S(2)}) copy-start(s32[128,8]{0,1:T(8,128)} %param.8) | copy-start | bytes 12292
  389.4 13.6 %copy-start.6 = (bf16[128,8]{0,1:T(8,128)(2,1)S(1)}, bf16[128,8]{0,1:T(8,128)(2,1)}, u32[]{:S(2)}) copy-start(bf16[128,8]{0,1:T(8,128)(2,1)} %param.9) | copy-start | bytes 6148

commit v6 on v5

--- a/solution.py
+++ b/solution.py
@@ -35,23 +35,33 @@
     slot_index = jnp.where(in_window, flat_routes * capacity + position, -1)
     slot_ids = jnp.arange(experts * capacity, dtype=jnp.int32)
     route_hit = slot_index[:, None] == slot_ids[None, :]
-    token_hit = jnp.any(route_hit.reshape(tok_count, top_k, -1), axis=1)
-    select = token_hit.astype(bf16).T
     flat_probs = gate_probs.reshape(-1).astype(f32)
-    prob_select = jnp.sum(
-        jnp.where(route_hit, flat_probs[:, None], 0.0).reshape(tok_count, top_k, -1), axis=1
-    ).astype(bf16).T
+
+    blocks = half // lanes
+    wide_rows = experts * capacity * blocks
+    wide_slot = jnp.where(in_window, slot_index * blocks, -blocks).reshape(tok_count, 1, top_k)
+    wide_target = wide_slot + jnp.arange(blocks, dtype=jnp.int32).reshape(1, blocks, 1)
+    wide_ids = jnp.arange(wide_rows, dtype=jnp.int32)
+    wide_hit = wide_target.reshape(1, tok_count * blocks, top_k) == wide_ids.reshape(-1, 1, 1)
+    wide_select = jnp.any(wide_hit, axis=2).astype(bf16)
+    wide_probs = jnp.broadcast_to(
+        gate_probs.reshape(tok_count, 1, top_k), (tok_count, blocks, top_k)
+    ).reshape(1, tok_count * blocks, top_k)
+    wide_prob_select = jnp.sum(jnp.where(wide_hit, wide_probs, 0.0), axis=2).astype(bf16)
+    gather_hit = wide_target.transpose(1, 0, 2)[:, :, None, :] == wide_ids.reshape(1, 1, -1, 1)
+    gather_back = jnp.any(gather_hit, axis=3).astype(bf16)
 
     def dispatch(x, sel):
-        x3 = x.reshape(tok_count, n_dp, half)
-        sent = jnp.einsum("st,thd->hsd", sel, x3, preferred_element_type=f32).astype(bf16)
+        xb = x.reshape(tok_count, n_dp, blocks, lanes).transpose(1, 0, 2, 3)
+        xb = xb.reshape(n_dp, tok_count * blocks, lanes)
+        sent = jnp.einsum("qk,hkl->hql", sel, xb, preferred_element_type=f32).astype(bf16)
         got = lax.all_to_all(
             sent.reshape(devices, rows_per_chunk, lanes), WIRE, 0, 0, tiled=True
         )
         return got.reshape(slots_all, half)
 
-    recv_pgrads = dispatch(out_grad, prob_select)
-    recv_rows = dispatch(activations, select)
+    recv_pgrads = dispatch(out_grad, wide_prob_select)
+    recv_rows = dispatch(activations, wide_select)
 
     own_saved = saved_pre[0, 0]
     if n_dp == 2:
@@ -100,8 +110,8 @@
     weight_grad = jnp.concatenate([gate_up_term, down_term], axis=1).astype(bf16)[None]
 
     back = lax.all_to_all(row_grad.reshape(devices, rows_per_chunk, lanes), WIRE, 0, 0, tiled=True)
-    back = back.reshape(n_dp, experts * capacity, half)
-    input_grad = jnp.einsum("st,hsd->thd", select, back, preferred_element_type=f32)
+    back = back.reshape(n_dp, -1, lanes)
+    input_grad = jnp.einsum("ctk,hkl->thcl", gather_back, back, preferred_element_type=f32)
     input_grad = input_grad.reshape(tok_count, model_width).astype(bf16)
 
     back_probs = lax.all_to_all(scaled_slot_prob.reshape(devices, capacity), WIRE, 0, 0, tiled=True)

time: 454 us -> 536 us (1.18)
  other arithmetic: 25.3 us -> 205 us
  waiting for transfers between devices: 224 us -> 158 us
  local copies, waits for them, and re-layouts: 91.4 us -> 56.4 us
    reduce_or x1 -> x2, other arithmetic: 1.01 us -> 117 us  [the longest x1 61.5 us: body(): gather_back = jnp.any(gather_hit, axis=3).astype(bf16)]
    reduce_sum x1, other arithmetic: 1.01 us -> 64.2 us  [body(): jnp.sum(jnp.where(wide_hit, wide_probs, 0.0), axis=2).astype(bf16)]
    all_to_all x2, waiting for transfers between devices: 61.8 us -> 16.1 us  [dispatch(): lax.all_to_all(sent.reshape(devices, rows_per_chunk, lanes), WIRE, 0, 0,...]
    reshape x3 -> x4, local copies, waits for them, and re-layouts: 32.1 us -> 3.24 us  [the longest x2 2.66 us: dispatch(): xb = x.reshape(tok_count, n_dp, blocks, lanes).transpose(1, 0, 2, 3)]
    all_to_all x1, waiting for transfers between devices: 20.8 us -> 0.01 us  [body(): lax.all_to_all(row_grad.reshape(devices, rows_per_chunk, lanes), WIRE, 0,...]
    dot_general x1 -> x0, local copies, waits for them, and re-layouts: 8.64 us -> none  [body(): jnp.einsum('st,hsd->thd', select, back, preferred_element_type=f32)]
    unnamed x17 -> x21, local copies, waits for them, and re-layouts: 16.3 us -> 18.5 us
  transfers between devices with their start and end apart: 6 -> 6, of which waited for: 4 -> 3; matrix products, arithmetic and copies ran while one was open for 29% -> 45% of each run, Pallas kernels for 0% -> 0%
where the time goes in v6:
time: 536 us; the launch traced here: 527 us
  other arithmetic  205 us (38%)
  waiting for transfers between devices  158 us (29%)
  matrix products  61.6 us (11%)
  local copies, waits for them, and re-layouts  56.4 us (11%)
  starting transfers between devices  45.5 us (8%)
    ppermute x1, waiting for transfers between devices, body(): other_saved = lax.ppermute(own_saved, 'dp', [(0, 1), (1, 0)])  94.8 us
    reduce_sum x1, other arithmetic, body(): jnp.sum(jnp.where(wide_hit, wide_probs, 0.0), axis=2).astype(bf16)  64.2 us
    reduce_or x1, other arithmetic, body(): gather_back = jnp.any(gather_hit, axis=3).astype(bf16)  61.5 us
    reduce_or x1, other arithmetic, body(): wide_select = jnp.any(wide_hit, axis=2).astype(bf16)  56 us
    ppermute x1, waiting for transfers between devices, body(): lax.ppermute(partial_down.astype(bf16), 'dp', [(i, (i + 1) % n_dp) for i...  46.7 us
    all_to_all x2, starting transfers between devices, dispatch(): lax.all_to_all(sent.reshape(devices, rows_per_chunk, lanes), WIRE, 0, 0,...  21.7 us
    reshape x2, local copies, waits for them, and re-layouts, dispatch(): return got.reshape(slots_all, half)  21.4 us
    unnamed x21, local copies, waits for them, and re-layouts  18.5 us
  transfers between devices with their start and end apart: 6, of which 3 were waited for; matrix products, arithmetic and copies ran while one was open for 45% of the time, Pallas kernels for 0%

profile of v6, /device:TPU:1, one launch (start us, length us, event | category | flops | bytes accessed | tf_op | source)
XLA Modules:
  0.0 527.4 jit_solution(18220191442052375515)
XLA Ops:
  6.9 64.2 %fusion.3 = bf16[3072,512]{1,0:T(8,128)(2,1)S(1)} fusion(s32[512,8]{0,1:T(8,128)S(1)} %copy.77, bf16[512,8]{0,1:T(8,128)(2,1)S(1)} %copy.79), kind=kLoop, calls=%fused_computation.5 | loop fusion | flops 36175872 | bytes 3170304 | tf_op jit(solution)/shard_map/reduce_sum | solution.py:50
  71.1 5.3 %convolution_convert_fusion.2 = bf16[3072,2,512]{2,0,1:T(8,128)(2,1)} fusion(bf16[2,512,512]{2,1,0:T(8,128)(2,1)S(1)} %reshape.134, bf16[3072,512]{1,0:T(8,128)(2,1)S(1)} %fusion.3), kind=kOutput, calls=%fused_computation.20 | convolution fusion | flops 3224371200 | bytes 10485760 | tf_op jit(solution)/shard_map/qk,hkl->hql/dot_general | solution.py:57
  76.4 12.2 %all-to-all-start = ((bf16[128,48,512]{2,1,0:T(8,128)(2,1)}), bf16[128,48,512]{2,1,0:T(8,128)(2,1)}, u32[]{:S(2)}, u32[]{:S(2)}) async-start(bf16[128,48,512]{2,1,0:T(8,128)(2,1)} %bitcast.47), calls=%async_computation | async-start | bytes 12582912 | tf_op jit(solution)/shard_map/all_to_all | solution.py:58
  90.1 56.0 %fusion = pred[3072,512]{1,0:T(8,128)(4,1)S(1)} fusion(s32[512,8]{0,1:T(8,128)S(1)} %copy.77), kind=kLoop, calls=%fused_computation.2 | loop fusion | flops 23592960 | bytes 1589248 | tf_op jit(solution)/shard_map/reduce_or | solution.py:46
  146.2 5.3 fusion.10
  151.4 16.1 %all-to-all-done = bf16[128,48,512]{2,1,0:T(8,128)(2,1)} async-done(((bf16[128,48,512]{2,1,0:T(8,128)(2,1)}), bf16[128,48,512]{2,1,0:T(8,128)(2,1)}, u32[]{:S(2)}, u32[]{:S(2)}) %all-to-all-start) | async-done | bytes 6291488 | tf_op jit(solution)/shard_map/all_to_all | solution.py:58
  167.5 9.5 %all-to-all-start.3 = ((bf16[128,48,512]{2,1,0:T(8,128)(2,1)}), bf16[128,48,512]{2,1,0:T(8,128)(2,1)}, u32[]{:S(2)}, u32[]{:S(2)}) async-start(bf16[128,48,512]{2,1,0:T(8,128)(2,1)} %bitcast.46), calls=%async_computation.3 | async-start | bytes 12582912 | tf_op jit(solution)/shard_map/all_to_all | solution.py:58
  181.6 10.7 %reshape.136 = bf16[1536,2048]{1,0:T(8,128)(2,1)} reshape(bf16[128,48,512]{2,1,0:T(8,128)(2,1)} %all-to-all-done) | data formatting | bytes 12582912 | tf_op jit(solution)/shard_map/reshape | solution.py:61
  192.3 10.1 %fusion.33 = (bf16[1536,768]{0,1:T(8,128)(2,1)}, f32[1536,768]{0,1:T(8,128)}) fusion(bf16[1536,2048]{1,0:T(8,128)(2,1)} %reshape.136, bf16[2048,2304]{1,0:T(8,128)(2,1)} %bitcast.53), kind=kOutput, calls=%fused_computation.56 | convolution fusion | flops 4833017856 | bytes 16515072 | tf_op jit(solution)/shard_map/dot_general | solution.py:81
  202.5 94.8 %collective-permute-done.1 = bf16[768,1536]{0,1:T(8,128)(2,1)} collective-permute-done((bf16[768,1536]{0,1:T(8,128)(2,1)S(1)}, bf16[768,1536]{0,1:T(8,128)(2,1)}, u32[]{:S(2)}, u32[]{:S(2)}) %collective-permute-start.1) | collective-permute-done | bytes 2359328 | tf_op jit(solution)/shard_map/ppermute | solution.py:68
  297.3 3.8 maximum_select_fusion
  301.1 46.7 %collective-permute-done = bf16[1536,768]{0,1:T(8,128)(2,1)} collective-permute-done((bf16[1536,768]{0,1:T(8,128)(2,1)}, bf16[1536,768]{0,1:T(8,128)(2,1)}, u32[]{:S(2)}, u32[]{:S(2)}) %collective-permute-start) | collective-permute-done | bytes 2359328 | tf_op jit(solution)/shard_map/ppermute | solution.py:82
  347.8 5.6 %multiply_reduce_fusion = (f32[1536]{0:T(1024)S(1)}, bf16[1536,768]{0,1:T(8,128)(2,1)S(1)}, bf16[1536,768]{0,1:T(8,128)(2,1)}) fusion(f32[1536,768]{0,1:T(8,128)S(1)} %copy-done.2, bf16[1536,768]{0,1:T(8,128)(2,1)} %collective-permute-done, bf16[1536,1536]{0,1:T(8,128)(2,1)S(1)} %maximum_select_fusion), kind=kLoop, calls=%fused_computation.31 | loop fusion | flops 23591424 | bytes 16521216 | tf_op jit(solution)/shard_map/reduce_sum | solution.py:92
  354.2 11.8 %all-to-all-start.2 = ((f32[128,1,12]{2,1,0:T(1,128)}), f32[128,1,12]{2,1,0:T(1,128)S(1)}, u32[]{:S(2)}, u32[]{:S(2)}) async-start(f32[128,1,12]{2,1,0:T(1,128)} %bitcast.13), calls=%async_computation.2 | async-start | bytes 131072 | tf_op jit(solution)/shard_map/all_to_all | solution.py:117
  366.0 14.6 %convolution_convert_fusion.1 = bf16[1536,2048]{1,0:T(8,128)(2,1)} fusion(bf16[2048,2304]{1,0:T(8,128)(2,1)} %bitcast.54, bf16[1536,768]{0,1:T(8,128)(2,1)S(1)} %get-tuple-element.22, bf16[1536,768]{0,1:T(8,128)(2,1)} %get-tuple-element.23), kind=kOutput, calls=%fused_computation.8 | convolution fusion | flops 9676259328 | bytes 17301504 | tf_op jit(solution)/shard_map/dot_general | solution.py:101
  380.6 10.7 %reshape.137 = bf16[128,48,512]{2,1,0:T(8,128)(2,1)} reshape(bf16[1536,2048]{1,0:T(8,128)(2,1)} %convolution_convert_fusion.1) | data formatting | bytes 12582912 | tf_op jit(solution)/shard_map/reshape | solution.py:112
  391.3 10.2 %all-to-all-start.1 = ((bf16[128,48,512]{2,1,0:T(8,128)(2,1)}), bf16[128,48,512]{2,1,0:T(8,128)(2,1)}, u32[]{:S(2)}, u32[]{:S(2)}) async-start(bf16[128,48,512]{2,1,0:T(8,128)(2,1)} %reshape.137), calls=%async_computation.1 | async-start | bytes 12582912 | tf_op jit(solution)/shard_map/all_to_all | solution.py:112
  401.6 61.5 %fusion.2 = pred[4,128,3072]{2,1,0:T(8,128)(4,1)} fusion(s32[4,128,8]{2,1,0:T(8,128)S(1)} %iota_add_fusion), kind=kLoop, calls=%fused_computation.4 | loop fusion | flops 23592960 | bytes 1589248 | tf_op jit(solution)/shard_map/reduce_or | solution.py:52
  463.0 10.8 %reshape.142 = bf16[1536,2048]{1,0:T(8,128)(2,1)} reshape(bf16[128,48,512]{2,1,0:T(8,128)(2,1)} %all-to-all-done.3) | data formatting | bytes 12582912 | tf_op jit(solution)/shard_map/reshape | solution.py:61
  473.8 9.4 %fusion.25 = bf16[1,2048,768]{1,2,0:T(8,128)(2,1)S(1)} fusion(bf16[1536,2048]{1,0:T(8,128)(2,1)} %reshape.136, bf16[1536,1536]{0,1:T(8,128)(2,1)} %copy-done), kind=kOutput, calls=%fused_computation.44 | convolution fusion | flops 4842848256 | bytes 14155776 | tf_op jit(solution)/shard_map/dot_general | solution.py:107
  483.1 11.4 %fusion.4 = bf16[1,2048,1536]{1,2,0:T(8,128)(2,1)S(1)} fusion(bf16[1536,2048]{1,0:T(8,128)(2,1)S(1)} %copy-done.1, bf16[1536,768]{0,1:T(8,128)(2,1)S(1)} %get-tuple-element.22, bf16[1536,768]{0,1:T(8,128)(2,1)S(1)} %copy-done.3), kind=kOutput, calls=%fused_computation.12 | convolution fusion | flops 9676259328 | bytes 17301504 | tf_op jit(solution)/shard_map/dot_general | solution.py:104
  494.6 11.4 %pad_maximum_fusion = bf16[1,2048,2304]{1,2,0:T(8,128)(2,1)} fusion(bf16[1,2048,768]{1,2,0:T(8,128)(2,1)S(1)} %fusion.25, bf16[1,2048,1536]{1,2,0:T(8,128)(2,1)S(1)} %fusion.4), kind=kLoop, calls=%fused_computation.6 | loop fusion | flops 18874368 | bytes 18874368 | tf_op jit(solution)/shard_map/concatenate | solution.py:110
  506.0 12.7 %copy.88 = bf16[1,2048,2304]{2,1,0:T(8,128)(2,1)} copy(bf16[1,2048,2304]{1,2,0:T(8,128)(2,1)} %pad_maximum_fusion) | data formatting | bytes 18874368
  520.3 5.6 %fusion.28 = bf16[2,512,4,128]{3,1,2,0:T(8,128)(2,1)S(1)} fusion(bf16[2,3072,512,1]{2,1,3,0:T(8,128)(2,1)} %bitcast.22, pred[4,128,3072]{2,1,0:T(8,128)(4,1)S(1)} %copy-done.4), kind=kOutput, calls=%fused_computation.46 | convolution fusion | flops 3221749760 | bytes 8912896 | tf_op jit(solution)/shard_map/ctk,hkl->thcl/dot_general | solution.py:114
  (53 shorter events, 15.9 us)
Async XLA Ops:
  76.4 12.3 %copy-start.5 = (bf16[128,4096]{1,0:T(8,128)(2,1)S(1)}, bf16[128,4096]{1,0:T(8,128)(2,1)}, u32[]{:S(2)}) copy-start(bf16[128,4096]{1,0:T(8,128)(2,1)} %param.6) | copy-start | bytes 3145732
  76.4 91.2 %all-to-all-start = ((bf16[128,48,512]{2,1,0:T(8,128)(2,1)}), bf16[128,48,512]{2,1,0:T(8,128)(2,1)}, u32[]{:S(2)}, u32[]{:S(2)}) async-start(bf16[128,48,512]{2,1,0:T(8,128)(2,1)} %bitcast.47), calls=%async_computation | async-start | bytes 12582912 | tf_op jit(solution)/shard_map/all_to_all | solution.py:58
  167.5 186.6 %all-to-all-start.3 = ((bf16[128,48,512]{2,1,0:T(8,128)(2,1)}), bf16[128,48,512]{2,1,0:T(8,128)(2,1)}, u32[]{:S(2)}, u32[]{:S(2)}) async-start(bf16[128,48,512]{2,1,0:T(8,128)(2,1)} %bitcast.46), calls=%async_computation.3 | async-start | bytes 12582912 | tf_op jit(solution)/shard_map/all_to_all | solution.py:58
  179.9 117.4 %collective-permute-start.1 = (bf16[768,1536]{0,1:T(8,128)(2,1)S(1)}, bf16[768,1536]{0,1:T(8,128)(2,1)}, u32[]{:S(2)}, u32[]{:S(2)}) collective-permute-start(bf16[768,1536]{0,1:T(8,128)(2,1)S(1)} %bitcast.44), channel_id=1, source_target_pairs={{0,1},{1,0},{2,3},{3,2},{4,5},{5,4},{6,7},{7,6},{8,9},{9,8},{10,11... | collective-permute-start | bytes 7077896 | tf_op jit(solution)/shard_map/ppermute | solution.py:68
  202.4 145.4 %collective-permute-start = (bf16[1536,768]{0,1:T(8,128)(2,1)}, bf16[1536,768]{0,1:T(8,128)(2,1)}, u32[]{:S(2)}, u32[]{:S(2)}) collective-permute-start(bf16[1536,768]{0,1:T(8,128)(2,1)} %get-tuple-element.24), channel_id=1, source_target_pairs={{0,1},{1,0},{2,3},{3,2},{4,5},{5,4},{6,7},{7,6},{8,9},{9,8},{10,11... | collective-permute-start | bytes 7077896 | tf_op jit(solution)/shard_map/ppermute | solution.py:82
  202.4 145.4 %copy-start.2 = (f32[1536,768]{0,1:T(8,128)S(1)}, f32[1536,768]{0,1:T(8,128)}, u32[]{:S(2)}) copy-start(f32[1536,768]{0,1:T(8,128)} %get-tuple-element.25) | copy-start | bytes 14155780
  301.1 52.4 %copy-start = (bf16[1536,1536]{0,1:T(8,128)(2,1)}, bf16[1536,1536]{0,1:T(8,128)(2,1)S(1)}, u32[]{:S(2)}) copy-start(bf16[1536,1536]{0,1:T(8,128)(2,1)S(1)} %maximum_select_fusion) | copy-start | bytes 14155780
  354.2 37.2 %all-to-all-start.2 = ((f32[128,1,12]{2,1,0:T(1,128)}), f32[128,1,12]{2,1,0:T(1,128)S(1)}, u32[]{:S(2)}, u32[]{:S(2)}) async-start(f32[128,1,12]{2,1,0:T(1,128)} %bitcast.13), calls=%async_computation.2 | async-start | bytes 131072 | tf_op jit(solution)/shard_map/all_to_all | solution.py:117
  391.3 129.0 %all-to-all-start.1 = ((bf16[128,48,512]{2,1,0:T(8,128)(2,1)}), bf16[128,48,512]{2,1,0:T(8,128)(2,1)}, u32[]{:S(2)}, u32[]{:S(2)}) async-start(bf16[128,48,512]{2,1,0:T(8,128)(2,1)} %reshape.137), calls=%async_computation.1 | async-start | bytes 12582912 | tf_op jit(solution)/shard_map/all_to_all | solution.py:112
  473.8 9.4 %copy-start.1 = (bf16[1536,2048]{1,0:T(8,128)(2,1)S(1)}, bf16[1536,2048]{1,0:T(8,128)(2,1)}, u32[]{:S(2)}) copy-start(bf16[1536,2048]{1,0:T(8,128)(2,1)} %reshape.142) | copy-start | bytes 18874372
  473.8 9.4 %copy-start.3 = (bf16[1536,768]{0,1:T(8,128)(2,1)S(1)}, bf16[1536,768]{0,1:T(8,128)(2,1)}, u32[]{:S(2)}) copy-start(bf16[1536,768]{0,1:T(8,128)(2,1)} %get-tuple-element.23) | copy-start | bytes 7077892
  506.0 13.6 %copy-start.6 = (s32[128,8]{0,1:T(8,128)S(1)}, s32[128,8]{0,1:T(8,128)}, u32[]{:S(2)}) copy-start(s32[128,8]{0,1:T(8,128)} %param.8) | copy-start | bytes 12292
  506.0 13.7 %copy-start.7 = (bf16[128,8]{0,1:T(8,128)(2,1)S(1)}, bf16[128,8]{0,1:T(8,128)(2,1)}, u32[]{:S(2)}) copy-start(bf16[128,8]{0,1:T(8,128)(2,1)} %param.9) | copy-start | bytes 6148
  506.0 14.3 %copy-start.4 = (pred[4,128,3072]{2,1,0:T(8,128)(4,1)S(1)}, pred[4,128,3072]{2,1,0:T(8,128)(4,1)}, u32[]{:S(2)}) copy-start(pred[4,128,3072]{2,1,0:T(8,128)(4,1)} %fusion.2) | copy-start | bytes 4718596

commit v7 on v6

--- a/solution.py
+++ b/solution.py
@@ -39,17 +39,19 @@
 
     blocks = half // lanes
     wide_rows = experts * capacity * blocks
-    wide_slot = jnp.where(in_window, slot_index * blocks, -blocks).reshape(tok_count, 1, top_k)
-    wide_target = wide_slot + jnp.arange(blocks, dtype=jnp.int32).reshape(1, blocks, 1)
-    wide_ids = jnp.arange(wide_rows, dtype=jnp.int32)
-    wide_hit = wide_target.reshape(1, tok_count * blocks, top_k) == wide_ids.reshape(-1, 1, 1)
-    wide_select = jnp.any(wide_hit, axis=2).astype(bf16)
-    wide_probs = jnp.broadcast_to(
-        gate_probs.reshape(tok_count, 1, top_k), (tok_count, blocks, top_k)
-    ).reshape(1, tok_count * blocks, top_k)
-    wide_prob_select = jnp.sum(jnp.where(wide_hit, wide_probs, 0.0), axis=2).astype(bf16)
-    gather_hit = wide_target.transpose(1, 0, 2)[:, :, None, :] == wide_ids.reshape(1, 1, -1, 1)
-    gather_back = jnp.any(gather_hit, axis=3).astype(bf16)
+    route_token = (idx // top_k).reshape(-1, 1)
+    slot_filled = jnp.any(route_hit, axis=0)
+    slot_token = jnp.where(slot_filled, jnp.sum(jnp.where(route_hit, route_token, 0), axis=0), -1)
+    slot_prob = jnp.sum(jnp.where(route_hit, flat_probs[:, None], 0.0), axis=0)
+    block_ids = jnp.arange(blocks, dtype=jnp.int32)
+    row_key = (slot_token[:, None] * blocks + block_ids[None, :]).reshape(wide_rows)
+    row_prob = jnp.broadcast_to(slot_prob[:, None], (experts * capacity, blocks)).reshape(wide_rows)
+    col_ids = jnp.arange(tok_count * blocks, dtype=jnp.int32)
+    wide_hit = row_key[:, None] == col_ids[None, :]
+    wide_select = wide_hit.astype(bf16)
+    wide_prob_select = jnp.where(wide_hit, row_prob[:, None], 0.0).astype(bf16)
+    gather_key = col_ids.reshape(tok_count, blocks).T.reshape(blocks, tok_count, 1)
+    gather_back = (gather_key == row_key.reshape(1, 1, -1)).astype(bf16)
 
     def dispatch(x, sel):
         xb = x.reshape(tok_count, n_dp, blocks, lanes).transpose(1, 0, 2, 3)

time: 536 us -> 428 us (0.80)
  other arithmetic: 205 us -> 24.1 us
  waiting for transfers between devices: 158 us -> 234 us
    reduce_or x2 -> x1, other arithmetic: 117 us -> 0.49 us  [body(): slot_filled = jnp.any(route_hit, axis=0)]
    reduce_sum x1 -> x2, other arithmetic: 64.2 us -> 1.04 us  [the longest x1 0.65 us: body(): jnp.sum(jnp.where(route_hit, route_token, 0), axis=0)]
    all_to_all x2, waiting for transfers between devices: 16.1 us -> 70.9 us  [dispatch(): lax.all_to_all(sent.reshape(devices, rows_per_chunk, lanes), WIRE, 0, 0,...]
    all_to_all x1, waiting for transfers between devices: 0.01 us -> 21.1 us  [body(): lax.all_to_all(row_grad.reshape(devices, rows_per_chunk, lanes), WIRE, 0,...]
    unnamed x21 -> x18, local copies, waits for them, and re-layouts: 18.5 us -> 17.6 us
  transfers between devices with their start and end apart: 6 -> 6, of which waited for: 3 -> 4; matrix products, arithmetic and copies ran while one was open for 45% -> 29% of each run, Pallas kernels for 0% -> 0%
where the time goes in v7:
time: 428 us; the launch traced here: 425 us
  waiting for transfers between devices  234 us (55%)
  matrix products  63.3 us (15%)
  local copies, waits for them, and re-layouts  56.4 us (13%)
  starting transfers between devices  46.2 us (11%)
  other arithmetic  24.1 us (6%)
    ppermute x1, waiting for transfers between devices, body(): other_saved = lax.ppermute(own_saved, 'dp', [(0, 1), (1, 0)])  94.9 us
    all_to_all x2, waiting for transfers between devices, dispatch(): lax.all_to_all(sent.reshape(devices, rows_per_chunk, lanes), WIRE, 0, 0,...  70.9 us
    ppermute x1, waiting for transfers between devices, body(): lax.ppermute(partial_down.astype(bf16), 'dp', [(i, (i + 1) % n_dp) for i...  46.7 us
    all_to_all x2, starting transfers between devices, dispatch(): lax.all_to_all(sent.reshape(devices, rows_per_chunk, lanes), WIRE, 0, 0,...  22.5 us
    reshape x2, local copies, waits for them, and re-layouts, dispatch(): return got.reshape(slots_all, half)  21.4 us
    all_to_all x1, waiting for transfers between devices, body(): lax.all_to_all(row_grad.reshape(devices, rows_per_chunk, lanes), WIRE, 0,...  21.1 us
    unnamed x18, local copies, waits for them, and re-layouts  17.6 us
    dot_general x1, matrix products, body(): lax.dot_general(gate_up_grad, gate_up_part, (((1,), (1,)), ((), ())), pre...  14.6 us
  transfers between devices with their start and end apart: 6, of which 4 were waited for; matrix products, arithmetic and copies ran while one was open for 29% of the time, Pallas kernels for 0%

profile of v7, /device:TPU:1, one launch (start us, length us, event | category | flops | bytes accessed | tf_op | source)
XLA Modules:
  0.0 424.5 jit_solution(994509560431572120)
XLA Ops:
  5.3 1.8 reshape.173
  7.8 6.3 %convolution_convert_fusion.2 = bf16[3072,2,512]{2,0,1:T(8,128)(2,1)} fusion(bf16[2,512,512]{2,1,0:T(8,128)(2,1)S(1)} %reshape.174, bf16[3072]{0:T(1024)(128)(2,1)S(1)} %broadcast_in_dim.84, s32[3072]{0:T(1024)S(1)} %add.55), kind=kOutput, calls=%fused_computation.17 | convolution fusion | flops 3227516928 | bytes 7358464 | tf_op jit(solution)/shard_map/qk,hkl->hql/dot_general | solution.py:59
  14.1 11.9 %all-to-all-start = ((bf16[128,48,512]{2,1,0:T(8,128)(2,1)}), bf16[128,48,512]{2,1,0:T(8,128)(2,1)}, u32[]{:S(2)}, u32[]{:S(2)}) async-start(bf16[128,48,512]{2,1,0:T(8,128)(2,1)} %bitcast.45), calls=%async_computation | async-start | bytes 12582912 | tf_op jit(solution)/shard_map/all_to_all | solution.py:60
  27.5 5.8 %fusion.8 = bf16[3072,2,512]{2,0,1:T(8,128)(2,1)} fusion(bf16[2,512,512]{2,1,0:T(8,128)(2,1)S(1)} %reshape.183, s32[3072]{0:T(1024)S(1)} %add.55), kind=kOutput, calls=%fused_computation.18 | convolution fusion | flops 3225944064 | bytes 7352320 | tf_op jit(solution)/shard_map/qk,hkl->hql/dot_general | solution.py:59
  33.2 70.9 %all-to-all-done = bf16[128,48,512]{2,1,0:T(8,128)(2,1)} async-done(((bf16[128,48,512]{2,1,0:T(8,128)(2,1)}), bf16[128,48,512]{2,1,0:T(8,128)(2,1)}, u32[]{:S(2)}, u32[]{:S(2)}) %all-to-all-start) | async-done | bytes 6291488 | tf_op jit(solution)/shard_map/all_to_all | solution.py:60
  104.1 10.6 %all-to-all-start.3 = ((bf16[128,48,512]{2,1,0:T(8,128)(2,1)}), bf16[128,48,512]{2,1,0:T(8,128)(2,1)}, u32[]{:S(2)}, u32[]{:S(2)}) async-start(bf16[128,48,512]{2,1,0:T(8,128)(2,1)} %bitcast.44), calls=%async_computation.3 | async-start | bytes 12582912 | tf_op jit(solution)/shard_map/all_to_all | solution.py:60
  114.7 2.8 copy.52
  119.3 10.7 %reshape.176 = bf16[1536,2048]{1,0:T(8,128)(2,1)} reshape(bf16[128,48,512]{2,1,0:T(8,128)(2,1)} %all-to-all-done) | data formatting | bytes 12582912 | tf_op jit(solution)/shard_map/reshape | solution.py:63
  130.0 10.1 %fusion.43 = (bf16[1536,768]{0,1:T(8,128)(2,1)}, f32[1536,768]{0,1:T(8,128)}) fusion(bf16[1536,2048]{1,0:T(8,128)(2,1)} %reshape.176, bf16[2048,2304]{1,0:T(8,128)(2,1)} %bitcast.49), kind=kOutput, calls=%fused_computation.69 | convolution fusion | flops 4833017856 | bytes 16515072 | tf_op jit(solution)/shard_map/dot_general | solution.py:83
  140.2 94.9 %collective-permute-done.1 = bf16[768,1536]{0,1:T(8,128)(2,1)} collective-permute-done((bf16[768,1536]{0,1:T(8,128)(2,1)S(1)}, bf16[768,1536]{0,1:T(8,128)(2,1)}, u32[]{:S(2)}, u32[]{:S(2)}) %collective-permute-start.1) | collective-permute-done | bytes 2359328 | tf_op jit(solution)/shard_map/ppermute | solution.py:70
  235.0 3.8 maximum_select_fusion
  238.8 46.7 %collective-permute-done = bf16[1536,768]{0,1:T(8,128)(2,1)} collective-permute-done((bf16[1536,768]{0,1:T(8,128)(2,1)}, bf16[1536,768]{0,1:T(8,128)(2,1)}, u32[]{:S(2)}, u32[]{:S(2)}) %collective-permute-start) | collective-permute-done | bytes 2359328 | tf_op jit(solution)/shard_map/ppermute | solution.py:84
  285.6 5.6 %multiply_reduce_fusion = (f32[1536]{0:T(1024)S(1)}, bf16[1536,768]{0,1:T(8,128)(2,1)S(1)}, bf16[1536,768]{0,1:T(8,128)(2,1)}) fusion(f32[1536,768]{0,1:T(8,128)S(1)} %copy-done.2, bf16[1536,768]{0,1:T(8,128)(2,1)} %collective-permute-done, bf16[1536,1536]{0,1:T(8,128)(2,1)S(1)} %maximum_select_fusion), kind=kLoop, calls=%fused_computation.28 | loop fusion | flops 23591424 | bytes 16521216 | tf_op jit(solution)/shard_map/reduce_sum | solution.py:94
  291.9 11.8 %all-to-all-start.2 = ((f32[128,1,12]{2,1,0:T(1,128)}), f32[128,1,12]{2,1,0:T(1,128)S(1)}, u32[]{:S(2)}, u32[]{:S(2)}) async-start(f32[128,1,12]{2,1,0:T(1,128)} %bitcast.11), calls=%async_computation.2 | async-start | bytes 131072 | tf_op jit(solution)/shard_map/all_to_all | solution.py:119
  303.7 14.6 %convolution_convert_fusion.1 = bf16[1536,2048]{1,0:T(8,128)(2,1)} fusion(bf16[2048,2304]{1,0:T(8,128)(2,1)} %bitcast.50, bf16[1536,768]{0,1:T(8,128)(2,1)S(1)} %get-tuple-element.19, bf16[1536,768]{0,1:T(8,128)(2,1)} %get-tuple-element.20), kind=kOutput, calls=%fused_computation.2 | convolution fusion | flops 9676259328 | bytes 17301504 | tf_op jit(solution)/shard_map/dot_general | solution.py:103
  318.4 10.7 %reshape.177 = bf16[128,48,512]{2,1,0:T(8,128)(2,1)} reshape(bf16[1536,2048]{1,0:T(8,128)(2,1)} %convolution_convert_fusion.1) | data formatting | bytes 12582912 | tf_op jit(solution)/shard_map/reshape | solution.py:114
  329.1 10.2 %all-to-all-start.1 = ((bf16[128,48,512]{2,1,0:T(8,128)(2,1)}), bf16[128,48,512]{2,1,0:T(8,128)(2,1)}, u32[]{:S(2)}, u32[]{:S(2)}) async-start(bf16[128,48,512]{2,1,0:T(8,128)(2,1)} %reshape.177), calls=%async_computation.1 | async-start | bytes 12582912 | tf_op jit(solution)/shard_map/all_to_all | solution.py:114
  339.3 10.8 %reshape.185 = bf16[1536,2048]{1,0:T(8,128)(2,1)} reshape(bf16[128,48,512]{2,1,0:T(8,128)(2,1)} %all-to-all-done.3) | data formatting | bytes 12582912 | tf_op jit(solution)/shard_map/reshape | solution.py:63
  350.1 9.3 %fusion.31 = bf16[1,2048,768]{1,2,0:T(8,128)(2,1)S(1)} fusion(bf16[1536,2048]{1,0:T(8,128)(2,1)} %reshape.176, bf16[1536,1536]{0,1:T(8,128)(2,1)} %copy-done), kind=kOutput, calls=%fused_computation.50 | convolution fusion | flops 4842848256 | bytes 14155776 | tf_op jit(solution)/shard_map/dot_general | solution.py:109
  359.4 11.4 %fusion = bf16[1,2048,1536]{1,2,0:T(8,128)(2,1)S(1)} fusion(bf16[1536,2048]{1,0:T(8,128)(2,1)S(1)} %copy-done.1, bf16[1536,768]{0,1:T(8,128)(2,1)S(1)} %get-tuple-element.19, bf16[1536,768]{0,1:T(8,128)(2,1)S(1)} %copy-done.3), kind=kOutput, calls=%fused_computation.6 | convolution fusion | flops 9676259328 | bytes 17301504 | tf_op jit(solution)/shard_map/dot_general | solution.py:106
  370.8 11.3 %pad_maximum_fusion = bf16[1,2048,2304]{1,2,0:T(8,128)(2,1)} fusion(bf16[1,2048,768]{1,2,0:T(8,128)(2,1)S(1)} %fusion.31, bf16[1,2048,1536]{1,2,0:T(8,128)(2,1)S(1)} %fusion), kind=kLoop, calls=%fused_computation | loop fusion | flops 18874368 | bytes 18874368 | tf_op jit(solution)/shard_map/concatenate | solution.py:112
  382.1 12.6 %copy.58 = bf16[1,2048,2304]{2,1,0:T(8,128)(2,1)} copy(bf16[1,2048,2304]{1,2,0:T(8,128)(2,1)} %pad_maximum_fusion) | data formatting | bytes 18874368
  396.3 21.1 %all-to-all-done.1 = bf16[128,48,512]{2,1,0:T(8,128)(2,1)} async-done(((bf16[128,48,512]{2,1,0:T(8,128)(2,1)}), bf16[128,48,512]{2,1,0:T(8,128)(2,1)}, u32[]{:S(2)}, u32[]{:S(2)}) %all-to-all-start.1) | async-done | bytes 6291488 | tf_op jit(solution)/shard_map/all_to_all | solution.py:114
  417.4 5.8 %fusion.34 = bf16[2,512,4,128]{3,1,2,0:T(8,128)(2,1)S(1)} fusion(bf16[2,3072,512,1]{2,1,3,0:T(8,128)(2,1)} %bitcast.20, s32[3072]{0:T(1024)S(1)} %add.55, s32[4,128]{1,0:T(4,128)S(1)} %multiply_add_fusion), kind=kOutput, calls=%fused_computation.52 | convolution fusion | flops 3223322624 | bytes 7354368 | tf_op jit(solution)/shard_map/ctk,hkl->thcl/dot_general | solution.py:116
  (46 shorter events, 12.1 us)
Async XLA Ops:
  14.1 11.9 %copy-start.4 = (bf16[128,4096]{1,0:T(8,128)(2,1)S(1)}, bf16[128,4096]{1,0:T(8,128)(2,1)}, u32[]{:S(2)}) copy-start(bf16[128,4096]{1,0:T(8,128)(2,1)} %param.6) | copy-start | bytes 3145732
  14.1 90.0 %all-to-all-start = ((bf16[128,48,512]{2,1,0:T(8,128)(2,1)}), bf16[128,48,512]{2,1,0:T(8,128)(2,1)}, u32[]{:S(2)}, u32[]{:S(2)}) async-start(bf16[128,48,512]{2,1,0:T(8,128)(2,1)} %bitcast.45), calls=%async_computation | async-start | bytes 12582912 | tf_op jit(solution)/shard_map/all_to_all | solution.py:60
  104.1 187.8 %all-to-all-start.3 = ((bf16[128,48,512]{2,1,0:T(8,128)(2,1)}), bf16[128,48,512]{2,1,0:T(8,128)(2,1)}, u32[]{:S(2)}, u32[]{:S(2)}) async-start(bf16[128,48,512]{2,1,0:T(8,128)(2,1)} %bitcast.44), calls=%async_computation.3 | async-start | bytes 12582912 | tf_op jit(solution)/shard_map/all_to_all | solution.py:60
  117.6 117.4 %collective-permute-start.1 = (bf16[768,1536]{0,1:T(8,128)(2,1)S(1)}, bf16[768,1536]{0,1:T(8,128)(2,1)}, u32[]{:S(2)}, u32[]{:S(2)}) collective-permute-start(bf16[768,1536]{0,1:T(8,128)(2,1)S(1)} %bitcast.42), channel_id=1, source_target_pairs={{0,1},{1,0},{2,3},{3,2},{4,5},{5,4},{6,7},{7,6},{8,9},{9,8},{10,11... | collective-permute-start | bytes 7077896 | tf_op jit(solution)/shard_map/ppermute | solution.py:70
  140.1 145.4 %collective-permute-start = (bf16[1536,768]{0,1:T(8,128)(2,1)}, bf16[1536,768]{0,1:T(8,128)(2,1)}, u32[]{:S(2)}, u32[]{:S(2)}) collective-permute-start(bf16[1536,768]{0,1:T(8,128)(2,1)} %get-tuple-element.21), channel_id=1, source_target_pairs={{0,1},{1,0},{2,3},{3,2},{4,5},{5,4},{6,7},{7,6},{8,9},{9,8},{10,11... | collective-permute-start | bytes 7077896 | tf_op jit(solution)/shard_map/ppermute | solution.py:84
  140.1 145.4 %copy-start.2 = (f32[1536,768]{0,1:T(8,128)S(1)}, f32[1536,768]{0,1:T(8,128)}, u32[]{:S(2)}) copy-start(f32[1536,768]{0,1:T(8,128)} %get-tuple-element.22) | copy-start | bytes 14155780
  238.8 52.4 %copy-start = (bf16[1536,1536]{0,1:T(8,128)(2,1)}, bf16[1536,1536]{0,1:T(8,128)(2,1)S(1)}, u32[]{:S(2)}) copy-start(bf16[1536,1536]{0,1:T(8,128)(2,1)S(1)} %maximum_select_fusion) | copy-start | bytes 14155780
  291.9 37.2 %all-to-all-start.2 = ((f32[128,1,12]{2,1,0:T(1,128)}), f32[128,1,12]{2,1,0:T(1,128)S(1)}, u32[]{:S(2)}, u32[]{:S(2)}) async-start(f32[128,1,12]{2,1,0:T(1,128)} %bitcast.11), calls=%async_computation.2 | async-start | bytes 131072 | tf_op jit(solution)/shard_map/all_to_all | solution.py:119
  329.1 88.3 %all-to-all-start.1 = ((bf16[128,48,512]{2,1,0:T(8,128)(2,1)}), bf16[128,48,512]{2,1,0:T(8,128)(2,1)}, u32[]{:S(2)}, u32[]{:S(2)}) async-start(bf16[128,48,512]{2,1,0:T(8,128)(2,1)} %reshape.177), calls=%async_computation.1 | async-start | bytes 12582912 | tf_op jit(solution)/shard_map/all_to_all | solution.py:114
  350.1 9.4 %copy-start.1 = (bf16[1536,2048]{1,0:T(8,128)(2,1)S(1)}, bf16[1536,2048]{1,0:T(8,128)(2,1)}, u32[]{:S(2)}) copy-start(bf16[1536,2048]{1,0:T(8,128)(2,1)} %reshape.185) | copy-start | bytes 18874372
  350.1 9.4 %copy-start.3 = (bf16[1536,768]{0,1:T(8,128)(2,1)S(1)}, bf16[1536,768]{0,1:T(8,128)(2,1)}, u32[]{:S(2)}) copy-start(bf16[1536,768]{0,1:T(8,128)(2,1)} %get-tuple-element.20) | copy-start | bytes 7077892
  382.1 13.6 %copy-start.5 = (s32[128,8]{0,1:T(8,128)S(1)}, s32[128,8]{0,1:T(8,128)}, u32[]{:S(2)}) copy-start(s32[128,8]{0,1:T(8,128)} %param.8) | copy-start | bytes 12292
  382.1 13.6 %copy-start.6 = (bf16[128,8]{0,1:T(8,128)(2,1)S(1)}, bf16[128,8]{0,1:T(8,128)(2,1)}, u32[]{:S(2)}) copy-start(bf16[128,8]{0,1:T(8,128)(2,1)} %param.9) | copy-start | bytes 6148

commit v8 on v7

--- a/solution.py
+++ b/solution.py
@@ -44,18 +44,20 @@
     slot_token = jnp.where(slot_filled, jnp.sum(jnp.where(route_hit, route_token, 0), axis=0), -1)
     slot_prob = jnp.sum(jnp.where(route_hit, flat_probs[:, None], 0.0), axis=0)
     block_ids = jnp.arange(blocks, dtype=jnp.int32)
-    row_key = (slot_token[:, None] * blocks + block_ids[None, :]).reshape(wide_rows)
+    row_key = jnp.where(
+        slot_filled[:, None], block_ids[None, :] * tok_count + slot_token[:, None], -1
+    ).reshape(wide_rows)
     row_prob = jnp.broadcast_to(slot_prob[:, None], (experts * capacity, blocks)).reshape(wide_rows)
     col_ids = jnp.arange(tok_count * blocks, dtype=jnp.int32)
     wide_hit = row_key[:, None] == col_ids[None, :]
     wide_select = wide_hit.astype(bf16)
     wide_prob_select = jnp.where(wide_hit, row_prob[:, None], 0.0).astype(bf16)
-    gather_key = col_ids.reshape(tok_count, blocks).T.reshape(blocks, tok_count, 1)
+    gather_key = col_ids.reshape(blocks, tok_count, 1)
     gather_back = (gather_key == row_key.reshape(1, 1, -1)).astype(bf16)
 
     def dispatch(x, sel):
-        xb = x.reshape(tok_count, n_dp, blocks, lanes).transpose(1, 0, 2, 3)
-        xb = xb.reshape(n_dp, tok_count * blocks, lanes)
+        xb = x.reshape(tok_count, n_dp * blocks, lanes).transpose(1, 0, 2)
+        xb = xb.reshape(n_dp, blocks * tok_count, lanes)
         sent = jnp.einsum("qk,hkl->hql", sel, xb, preferred_element_type=f32).astype(bf16)
         got = lax.all_to_all(
             sent.reshape(devices, rows_per_chunk, lanes), WIRE, 0, 0, tiled=True

time: 428 us -> 427 us (level)
    unnamed x18 -> x20, local copies, waits for them, and re-layouts: 17.6 us -> 19.6 us
where the time goes in v8:
time: 427 us; the launch traced here: 424 us
  waiting for transfers between devices  234 us (55%)
  matrix products  63.3 us (15%)
  local copies, waits for them, and re-layouts  55.1 us (13%)
  starting transfers between devices  46.2 us (11%)
  other arithmetic  24.2 us (6%)
    ppermute x1, waiting for transfers between devices, body(): other_saved = lax.ppermute(own_saved, 'dp', [(0, 1), (1, 0)])  94.9 us
    all_to_all x2, waiting for transfers between devices, dispatch(): lax.all_to_all(sent.reshape(devices, rows_per_chunk, lanes), WIRE, 0, 0,...  71.6 us
    ppermute x1, waiting for transfers between devices, body(): lax.ppermute(partial_down.astype(bf16), 'dp', [(i, (i + 1) % n_dp) for i...  46.7 us
    all_to_all x2, starting transfers between devices, dispatch(): lax.all_to_all(sent.reshape(devices, rows_per_chunk, lanes), WIRE, 0, 0,...  22.5 us
    reshape x2, local copies, waits for them, and re-layouts, dispatch(): return got.reshape(slots_all, half)  21.4 us
    all_to_all x1, waiting for transfers between devices, body(): lax.all_to_all(row_grad.reshape(devices, rows_per_chunk, lanes), WIRE, 0,...  21.1 us
    unnamed x20, local copies, waits for them, and re-layouts  19.6 us
    dot_general x1, matrix products, body(): lax.dot_general(gate_up_grad, gate_up_part, (((1,), (1,)), ((), ())), pre...  14.6 us
  transfers between devices with their start and end apart: 6, of which 4 were waited for; matrix products, arithmetic and copies ran while one was open for 29% of the time, Pallas kernels for 0%

profile of v8, /device:TPU:1, one launch (start us, length us, event | category | flops | bytes accessed | tf_op | source)
XLA Modules:
  0.0 424.0 jit_solution(17709948950289454520)
XLA Ops:
  7.3 6.3 %convolution_convert_fusion.2 = bf16[3072,2,512]{2,0,1:T(8,128)(2,1)} fusion(bf16[2,512,512]{2,1,0:T(8,128)(2,1)S(1)} %bitcast.59, bf16[3072]{0:T(1024)(128)(2,1)S(1)} %broadcast_in_dim.99, s32[3072]{0:T(1024)S(1)} %select_n.74), kind=kOutput, calls=%fused_computation.17 | convolution fusion | flops 3227516928 | bytes 7358464 | tf_op jit(solution)/shard_map/qk,hkl->hql/dot_general | solution.py:61
  13.6 11.9 %all-to-all-start = ((bf16[128,48,512]{2,1,0:T(8,128)(2,1)}), bf16[128,48,512]{2,1,0:T(8,128)(2,1)}, u32[]{:S(2)}, u32[]{:S(2)}) async-start(bf16[128,48,512]{2,1,0:T(8,128)(2,1)} %bitcast.53), calls=%async_computation | async-start | bytes 12582912 | tf_op jit(solution)/shard_map/all_to_all | solution.py:62
  26.2 5.8 %fusion.8 = bf16[3072,2,512]{2,0,1:T(8,128)(2,1)} fusion(bf16[2,512,512]{2,1,0:T(8,128)(2,1)S(1)} %bitcast.60, s32[3072]{0:T(1024)S(1)} %select_n.74), kind=kOutput, calls=%fused_computation.18 | convolution fusion | flops 3225944064 | bytes 7352320 | tf_op jit(solution)/shard_map/qk,hkl->hql/dot_general | solution.py:61
  32.0 71.6 %all-to-all-done = bf16[128,48,512]{2,1,0:T(8,128)(2,1)} async-done(((bf16[128,48,512]{2,1,0:T(8,128)(2,1)}), bf16[128,48,512]{2,1,0:T(8,128)(2,1)}, u32[]{:S(2)}, u32[]{:S(2)}) %all-to-all-start) | async-done | bytes 6291488 | tf_op jit(solution)/shard_map/all_to_all | solution.py:62
  103.6 10.6 %all-to-all-start.3 = ((bf16[128,48,512]{2,1,0:T(8,128)(2,1)}), bf16[128,48,512]{2,1,0:T(8,128)(2,1)}, u32[]{:S(2)}, u32[]{:S(2)}) async-start(bf16[128,48,512]{2,1,0:T(8,128)(2,1)} %bitcast.52), calls=%async_computation.3 | async-start | bytes 12582912 | tf_op jit(solution)/shard_map/all_to_all | solution.py:62
  114.3 2.8 copy.52
  117.1 1.7 collective-permute-start.1
  118.9 10.7 %reshape.197 = bf16[1536,2048]{1,0:T(8,128)(2,1)} reshape(bf16[128,48,512]{2,1,0:T(8,128)(2,1)} %all-to-all-done) | data formatting | bytes 12582912 | tf_op jit(solution)/shard_map/reshape | solution.py:65
  129.6 10.1 %fusion.43 = (bf16[1536,768]{0,1:T(8,128)(2,1)}, f32[1536,768]{0,1:T(8,128)}) fusion(bf16[1536,2048]{1,0:T(8,128)(2,1)} %reshape.197, bf16[2048,2304]{1,0:T(8,128)(2,1)} %bitcast.61), kind=kOutput, calls=%fused_computation.70 | convolution fusion | flops 4833017856 | bytes 16515072 | tf_op jit(solution)/shard_map/dot_general | solution.py:85
  139.7 94.9 %collective-permute-done.1 = bf16[768,1536]{0,1:T(8,128)(2,1)} collective-permute-done((bf16[768,1536]{0,1:T(8,128)(2,1)S(1)}, bf16[768,1536]{0,1:T(8,128)(2,1)}, u32[]{:S(2)}, u32[]{:S(2)}) %collective-permute-start.1) | collective-permute-done | bytes 2359328 | tf_op jit(solution)/shard_map/ppermute | solution.py:72
  234.5 3.8 maximum_select_fusion
  238.4 46.7 %collective-permute-done = bf16[1536,768]{0,1:T(8,128)(2,1)} collective-permute-done((bf16[1536,768]{0,1:T(8,128)(2,1)}, bf16[1536,768]{0,1:T(8,128)(2,1)}, u32[]{:S(2)}, u32[]{:S(2)}) %collective-permute-start) | collective-permute-done | bytes 2359328 | tf_op jit(solution)/shard_map/ppermute | solution.py:86
  285.1 5.6 %multiply_reduce_fusion = (f32[1536]{0:T(1024)S(1)}, bf16[1536,768]{0,1:T(8,128)(2,1)S(1)}, bf16[1536,768]{0,1:T(8,128)(2,1)}) fusion(f32[1536,768]{0,1:T(8,128)S(1)} %copy-done.2, bf16[1536,768]{0,1:T(8,128)(2,1)} %collective-permute-done, bf16[1536,1536]{0,1:T(8,128)(2,1)S(1)} %maximum_select_fusion), kind=kLoop, calls=%fused_computation.28 | loop fusion | flops 23591424 | bytes 16521216 | tf_op jit(solution)/shard_map/reduce_sum | solution.py:96
  291.4 11.8 %all-to-all-start.2 = ((f32[128,1,12]{2,1,0:T(1,128)}), f32[128,1,12]{2,1,0:T(1,128)S(1)}, u32[]{:S(2)}, u32[]{:S(2)}) async-start(f32[128,1,12]{2,1,0:T(1,128)} %bitcast.12), calls=%async_computation.2 | async-start | bytes 131072 | tf_op jit(solution)/shard_map/all_to_all | solution.py:121
  303.3 14.6 %convolution_convert_fusion.1 = bf16[1536,2048]{1,0:T(8,128)(2,1)} fusion(bf16[2048,2304]{1,0:T(8,128)(2,1)} %bitcast.62, bf16[1536,768]{0,1:T(8,128)(2,1)S(1)} %get-tuple-element.19, bf16[1536,768]{0,1:T(8,128)(2,1)} %get-tuple-element.20), kind=kOutput, calls=%fused_computation.2 | convolution fusion | flops 9676259328 | bytes 17301504 | tf_op jit(solution)/shard_map/dot_general | solution.py:105
  317.9 10.7 %reshape.198 = bf16[128,48,512]{2,1,0:T(8,128)(2,1)} reshape(bf16[1536,2048]{1,0:T(8,128)(2,1)} %convolution_convert_fusion.1) | data formatting | bytes 12582912 | tf_op jit(solution)/shard_map/reshape | solution.py:116
  328.7 10.2 %all-to-all-start.1 = ((bf16[128,48,512]{2,1,0:T(8,128)(2,1)}), bf16[128,48,512]{2,1,0:T(8,128)(2,1)}, u32[]{:S(2)}, u32[]{:S(2)}) async-start(bf16[128,48,512]{2,1,0:T(8,128)(2,1)} %reshape.198), calls=%async_computation.1 | async-start | bytes 12582912 | tf_op jit(solution)/shard_map/all_to_all | solution.py:116
  338.8 10.8 %reshape.206 = bf16[1536,2048]{1,0:T(8,128)(2,1)} reshape(bf16[128,48,512]{2,1,0:T(8,128)(2,1)} %all-to-all-done.3) | data formatting | bytes 12582912 | tf_op jit(solution)/shard_map/reshape | solution.py:65
  349.6 9.4 %fusion.31 = bf16[1,2048,768]{1,2,0:T(8,128)(2,1)S(1)} fusion(bf16[1536,2048]{1,0:T(8,128)(2,1)} %reshape.197, bf16[1536,1536]{0,1:T(8,128)(2,1)} %copy-done), kind=kOutput, calls=%fused_computation.50 | convolution fusion | flops 4842848256 | bytes 14155776 | tf_op jit(solution)/shard_map/dot_general | solution.py:111
  359.0 11.4 %fusion = bf16[1,2048,1536]{1,2,0:T(8,128)(2,1)S(1)} fusion(bf16[1536,2048]{1,0:T(8,128)(2,1)S(1)} %copy-done.1, bf16[1536,768]{0,1:T(8,128)(2,1)S(1)} %get-tuple-element.19, bf16[1536,768]{0,1:T(8,128)(2,1)S(1)} %copy-done.3), kind=kOutput, calls=%fused_computation.6 | convolution fusion | flops 9676259328 | bytes 17301504 | tf_op jit(solution)/shard_map/dot_general | solution.py:108
  370.4 11.3 %pad_maximum_fusion = bf16[1,2048,2304]{1,2,0:T(8,128)(2,1)} fusion(bf16[1,2048,768]{1,2,0:T(8,128)(2,1)S(1)} %fusion.31, bf16[1,2048,1536]{1,2,0:T(8,128)(2,1)S(1)} %fusion), kind=kLoop, calls=%fused_computation | loop fusion | flops 18874368 | bytes 18874368 | tf_op jit(solution)/shard_map/concatenate | solution.py:114
  381.7 12.6 %copy.58 = bf16[1,2048,2304]{2,1,0:T(8,128)(2,1)} copy(bf16[1,2048,2304]{1,2,0:T(8,128)(2,1)} %pad_maximum_fusion) | data formatting | bytes 18874368
  395.9 21.1 %all-to-all-done.1 = bf16[128,48,512]{2,1,0:T(8,128)(2,1)} async-done(((bf16[128,48,512]{2,1,0:T(8,128)(2,1)}), bf16[128,48,512]{2,1,0:T(8,128)(2,1)}, u32[]{:S(2)}, u32[]{:S(2)}) %all-to-all-start.1) | async-done | bytes 6291488 | tf_op jit(solution)/shard_map/all_to_all | solution.py:116
  417.0 5.8 %fusion.34 = bf16[2,512,4,128]{3,1,2,0:T(8,128)(2,1)S(1)} fusion(bf16[2,3072,512,1]{2,1,3,0:T(8,128)(2,1)} %bitcast.22, s32[3072]{0:T(1024)S(1)} %select_n.74, s32[4,128]{1,0:T(4,128)S(1)} %multiply_add_fusion), kind=kOutput, calls=%fused_computation.52 | convolution fusion | flops 3223322624 | bytes 7354368 | tf_op jit(solution)/shard_map/ctk,hkl->thcl/dot_general | solution.py:118
  (45 shorter events, 11.0 us)
Async XLA Ops:
  13.6 11.9 %copy-start.4 = (bf16[128,4096]{1,0:T(8,128)(2,1)S(1)}, bf16[128,4096]{1,0:T(8,128)(2,1)}, u32[]{:S(2)}) copy-start(bf16[128,4096]{1,0:T(8,128)(2,1)} %param.6) | copy-start | bytes 3145732
  13.6 90.0 %all-to-all-start = ((bf16[128,48,512]{2,1,0:T(8,128)(2,1)}), bf16[128,48,512]{2,1,0:T(8,128)(2,1)}, u32[]{:S(2)}, u32[]{:S(2)}) async-start(bf16[128,48,512]{2,1,0:T(8,128)(2,1)} %bitcast.53), calls=%async_computation | async-start | bytes 12582912 | tf_op jit(solution)/shard_map/all_to_all | solution.py:62
  103.6 187.8 %all-to-all-start.3 = ((bf16[128,48,512]{2,1,0:T(8,128)(2,1)}), bf16[128,48,512]{2,1,0:T(8,128)(2,1)}, u32[]{:S(2)}, u32[]{:S(2)}) async-start(bf16[128,48,512]{2,1,0:T(8,128)(2,1)} %bitcast.52), calls=%async_computation.3 | async-start | bytes 12582912 | tf_op jit(solution)/shard_map/all_to_all | solution.py:62
  117.1 117.4 %collective-permute-start.1 = (bf16[768,1536]{0,1:T(8,128)(2,1)S(1)}, bf16[768,1536]{0,1:T(8,128)(2,1)}, u32[]{:S(2)}, u32[]{:S(2)}) collective-permute-start(bf16[768,1536]{0,1:T(8,128)(2,1)S(1)} %bitcast.50), channel_id=1, source_target_pairs={{0,1},{1,0},{2,3},{3,2},{4,5},{5,4},{6,7},{7,6},{8,9},{9,8},{10,11... | collective-permute-start | bytes 7077896 | tf_op jit(solution)/shard_map/ppermute | solution.py:72
  139.7 145.4 %collective-permute-start = (bf16[1536,768]{0,1:T(8,128)(2,1)}, bf16[1536,768]{0,1:T(8,128)(2,1)}, u32[]{:S(2)}, u32[]{:S(2)}) collective-permute-start(bf16[1536,768]{0,1:T(8,128)(2,1)} %get-tuple-element.21), channel_id=1, source_target_pairs={{0,1},{1,0},{2,3},{3,2},{4,5},{5,4},{6,7},{7,6},{8,9},{9,8},{10,11... | collective-permute-start | bytes 7077896 | tf_op jit(solution)/shard_map/ppermute | solution.py:86
  139.7 145.4 %copy-start.2 = (f32[1536,768]{0,1:T(8,128)S(1)}, f32[1536,768]{0,1:T(8,128)}, u32[]{:S(2)}) copy-start(f32[1536,768]{0,1:T(8,128)} %get-tuple-element.22) | copy-start | bytes 14155780
  238.4 52.4 %copy-start = (bf16[1536,1536]{0,1:T(8,128)(2,1)}, bf16[1536,1536]{0,1:T(8,128)(2,1)S(1)}, u32[]{:S(2)}) copy-start(bf16[1536,1536]{0,1:T(8,128)(2,1)S(1)} %maximum_select_fusion) | copy-start | bytes 14155780
  291.4 37.2 %all-to-all-start.2 = ((f32[128,1,12]{2,1,0:T(1,128)}), f32[128,1,12]{2,1,0:T(1,128)S(1)}, u32[]{:S(2)}, u32[]{:S(2)}) async-start(f32[128,1,12]{2,1,0:T(1,128)} %bitcast.12), calls=%async_computation.2 | async-start | bytes 131072 | tf_op jit(solution)/shard_map/all_to_all | solution.py:121
  328.7 88.3 %all-to-all-start.1 = ((bf16[128,48,512]{2,1,0:T(8,128)(2,1)}), bf16[128,48,512]{2,1,0:T(8,128)(2,1)}, u32[]{:S(2)}, u32[]{:S(2)}) async-start(bf16[128,48,512]{2,1,0:T(8,128)(2,1)} %reshape.198), calls=%async_computation.1 | async-start | bytes 12582912 | tf_op jit(solution)/shard_map/all_to_all | solution.py:116
  349.6 9.4 %copy-start.1 = (bf16[1536,2048]{1,0:T(8,128)(2,1)S(1)}, bf16[1536,2048]{1,0:T(8,128)(2,1)}, u32[]{:S(2)}) copy-start(bf16[1536,2048]{1,0:T(8,128)(2,1)} %reshape.206) | copy-start | bytes 18874372
  349.6 9.4 %copy-start.3 = (bf16[1536,768]{0,1:T(8,128)(2,1)S(1)}, bf16[1536,768]{0,1:T(8,128)(2,1)}, u32[]{:S(2)}) copy-start(bf16[1536,768]{0,1:T(8,128)(2,1)} %get-tuple-element.20) | copy-start | bytes 7077892
  381.7 13.6 %copy-start.5 = (s32[128,8]{0,1:T(8,128)S(1)}, s32[128,8]{0,1:T(8,128)}, u32[]{:S(2)}) copy-start(s32[128,8]{0,1:T(8,128)} %param.8) | copy-start | bytes 12292
  381.7 13.6 %copy-start.6 = (bf16[128,8]{0,1:T(8,128)(2,1)S(1)}, bf16[128,8]{0,1:T(8,128)(2,1)}, u32[]{:S(2)}) copy-start(bf16[128,8]{0,1:T(8,128)(2,1)} %param.9) | copy-start | bytes 6148

commit v9 on v8

--- a/solution.py
+++ b/solution.py
@@ -93,13 +93,13 @@
     sigmoid_gate = jax.nn.sigmoid(pre_gate)
     activated = pre_gate * sigmoid_gate
     hidden_act = activated * pre_up
+    gate_factor = pre_up * sigmoid_gate * (1.0 + pre_gate * (1.0 - sigmoid_gate))
+    activated, hidden_act, gate_factor = lax.optimization_barrier(
+        (activated, hidden_act, gate_factor)
+    )
     scaled_slot_prob = jnp.sum(hidden_act * scaled_grad, axis=1)
     gate_up_grad = jnp.concatenate(
-        [
-            scaled_grad * pre_up * sigmoid_gate * (1.0 + pre_gate * (1.0 - sigmoid_gate)),
-            scaled_grad * activated,
-        ],
-        axis=1,
+        [scaled_grad * gate_factor, scaled_grad * activated], axis=1
     ).astype(bf16)
 
     row_grad = lax.dot_general(

time: 427 us -> 432 us (1.012)
  other arithmetic: 24.2 us -> 35.7 us
  waiting for transfers between devices: 234 us -> 229 us
    ppermute x1, waiting for transfers between devices: 46.7 us -> 40.7 us  [body(): lax.ppermute(partial_down.astype(bf16), 'dp', [(i, (i + 1) % n_dp) for i...]
    mul x0 -> x1, other arithmetic: none -> 5.91 us  [body(): pre_up * sigmoid_gate * (1.0 + pre_gate * (1.0 - sigmoid_gate))]
    reduce_sum x1, other arithmetic: 5.6 us -> 11.2 us  [body(): scaled_slot_prob = jnp.sum(hidden_act * scaled_grad, axis=1)]
    unnamed x20 -> x16, local copies, waits for them, and re-layouts: 19.6 us -> 19.6 us
  transfers between devices with their start and end apart: 6 -> 6, of which waited for: 4 -> 4; matrix products, arithmetic and copies ran while one was open for 29% -> 31% of each run, Pallas kernels for 0% -> 0%
where the time goes in v9:
time: 432 us; the launch traced here: 429 us
  waiting for transfers between devices  229 us (53%)
  matrix products  62.6 us (14%)
  local copies, waits for them, and re-layouts  55 us (13%)
  starting transfers between devices  46.3 us (11%)
  other arithmetic  35.7 us (8%)
    ppermute x1, waiting for transfers between devices, body(): other_saved = lax.ppermute(own_saved, 'dp', [(0, 1), (1, 0)])  94.9 us
    all_to_all x2, waiting for transfers between devices, dispatch(): lax.all_to_all(sent.reshape(devices, rows_per_chunk, lanes), WIRE, 0, 0,...  71.6 us
    ppermute x1, waiting for transfers between devices, body(): lax.ppermute(partial_down.astype(bf16), 'dp', [(i, (i + 1) % n_dp) for i...  40.7 us
    all_to_all x2, starting transfers between devices, dispatch(): lax.all_to_all(sent.reshape(devices, rows_per_chunk, lanes), WIRE, 0, 0,...  22.5 us
    all_to_all x1, waiting for transfers between devices, body(): lax.all_to_all(row_grad.reshape(devices, rows_per_chunk, lanes), WIRE, 0,...  21.6 us
    reshape x2, local copies, waits for them, and re-layouts, dispatch(): return got.reshape(slots_all, half)  21.4 us
    unnamed x16, local copies, waits for them, and re-layouts  19.6 us
    dot_general x1, matrix products, body(): lax.dot_general(gate_up_grad, gate_up_part, (((1,), (1,)), ((), ())), pre...  14.7 us
  transfers between devices with their start and end apart: 6, of which 4 were waited for; matrix products, arithmetic and copies ran while one was open for 31% of the time, Pallas kernels for 0%

profile of v9, /device:TPU:1, one launch (start us, length us, event | category | flops | bytes accessed | tf_op | source)
XLA Modules:
  0.0 429.3 jit_solution(3671554292470829675)
XLA Ops:
  7.3 6.3 %convolution_convert_fusion.2 = bf16[3072,2,512]{2,0,1:T(8,128)(2,1)} fusion(bf16[2,512,512]{2,1,0:T(8,128)(2,1)S(1)} %bitcast.59, bf16[3072]{0:T(1024)(128)(2,1)S(1)} %broadcast_in_dim.99, s32[3072]{0:T(1024)S(1)} %select_n.74), kind=kOutput, calls=%fused_computation.17 | convolution fusion | flops 3227516928 | bytes 7358464 | tf_op jit(solution)/shard_map/qk,hkl->hql/dot_general | solution.py:61
  13.6 11.9 %all-to-all-start = ((bf16[128,48,512]{2,1,0:T(8,128)(2,1)}), bf16[128,48,512]{2,1,0:T(8,128)(2,1)}, u32[]{:S(2)}, u32[]{:S(2)}) async-start(bf16[128,48,512]{2,1,0:T(8,128)(2,1)} %bitcast.53), calls=%async_computation | async-start | bytes 12582912 | tf_op jit(solution)/shard_map/all_to_all | solution.py:62
  26.2 5.8 %fusion.8 = bf16[3072,2,512]{2,0,1:T(8,128)(2,1)} fusion(bf16[2,512,512]{2,1,0:T(8,128)(2,1)S(1)} %bitcast.60, s32[3072]{0:T(1024)S(1)} %select_n.74), kind=kOutput, calls=%fused_computation.18 | convolution fusion | flops 3225944064 | bytes 7352320 | tf_op jit(solution)/shard_map/qk,hkl->hql/dot_general | solution.py:61
  32.0 71.6 %all-to-all-done = bf16[128,48,512]{2,1,0:T(8,128)(2,1)} async-done(((bf16[128,48,512]{2,1,0:T(8,128)(2,1)}), bf16[128,48,512]{2,1,0:T(8,128)(2,1)}, u32[]{:S(2)}, u32[]{:S(2)}) %all-to-all-start) | async-done | bytes 6291488 | tf_op jit(solution)/shard_map/all_to_all | solution.py:62
  103.6 10.6 %all-to-all-start.3 = ((bf16[128,48,512]{2,1,0:T(8,128)(2,1)}), bf16[128,48,512]{2,1,0:T(8,128)(2,1)}, u32[]{:S(2)}, u32[]{:S(2)}) async-start(bf16[128,48,512]{2,1,0:T(8,128)(2,1)} %bitcast.52), calls=%async_computation.3 | async-start | bytes 12582912 | tf_op jit(solution)/shard_map/all_to_all | solution.py:62
  114.3 2.8 copy.52
  118.9 10.7 %reshape.197 = bf16[1536,2048]{1,0:T(8,128)(2,1)} reshape(bf16[128,48,512]{2,1,0:T(8,128)(2,1)} %all-to-all-done) | data formatting | bytes 12582912 | tf_op jit(solution)/shard_map/reshape | solution.py:65
  129.6 10.0 %fusion.39 = (bf16[1536,768]{0,1:T(8,128)(2,1)}, f32[1536,768]{0,1:T(8,128)}) fusion(bf16[1536,2048]{1,0:T(8,128)(2,1)} %reshape.197, bf16[2048,2304]{1,0:T(8,128)(2,1)} %bitcast.61), kind=kOutput, calls=%fused_computation.68 | convolution fusion | flops 4833017856 | bytes 16515072 | tf_op jit(solution)/shard_map/dot_general | solution.py:85
  139.6 94.9 %collective-permute-done.1 = bf16[768,1536]{0,1:T(8,128)(2,1)} collective-permute-done((bf16[768,1536]{0,1:T(8,128)(2,1)S(1)}, bf16[768,1536]{0,1:T(8,128)(2,1)}, u32[]{:S(2)}, u32[]{:S(2)}) %collective-permute-start.1) | collective-permute-done | bytes 2359328 | tf_op jit(solution)/shard_map/ppermute | solution.py:72
  234.5 3.9 maximum_select_fusion
  238.5 5.9 %fusion.11 = (f32[1536,768]{0,1:T(8,128)}, f32[1536,768]{0,1:T(8,128)}, f32[1536,768]{0,1:T(8,128)}) fusion(bf16[1536,1536]{0,1:T(8,128)(2,1)S(1)} %maximum_select_fusion), kind=kLoop, calls=%fused_computation.19 | loop fusion | flops 14155776 | bytes 18874368 | tf_op jit(solution)/shard_map/mul | solution.py:96
  244.4 40.7 %collective-permute-done = bf16[1536,768]{0,1:T(8,128)(2,1)} collective-permute-done((bf16[1536,768]{0,1:T(8,128)(2,1)}, bf16[1536,768]{0,1:T(8,128)(2,1)}, u32[]{:S(2)}, u32[]{:S(2)}) %collective-permute-start) | collective-permute-done | bytes 2359328 | tf_op jit(solution)/shard_map/ppermute | solution.py:86
  285.1 11.2 %multiply_reduce_fusion = (f32[1536]{0:T(1024)S(1)}, bf16[1536,768]{0,1:T(8,128)(2,1)S(1)}, bf16[1536,768]{0,1:T(8,128)(2,1)}) fusion(f32[1536,768]{0,1:T(8,128)} %get-tuple-element.8, f32[1536,768]{0,1:T(8,128)} %get-tuple-element.31, bf16[1536,768]{0,1:T(8,128)(2,1)} %collective-permute-done, f32[1536,768]{0,1:T(8,128)} %get-tuple-element.7, ...), kind=kLoop, calls=%fused_computation.26 | loop fusion | flops 9435648 | bytes 25958400 | tf_op jit(solution)/shard_map/reduce_sum | solution.py:100
  297.0 11.8 %all-to-all-start.2 = ((f32[128,1,12]{2,1,0:T(1,128)}), f32[128,1,12]{2,1,0:T(1,128)S(1)}, u32[]{:S(2)}, u32[]{:S(2)}) async-start(f32[128,1,12]{2,1,0:T(1,128)} %bitcast.12), calls=%async_computation.2 | async-start | bytes 131072 | tf_op jit(solution)/shard_map/all_to_all | solution.py:121
  308.8 14.7 %convolution_convert_fusion.1 = bf16[1536,2048]{1,0:T(8,128)(2,1)} fusion(bf16[2048,2304]{1,0:T(8,128)(2,1)} %bitcast.62, bf16[1536,768]{0,1:T(8,128)(2,1)S(1)} %get-tuple-element.25, bf16[1536,768]{0,1:T(8,128)(2,1)} %get-tuple-element.26), kind=kOutput, calls=%fused_computation.2 | convolution fusion | flops 9676259328 | bytes 17301504 | tf_op jit(solution)/shard_map/dot_general | solution.py:105
  323.5 10.8 %reshape.198 = bf16[128,48,512]{2,1,0:T(8,128)(2,1)} reshape(bf16[1536,2048]{1,0:T(8,128)(2,1)} %convolution_convert_fusion.1) | data formatting | bytes 12582912 | tf_op jit(solution)/shard_map/reshape | solution.py:116
  334.2 10.2 %all-to-all-start.1 = ((bf16[128,48,512]{2,1,0:T(8,128)(2,1)}), bf16[128,48,512]{2,1,0:T(8,128)(2,1)}, u32[]{:S(2)}, u32[]{:S(2)}) async-start(bf16[128,48,512]{2,1,0:T(8,128)(2,1)} %reshape.198), calls=%async_computation.1 | async-start | bytes 12582912 | tf_op jit(solution)/shard_map/all_to_all | solution.py:116
  344.4 10.7 %reshape.206 = bf16[1536,2048]{1,0:T(8,128)(2,1)} reshape(bf16[128,48,512]{2,1,0:T(8,128)(2,1)} %all-to-all-done.3) | data formatting | bytes 12582912 | tf_op jit(solution)/shard_map/reshape | solution.py:65
  355.2 8.7 %fusion.28 = bf16[1,2048,768]{1,2,0:T(8,128)(2,1)S(1)} fusion(bf16[1536,2048]{1,0:T(8,128)(2,1)} %reshape.197, f32[1536,768]{0,1:T(8,128)} %get-tuple-element.8), kind=kOutput, calls=%fused_computation.48 | convolution fusion | flops 4834590720 | bytes 14155776 | tf_op jit(solution)/shard_map/dot_general | solution.py:111
  363.9 11.4 %fusion = bf16[1,2048,1536]{1,2,0:T(8,128)(2,1)S(1)} fusion(bf16[1536,2048]{1,0:T(8,128)(2,1)S(1)} %copy-done, bf16[1536,768]{0,1:T(8,128)(2,1)S(1)} %get-tuple-element.25, bf16[1536,768]{0,1:T(8,128)(2,1)S(1)} %copy-done.1), kind=kOutput, calls=%fused_computation.6 | convolution fusion | flops 9676259328 | bytes 17301504 | tf_op jit(solution)/shard_map/dot_general | solution.py:108
  375.3 11.2 %pad_maximum_fusion = bf16[1,2048,2304]{1,2,0:T(8,128)(2,1)} fusion(bf16[1,2048,768]{1,2,0:T(8,128)(2,1)S(1)} %fusion.28, bf16[1,2048,1536]{1,2,0:T(8,128)(2,1)S(1)} %fusion), kind=kLoop, calls=%fused_computation | loop fusion | flops 18874368 | bytes 18874368 | tf_op jit(solution)/shard_map/concatenate | solution.py:114
  386.5 12.6 %copy.58 = bf16[1,2048,2304]{2,1,0:T(8,128)(2,1)} copy(bf16[1,2048,2304]{1,2,0:T(8,128)(2,1)} %pad_maximum_fusion) | data formatting | bytes 18874368
  400.6 21.6 %all-to-all-done.1 = bf16[128,48,512]{2,1,0:T(8,128)(2,1)} async-done(((bf16[128,48,512]{2,1,0:T(8,128)(2,1)}), bf16[128,48,512]{2,1,0:T(8,128)(2,1)}, u32[]{:S(2)}, u32[]{:S(2)}) %all-to-all-start.1) | async-done | bytes 6291488 | tf_op jit(solution)/shard_map/all_to_all | solution.py:116
  422.2 5.8 %fusion.30 = bf16[2,512,4,128]{3,1,2,0:T(8,128)(2,1)S(1)} fusion(bf16[2,3072,512,1]{2,1,3,0:T(8,128)(2,1)} %bitcast.22, s32[3072]{0:T(1024)S(1)} %select_n.74, s32[4,128]{1,0:T(4,128)S(1)} %multiply_add_fusion), kind=kOutput, calls=%fused_computation.50 | convolution fusion | flops 3223322624 | bytes 7354368 | tf_op jit(solution)/shard_map/ctk,hkl->thcl/dot_general | solution.py:118
  (42 shorter events, 12.7 us)
Async XLA Ops:
  13.6 11.9 %copy-start.2 = (bf16[128,4096]{1,0:T(8,128)(2,1)S(1)}, bf16[128,4096]{1,0:T(8,128)(2,1)}, u32[]{:S(2)}) copy-start(bf16[128,4096]{1,0:T(8,128)(2,1)} %param.6) | copy-start | bytes 3145732
  13.6 90.0 %all-to-all-start = ((bf16[128,48,512]{2,1,0:T(8,128)(2,1)}), bf16[128,48,512]{2,1,0:T(8,128)(2,1)}, u32[]{:S(2)}, u32[]{:S(2)}) async-start(bf16[128,48,512]{2,1,0:T(8,128)(2,1)} %bitcast.53), calls=%async_computation | async-start | bytes 12582912 | tf_op jit(solution)/shard_map/all_to_all | solution.py:62
  103.6 193.3 %all-to-all-start.3 = ((bf16[128,48,512]{2,1,0:T(8,128)(2,1)}), bf16[128,48,512]{2,1,0:T(8,128)(2,1)}, u32[]{:S(2)}, u32[]{:S(2)}) async-start(bf16[128,48,512]{2,1,0:T(8,128)(2,1)} %bitcast.52), calls=%async_computation.3 | async-start | bytes 12582912 | tf_op jit(solution)/shard_map/all_to_all | solution.py:62
  117.1 117.4 %collective-permute-start.1 = (bf16[768,1536]{0,1:T(8,128)(2,1)S(1)}, bf16[768,1536]{0,1:T(8,128)(2,1)}, u32[]{:S(2)}, u32[]{:S(2)}) collective-permute-start(bf16[768,1536]{0,1:T(8,128)(2,1)S(1)} %bitcast.50), channel_id=1, source_target_pairs={{0,1},{1,0},{2,3},{3,2},{4,5},{5,4},{6,7},{7,6},{8,9},{9,8},{10,11... | collective-permute-start | bytes 7077896 | tf_op jit(solution)/shard_map/ppermute | solution.py:72
  139.6 145.5 %collective-permute-start = (bf16[1536,768]{0,1:T(8,128)(2,1)}, bf16[1536,768]{0,1:T(8,128)(2,1)}, u32[]{:S(2)}, u32[]{:S(2)}) collective-permute-start(bf16[1536,768]{0,1:T(8,128)(2,1)} %get-tuple-element.30), channel_id=1, source_target_pairs={{0,1},{1,0},{2,3},{3,2},{4,5},{5,4},{6,7},{7,6},{8,9},{9,8},{10,11... | collective-permute-start | bytes 7077896 | tf_op jit(solution)/shard_map/ppermute | solution.py:86
  297.0 37.3 %all-to-all-start.2 = ((f32[128,1,12]{2,1,0:T(1,128)}), f32[128,1,12]{2,1,0:T(1,128)S(1)}, u32[]{:S(2)}, u32[]{:S(2)}) async-start(f32[128,1,12]{2,1,0:T(1,128)} %bitcast.12), calls=%async_computation.2 | async-start | bytes 131072 | tf_op jit(solution)/shard_map/all_to_all | solution.py:121
  334.2 88.0 %all-to-all-start.1 = ((bf16[128,48,512]{2,1,0:T(8,128)(2,1)}), bf16[128,48,512]{2,1,0:T(8,128)(2,1)}, u32[]{:S(2)}, u32[]{:S(2)}) async-start(bf16[128,48,512]{2,1,0:T(8,128)(2,1)} %reshape.198), calls=%async_computation.1 | async-start | bytes 12582912 | tf_op jit(solution)/shard_map/all_to_all | solution.py:116
  355.2 8.7 %copy-start = (bf16[1536,2048]{1,0:T(8,128)(2,1)S(1)}, bf16[1536,2048]{1,0:T(8,128)(2,1)}, u32[]{:S(2)}) copy-start(bf16[1536,2048]{1,0:T(8,128)(2,1)} %reshape.206) | copy-start | bytes 18874372
  355.2 8.7 %copy-start.1 = (bf16[1536,768]{0,1:T(8,128)(2,1)S(1)}, bf16[1536,768]{0,1:T(8,128)(2,1)}, u32[]{:S(2)}) copy-start(bf16[1536,768]{0,1:T(8,128)(2,1)} %get-tuple-element.26) | copy-start | bytes 7077892
  386.5 13.6 %copy-start.3 = (s32[128,8]{0,1:T(8,128)S(1)}, s32[128,8]{0,1:T(8,128)}, u32[]{:S(2)}) copy-start(s32[128,8]{0,1:T(8,128)} %param.8) | copy-start | bytes 12292
  386.5 13.6 %copy-start.4 = (bf16[128,8]{0,1:T(8,128)(2,1)S(1)}, bf16[128,8]{0,1:T(8,128)(2,1)}, u32[]{:S(2)}) copy-start(bf16[128,8]{0,1:T(8,128)(2,1)} %param.9) | copy-start | bytes 6148
